TPU v7x, 32 devices: a whole 2x2x4 slice. The times are simulated.
32 devices in a mesh: groups: 2 (over y), spec: 8 (over z, core), lat: 2 (over x).
Axes of the slice: x: 2, y: 2, z: 4, core: 2. Of those that a mesh axis runs over, the one named last changes fastest.
Arguments:
- spectrum: float32 [1152, 64, 256], P('spec', 'lat', 'groups'), parts along dimension 2, may hold values from 0.05 to 1
- transparency: float32 [64, 256], P('lat', 'groups'), parts along dimension 1, may hold values from 0 to 1, as said below
- sea_order: int32 [64, 256], P('lat', 'groups'), parts along dimension 1, may hold values from 0 to 4095, as said below
- speeds: float32 [32], replicated, may hold values from 0.15 to 0.9
- sprinkle: float32 [32], replicated, may hold values from 0.04 to 0.25
- coupling: float32 [32], replicated, may hold values from 0.3 to 3
- quad_offsets: int32 [4], replicated, may hold values from 1 to 4, as said below
Outputs:
- updated: float32 [1152, 64, 256], P('spec', 'lat', 'groups'), parts along dimension 2
- source: bfloat16 [4, 1152, 3072], P(('groups', 'lat'), None, 'spec'), parts along dimension 0
There are 2 independent parts, one for each index of `groups`. A program takes and returns all parts, laid end to end along the dimension named above; an argument that names none is the same for every part. Nothing has to cross between parts.
Inputs may be any that keep to these rules, and one draw needn't show every extreme that they name: Every band of 32 rows holds at most 3072 cells of positive transparency (sea cells), and some band exactly 3072; land cells are exactly 0. `sea_order`: read row by row, each band of 32 rows holds a permutation of its row-major cell positions, all sea cells first. `quad_offsets`: bins up and down in frequency, then direction bins of the first and second partner.
All inputs are finite; a program needn't handle non-finite values.
Results may differ from a plain program's by a relative error of at most 0.001.
Values sent between devices are 32-bit elements; how exact they have to be, the bound alone decides.
No kernel may reach another device: no remote copies, remote signals or barrier semaphores. Data moves between devices by JAX's collectives and lax.ppermute only.
A program may use at most 64 MiB of HBM per device.

v0:
```python
import math

import jax
import jax.numpy as jnp
from jax import lax
from jax.sharding import PartitionSpec as P

NDIR = 36
NFREQ = 32
SUBSTEPS = 2
SEA_MAX = 3072


gain_up = 1.25 ** (-4)
gain_down = 0.75 ** (-4)
gain_cross = 0.9375 ** (-4)


def extended_2(block, sides, width):
    for axis, dim in sides:
        count = lax.axis_size(axis)
        forward = [(i, i + 1) for i in range(count - 1)]
        backward = [(target, source) for source, target in forward]
        low = lax.ppermute(
            lax.slice_in_dim(block, block.shape[dim] - width, None, axis=dim), axis, forward
        )
        high = lax.ppermute(lax.slice_in_dim(block, 0, width, axis=dim), axis, backward)
        block = jnp.concatenate([low, block, high], axis=dim)
    return block


def cut_slab(values, offset, length, along):
    return lax.slice_in_dim(values, offset, offset + length, axis=along)


def pad_along(values):
    return jnp.pad(values, ((0, 0), (0, 0), (2, 2)))


def quickest(padded, courant, along):
    length = padded.shape[along] - 4
    before_cell = cut_slab(padded, 0, length + 1, along)
    left_cell = cut_slab(padded, 1, length + 1, along)
    right_cell = cut_slab(padded, 2, length + 1, along)
    after_cell = cut_slab(padded, 3, length + 1, along)
    curvature = jnp.where(
        courant > 0,
        right_cell - 2.0 * left_cell + before_cell,
        after_cell - 2.0 * right_cell + left_cell,
    )
    face_value = (
        0.5 * (left_cell + right_cell)
        - 0.5 * courant * (right_cell - left_cell)
        - (1.0 - courant * courant) / 6.0 * curvature
    )
    face_flux = courant * face_value
    return cut_slab(padded, 2, length, along) - (
        cut_slab(face_flux, 1, length, along) - cut_slab(face_flux, 0, length, along)
    )


def laplace(padded, along):
    length = padded.shape[along] - 4
    centre = cut_slab(padded, 2, length, along)
    near_sum = (
        cut_slab(padded, 1, length, along) + cut_slab(padded, 3, length, along) - 2.0 * centre
    )
    far_sum = cut_slab(padded, 0, length, along) + cut_slab(padded, 4, length, along) - 2.0 * centre
    return 4.0 / 3.0 * near_sum - 1.0 / 12.0 * far_sum


def interact(columns, coupling, quad_offsets):
    initial = columns.shape
    spectra = columns.reshape(NFREQ, NDIR, -1)
    up_freq = quad_offsets[0]
    down_freq = quad_offsets[1]
    dir_one = quad_offsets[2]
    dir_two = quad_offsets[3]
    freq_index = lax.iota(jnp.int32, NFREQ)[:, None, None]
    inside = ((freq_index + up_freq < NFREQ) & (freq_index - down_freq >= 0)).astype(jnp.float32)
    weight = coupling[:, None, None] * inside
    source_sum = jnp.zeros_like(spectra)
    for mirror in (1, -1):
        upper_bin = jnp.roll(jnp.roll(spectra, -up_freq, 0), -mirror * dir_one, 1)
        lower_bin = jnp.roll(jnp.roll(spectra, down_freq, 0), mirror * dir_two, 1)
        squared = spectra * spectra
        transfer = weight * (
            squared * (upper_bin * gain_up + lower_bin * gain_down)
            - 2.0 * gain_cross * spectra * upper_bin * lower_bin
        )
        source_sum = source_sum - 2.0 * transfer
        source_sum = source_sum + jnp.roll(jnp.roll(transfer, up_freq, 0), mirror * dir_one, 1)
        source_sum = source_sum + jnp.roll(jnp.roll(transfer, -down_freq, 0), -mirror * dir_two, 1)
    return source_sum.reshape(initial)


def per_component(lookup, freq_index):
    matches = freq_index[:, None] == lax.iota(jnp.int32, lookup.shape[0])[None, :]
    return jnp.sum(jnp.where(matches, lookup[None, :], 0.0), axis=1)


def propagate(energy, ext_mask, courant_y, courant_x):
    for substep in range(SUBSTEPS):
        energy = quickest(energy, courant_y, 1)
        ext_mask = cut_slab(ext_mask, 2, ext_mask.shape[0] - 4, 0)
        energy = quickest(pad_along(energy), courant_x, 2) * ext_mask
    return energy


def on_device(spectrum, transparency, sea_order, speeds, sprinkle, coupling, quad_offsets):
    local_comps = spectrum.shape[0]
    band_rows = spectrum.shape[1]
    first_comp = lax.axis_index("spec") * local_comps
    comp_index = first_comp + lax.iota(jnp.int32, local_comps)
    freq_index = comp_index // NDIR
    dir_index = comp_index % NDIR
    angles = 2.0 * math.pi * (dir_index.astype(jnp.float32) + 0.5) / NDIR
    sines = jnp.sin(angles)
    cosines = jnp.cos(angles)
    speed_comp = per_component(speeds, freq_index)
    spread = per_component(sprinkle, freq_index)
    courant_y = (speed_comp * sines)[:, None, None]
    courant_x = (speed_comp * cosines)[:, None, None]
    spread_y = (spread * (sines * sines + 0.25 * cosines * cosines))[:, None, None]
    spread_x = (spread * (cosines * cosines + 0.25 * sines * sines))[:, None, None]
    stacked = jnp.concatenate([transparency[None], spectrum], axis=0)
    reach = 2 * SUBSTEPS
    extended = extended_2(stacked, (("lat", 1),), reach + 2)
    with_rim = propagate(extended[1:], extended[0], courant_y, courant_x)
    centre = cut_slab(with_rim, 2, band_rows, 1)
    smoothed = (
        centre + spread_y * laplace(with_rim, 1) + spread_x * laplace(pad_along(centre), 2)
    ) * transparency
    flat_cells = smoothed.reshape(local_comps, -1)
    sea_cells = sea_order.reshape(-1)[:SEA_MAX]
    columns = jnp.take(flat_cells, sea_cells, axis=1)
    gathered = lax.all_to_all(columns, "spec", split_axis=1, concat_axis=0, tiled=True)
    source_terms = interact(gathered, coupling, quad_offsets)
    returned = lax.all_to_all(source_terms, "spec", split_axis=0, concat_axis=1, tiled=True)
    new_cells = flat_cells.at[:, sea_cells].add(returned)
    updated = new_cells.reshape(smoothed.shape)
    return (updated, source_terms.astype(jnp.bfloat16)[None])


def solution(mesh):
    in_specs = (
        P("spec", "lat", "groups"),
        P("lat", "groups"),
        P("lat", "groups"),
        P(),
        P(),
        P(),
        P(),
    )
    out_specs = (P("spec", "lat", "groups"), P(("groups", "lat"), None, "spec"))
    return jax.shard_map(
        on_device, mesh=mesh, in_specs=in_specs, out_specs=out_specs, check_vma=False
    )
```

profile of v0, /device:TPU:0, one launch (start us, length us, event | category | flops | bytes accessed | tf_op | source)
XLA Modules:
  0.0 205.3 jit_solution(7874196850254106568)
XLA Ops:
  4.4 5.7 %collective-permute-start = (f32[145,6,128]{2,0,1:T(8,128)}, f32[145,6,128]{2,0,1:T(8,128)}, u32[]{:S(2)}, u32[]{:S(2)}) collective-permute-start(f32[145,6,128]{2,0,1:T(8,128)} %copy.35), channel_id=1, source_target_pairs={{0,1},{2,3},{4,5},{6,7},{8,9},{10,11},{12,13},{14,15},{16,17},{18,... | collective-permute-start | bytes 1336328 | tf_op jit(solution)/shard_map/ppermute | solution.py:24
  10.4 6.8 %collective-permute-done.1 = f32[145,6,128]{2,0,1:T(8,128)S(1)} collective-permute-done((f32[145,6,128]{2,0,1:T(8,128)S(1)}, f32[145,6,128]{2,0,1:T(8,128)S(1)}, u32[]{:S(2)}, u32[]{:S(2)}) %collective-permute-start.1) | collective-permute-done | bytes 445472 | tf_op jit(solution)/shard_map/ppermute | solution.py:27
  17.4 2.2 %collective-permute-done = f32[145,6,128]{2,0,1:T(8,128)} collective-permute-done((f32[145,6,128]{2,0,1:T(8,128)}, f32[145,6,128]{2,0,1:T(8,128)}, u32[]{:S(2)}, u32[]{:S(2)}) %collective-permute-start) | collective-permute-done | bytes 445472 | tf_op jit(solution)/shard_map/ppermute | solution.py:24
  21.3 2.8 %fusion.18 = f32[144,41,128]{2,1,0:T(8,128)S(1)} fusion(f32[145,44,128]{2,1,0:T(8,128)S(1)} %pad_maximum_fusion, f32[144]{0:T(256)S(1)} %get-tuple-element.46, f32[144]{0:T(256)S(1)} %get-tuple-element.47, f32[144]{0:T(256)S(1)} %get-tuple-element.39, pred[144]{0:T(512)(128)(4,1)S(1)} %get-tuple-element.38), kind=kLoop, calls=%fused_computation.50 | loop fusion | flops 11335680 | bytes 15116112 | tf_op jit(solution)/shard_map/mul | solution.py:56
  25.2 5.4 %fusion.4 = f32[144,40,129]{2,1,0:T(8,128)S(1)} fusion(f32[144,40,128]{2,1,0:T(8,128)S(1)} %fusion.29, f32[144]{0:T(256)S(1)} %get-tuple-element.37, f32[144]{0:T(256)S(1)} %get-tuple-element.36, f32[144]{0:T(256)S(1)} %get-tuple-element.21, pred[144]{0:T(512)(128)(4,1)S(1)} %get-tuple-element.20), kind=kLoop, calls=%fused_computation.18 | loop fusion | flops 11145600 | bytes 5923152 | tf_op jit(solution)/shard_map/mul | solution.py:56
  31.5 2.6 %fusion.26 = f32[144,37,128]{2,1,0:T(8,128)S(1)} fusion(f32[144,40,128]{2,1,0:T(8,128)S(1)} %fusion.28, f32[144]{0:T(256)S(1)} %get-tuple-element.46, f32[144]{0:T(256)S(1)} %get-tuple-element.47, f32[144]{0:T(256)S(1)} %get-tuple-element.39, pred[144]{0:T(512)(128)(4,1)S(1)} %get-tuple-element.38), kind=kLoop, calls=%fused_computation.70 | loop fusion | flops 10229760 | bytes 13641552 | tf_op jit(solution)/shard_map/mul | solution.py:56
  35.0 5.4 %fusion.11 = f32[144,36,129]{2,1,0:T(8,128)S(1)} fusion(f32[144,36,128]{2,1,0:T(8,128)S(1)} %fusion.21, f32[144]{0:T(256)S(1)} %get-tuple-element.37, f32[144]{0:T(256)S(1)} %get-tuple-element.36, f32[144]{0:T(256)S(1)} %get-tuple-element.21, pred[144]{0:T(512)(128)(4,1)S(1)} %get-tuple-element.20), kind=kLoop, calls=%fused_computation.25 | loop fusion | flops 10031040 | bytes 5331024 | tf_op jit(solution)/shard_map/mul | solution.py:56
  41.6 3.9 %fusion.36 = f32[144,32,128]{2,1,0:T(8,128)S(1)} fusion(f32[144,32,128]{2,1,0:T(8,128)S(1)} %slice.218, f32[144,36,128]{2,1,0:T(8,128)S(1)} %fusion.20, f32[32,128]{1,0:T(8,128)S(1)} %copy-done.2, f32[144]{0:T(256)S(1)} %get-tuple-element.35, f32[144]{0:T(256)S(1)} %get-tuple-element.34), kind=kLoop, calls=%fused_computation.83 | loop fusion | flops 11796480 | bytes 14173312 | tf_op jit(solution)/shard_map/mul | solution.py:131
  45.5 3.3 %copy.39 = f32[144,32,128]{0,2,1:T(8,128)} copy(f32[144,32,128]{2,1,0:T(8,128)S(1)} %fusion.36) | data formatting | bytes 4718592 | tf_op jit(solution)/shard_map/mul | solution.py:131
  48.8 12.0 %gather_fusion = f32[3072,144]{1,0:T(8,128)S(1)} fusion(f32[144,4096]{0,1:T(8,128)} %bitcast.22, s32[3072]{0:T(1024)S(1)} %broadcast_clamp_fusion), kind=kCustom, calls=%fused_computation | custom fusion | bytes 3551232 | tf_op jit(solution)/shard_map/jit(_take)/gather | solution.py:136
  60.8 2.0 copy.40
  62.9 2.8 %broadcast_select_fusion = f32[144,8,384]{2,0,1:T(8,128)} fusion(f32[144,8,384]{2,0,1:T(8,128)} %copy.40, pred[8,384]{1,0:T(8,128)(4,1)S(1)} %compare_and_fusion), kind=kLoop, calls=%fused_computation.115 | loop fusion | flops 442368 | bytes 3542016 | tf_op jit(solution)/shard_map/jit(_take)/select_n | solution.py:136
  65.7 5.7 %all-to-all-start = ((f32[144,8,384]{2,0,1:T(8,128)}), f32[144,8,384]{2,0,1:T(8,128)S(1)}, u32[]{:S(2)}, u32[]{:S(2)}) async-start(f32[144,8,384]{2,0,1:T(8,128)} %broadcast_select_fusion), calls=%async_computation | async-start | bytes 3538944 | tf_op jit(solution)/shard_map/all_to_all | solution.py:137
  81.4 32.0 %all-to-all-done = f32[144,8,384]{2,0,1:T(8,128)S(1)} async-done(((f32[144,8,384]{2,0,1:T(8,128)}), f32[144,8,384]{2,0,1:T(8,128)S(1)}, u32[]{:S(2)}, u32[]{:S(2)}) %all-to-all-start) | async-done | bytes 1769504 | tf_op jit(solution)/shard_map/all_to_all | solution.py:137
  114.6 1.5 reshape.189
  116.7 5.0 %subtract_multiply_fusion.1 = (f32[32,36,384]{2,1,0:T(8,128)S(1)}, f32[32,36,384]{2,1,0:T(8,128)S(1)}) fusion(s32[]{:T(128)S(6)} %select_n.151, f32[32,36,384]{2,1,0:T(8,128)S(1)} %get-tuple-element.27, s32[]{:T(128)S(6)} %select_n.147, f32[32,36,384]{2,1,0:T(8,128)S(1)} %get-tuple-element.26, f32[32,36,384]{2,1,0:T(8,128)S(1)} %reshape.189, ...), kind=kLoop, calls=%fused_computation.114 | loop fusion | flops 9732096 | bytes 8847504 | tf_op jit(solution)/shard_map/mul | solution.py:87
  121.7 1.4 fusion.62
  123.2 1.4 fusion.60
  124.6 4.3 %fusion.76 = (bf16[32,36,384]{2,1,0:T(8,128)(2,1)S(1)}, f32[32,36,384]{2,1,0:T(8,128)S(1)}) fusion(s32[]{:T(128)S(6)} %select_n.151, f32[32,36,384]{2,1,0:T(8,128)S(1)} %get-tuple-element.33, s32[]{:T(128)S(6)} %select_n.147, f32[32,36,384]{2,1,0:T(8,128)S(1)} %get-tuple-element.32, f32[32,36,384]{2,1,0:T(8,128)S(1)} %get-tuple-element.25, ...), kind=kLoop, calls=%fused_computation.156 | loop fusion | flops 5750784 | bytes 13271056 | tf_op jit(solution)/shard_map/convert_element_type | solution.py:142
  130.3 3.8 %all-to-all-start.1 = ((f32[8,144,384]{2,1,0:T(8,128)}), f32[8,144,384]{2,1,0:T(8,128)S(1)}, u32[]{:S(2)}, u32[]{:S(2)}) async-start(f32[8,144,384]{2,1,0:T(8,128)} %all_to_all.26), calls=%async_computation.1 | async-start | bytes 3538944 | tf_op jit(solution)/shard_map/all_to_all | solution.py:139
  135.2 40.6 %all-to-all-done.1 = f32[8,144,384]{2,1,0:T(8,128)S(1)} async-done(((f32[8,144,384]{2,1,0:T(8,128)}), f32[8,144,384]{2,1,0:T(8,128)S(1)}, u32[]{:S(2)}, u32[]{:S(2)}) %all-to-all-start.1) | async-done | bytes 1769504 | tf_op jit(solution)/shard_map/all_to_all | solution.py:139
  177.2 2.1 %copy.42 = f32[3072,144]{1,0:T(8,128)S(1)} copy(f32[3072,144]{0,1:T(8,128)} %bitcast.28) | data formatting | bytes 3538944 | tf_op jit(solution)/shard_map/all_to_all | solution.py:139
  179.4 21.2 %scatter_fusion = f32[144,4096]{0,1:T(8,128)} fusion(f32[144,4096]{0,1:T(8,128)} %bitcast.23, s32[3072]{0:T(1024)S(1)} %bitcast.34, f32[3072,144]{1,0:T(8,128)S(1)} %copy.42), kind=kCustom, calls=%fused_computation.1 | custom fusion | flops 442368 | bytes 5320704 | tf_op jit(solution)/shard_map/scatter-add | solution.py:140
  200.5 4.8 %copy.43 = f32[144,32,128]{2,1,0:T(8,128)} copy(f32[144,32,128]{0,2,1:T(8,128)} %bitcast.24) | data formatting | bytes 4718592
  (48 shorter events, 17.3 us)
Async XLA Ops:
  0.6 9.5 %copy-start.6 = (f32[32]{0:T(128)S(1)}, f32[32]{0:T(128)}, u32[]{:S(2)}) copy-start(f32[32]{0:T(128)} %param.15) | copy-start | bytes 388
  0.6 9.5 %copy-start.7 = (f32[32]{0:T(128)S(1)}, f32[32]{0:T(128)}, u32[]{:S(2)}) copy-start(f32[32]{0:T(128)} %param.14) | copy-start | bytes 388
  0.7 9.6 %copy-start.3 = (s32[32,128]{1,0:T(8,128)S(1)}, s32[32,128]{1,0:T(8,128)}, u32[]{:S(2)}) copy-start(s32[32,128]{1,0:T(8,128)} %param.13) | copy-start | bytes 49156
  2.0 18.7 %copy-start = (f32[144,32,128]{2,1,0:T(8,128)S(1)}, f32[144,32,128]{2,1,0:T(8,128)}, u32[]{:S(2)}) copy-start(f32[144,32,128]{2,1,0:T(8,128)} %param.11) | copy-start | bytes 7077892
  2.0 18.7 %copy-start.2 = (f32[32,128]{1,0:T(8,128)S(1)}, f32[32,128]{1,0:T(8,128)}, u32[]{:S(2)}) copy-start(f32[32,128]{1,0:T(8,128)} %param.12) | copy-start | bytes 49156
  2.1 15.1 %collective-permute-start.1 = (f32[145,6,128]{2,0,1:T(8,128)S(1)}, f32[145,6,128]{2,0,1:T(8,128)S(1)}, u32[]{:S(2)}, u32[]{:S(2)}) collective-permute-start(f32[145,6,128]{2,0,1:T(8,128)S(1)} %copy.36), channel_id=1, source_target_pairs={{1,0},{3,2},{5,4},{7,6},{9,8},{11,10},{13,12},{15,14},{17,16},{19,... | collective-permute-start | bytes 1336328 | tf_op jit(solution)/shard_map/ppermute | solution.py:27
  4.4 15.2 %collective-permute-start = (f32[145,6,128]{2,0,1:T(8,128)}, f32[145,6,128]{2,0,1:T(8,128)}, u32[]{:S(2)}, u32[]{:S(2)}) collective-permute-start(f32[145,6,128]{2,0,1:T(8,128)} %copy.35), channel_id=1, source_target_pairs={{0,1},{2,3},{4,5},{6,7},{8,9},{10,11},{12,13},{14,15},{16,17},{18,... | collective-permute-start | bytes 1336328 | tf_op jit(solution)/shard_map/ppermute | solution.py:24
  62.9 8.5 %copy-start.4 = (s32[4]{0:T(128)S(1)}, s32[4]{0:T(128)}, u32[]{:S(2)}) copy-start(s32[4]{0:T(128)} %param.17) | copy-start | bytes 52
  62.9 17.2 %copy-start.5 = (f32[32]{0:T(128)S(1)}, f32[32]{0:T(128)}, u32[]{:S(2)}) copy-start(f32[32]{0:T(128)} %param.16) | copy-start | bytes 388
  65.7 47.7 %all-to-all-start = ((f32[144,8,384]{2,0,1:T(8,128)}), f32[144,8,384]{2,0,1:T(8,128)S(1)}, u32[]{:S(2)}, u32[]{:S(2)}) async-start(f32[144,8,384]{2,0,1:T(8,128)} %broadcast_select_fusion), calls=%async_computation | async-start | bytes 3538944 | tf_op jit(solution)/shard_map/all_to_all | solution.py:137
  113.4 1.2 copy-start.1
  130.3 45.5 %all-to-all-start.1 = ((f32[8,144,384]{2,1,0:T(8,128)}), f32[8,144,384]{2,1,0:T(8,128)S(1)}, u32[]{:S(2)}, u32[]{:S(2)}) async-start(f32[8,144,384]{2,1,0:T(8,128)} %all_to_all.26), calls=%async_computation.1 | async-start | bytes 3538944 | tf_op jit(solution)/shard_map/all_to_all | solution.py:139
where the time goes:
time: 206 us; the launch traced here: 205 us
  waiting for transfers between devices  81.7 us (40%)
  other arithmetic  63.4 us (31%)
  local copies, waits for them, and re-layouts  34.7 us (17%)
  starting transfers between devices  16.6 us (8%)
  between operations  8.97 us (4%)
    all_to_all x1, waiting for transfers between devices, on_device(): lax.all_to_all(source_terms, 'spec', split_axis=0, concat_axis=1, tiled=T...  40.6 us
    all_to_all x1, waiting for transfers between devices, on_device(): lax.all_to_all(columns, 'spec', split_axis=1, concat_axis=0, tiled=True)  32 us
    scatter-add x1, other arithmetic, on_device(): new_cells = flat_cells.at[:, sea_cells].add(returned)  21.2 us
    mul x4, other arithmetic, quickest(): face_flux = courant * face_value  16.3 us
    gather x2, local copies, waits for them, and re-layouts, on_device(): columns = jnp.take(flat_cells, sea_cells, axis=1)  14 us
    ppermute x1, waiting for transfers between devices, extended_2(): lax.ppermute(lax.slice_in_dim(block, 0, width, axis=dim), axis, backward)  6.81 us
    unnamed x18, local copies, waits for them, and re-layouts  6.19 us
    all_to_all x1, starting transfers between devices, on_device(): lax.all_to_all(columns, 'spec', split_axis=1, concat_axis=0, tiled=True)  5.7 us
  transfers between devices with their start and end apart: 4, of which 4 were waited for; matrix products, arithmetic and copies ran while one was open for 2% of the time, Pallas kernels for 0%

commit v1 on v0

--- a/solution.py
+++ b/solution.py
@@ -136,9 +136,9 @@
     columns = jnp.take(flat_cells, sea_cells, axis=1)
     gathered = lax.all_to_all(columns, "spec", split_axis=1, concat_axis=0, tiled=True)
     source_terms = interact(gathered, coupling, quad_offsets)
-    returned = lax.all_to_all(source_terms, "spec", split_axis=0, concat_axis=1, tiled=True)
-    new_cells = flat_cells.at[:, sea_cells].add(returned)
-    updated = new_cells.reshape(smoothed.shape)
+    returned = lax.all_to_all(source_terms.T, "spec", split_axis=1, concat_axis=0, tiled=True)
+    placed = jnp.zeros((flat_cells.shape[1], local_comps), jnp.float32).at[sea_cells].set(returned)
+    updated = (flat_cells + placed.T).reshape(smoothed.shape)
     return (updated, source_terms.astype(jnp.bfloat16)[None])
 
 

time: 206 us -> 209 us (1.015)
  local copies, waits for them, and re-layouts: 34.7 us -> 49.3 us
  other arithmetic: 63.4 us -> 51.5 us
    scatter-add x1 -> x0, other arithmetic: 21.2 us -> none  [on_device(): new_cells = flat_cells.at[:, sea_cells].add(returned)]
    scatter x0 -> x1, local copies, waits for them, and re-layouts: none -> 15.8 us  [on_device(): jnp.zeros((flat_cells.shape[1], local_comps), jnp.float32).at[sea_cells]]
    add x0 -> x1, other arithmetic: none -> 5.98 us  [on_device(): updated = (flat_cells + placed.T).reshape(smoothed.shape)]
    all_to_all x3 -> x1, local copies, waits for them, and re-layouts: 4.92 us -> 2.33 us  [on_device(): lax.all_to_all(source_terms.T, 'spec', split_axis=1, concat_axis=0, tiled...]
    convert_element_type x1, other arithmetic: 4.28 us -> 6.37 us  [on_device(): return (updated, source_terms.astype(jnp.bfloat16)[None])]
where the time goes in v1:
time: 209 us; the launch traced here: 208 us
  waiting for transfers between devices  82.2 us (39%)
  other arithmetic  51.5 us (25%)
  local copies, waits for them, and re-layouts  49.3 us (24%)
  starting transfers between devices  16.4 us (8%)
  between operations  8.73 us (4%)
    all_to_all x1, waiting for transfers between devices, on_device(): lax.all_to_all(source_terms.T, 'spec', split_axis=1, concat_axis=0, tiled...  40.9 us
    all_to_all x1, waiting for transfers between devices, on_device(): lax.all_to_all(columns, 'spec', split_axis=1, concat_axis=0, tiled=True)  32.3 us
    mul x4, other arithmetic, quickest(): face_flux = courant * face_value  16.3 us
    scatter x1, local copies, waits for them, and re-layouts, on_device(): jnp.zeros((flat_cells.shape[1], local_comps), jnp.float32).at[sea_cells]  15.8 us
    gather x2, local copies, waits for them, and re-layouts, on_device(): columns = jnp.take(flat_cells, sea_cells, axis=1)  14 us
    ppermute x1, waiting for transfers between devices, extended_2(): lax.ppermute(lax.slice_in_dim(block, 0, width, axis=dim), axis, backward)  6.81 us
    convert_element_type x1, other arithmetic, on_device(): return (updated, source_terms.astype(jnp.bfloat16)[None])  6.37 us
    unnamed x18, local copies, waits for them, and re-layouts  6.19 us
  transfers between devices with their start and end apart: 4, of which 4 were waited for; matrix products, arithmetic and copies ran while one was open for 2% of the time, Pallas kernels for 0%

profile of v1, /device:TPU:0, one launch (start us, length us, event | category | flops | bytes accessed | tf_op | source)
XLA Modules:
  0.0 208.1 jit_solution(6400977625691144015)
XLA Ops:
  4.4 5.7 %collective-permute-start = (f32[145,6,128]{2,0,1:T(8,128)}, f32[145,6,128]{2,0,1:T(8,128)}, u32[]{:S(2)}, u32[]{:S(2)}) collective-permute-start(f32[145,6,128]{2,0,1:T(8,128)} %copy.28), channel_id=1, source_target_pairs={{0,1},{2,3},{4,5},{6,7},{8,9},{10,11},{12,13},{14,15},{16,17},{18,... | collective-permute-start | bytes 1336328 | tf_op jit(solution)/shard_map/ppermute | solution.py:24
  10.4 6.8 %collective-permute-done.1 = f32[145,6,128]{2,0,1:T(8,128)S(1)} collective-permute-done((f32[145,6,128]{2,0,1:T(8,128)S(1)}, f32[145,6,128]{2,0,1:T(8,128)S(1)}, u32[]{:S(2)}, u32[]{:S(2)}) %collective-permute-start.1) | collective-permute-done | bytes 445472 | tf_op jit(solution)/shard_map/ppermute | solution.py:27
  17.4 2.2 %collective-permute-done = f32[145,6,128]{2,0,1:T(8,128)} collective-permute-done((f32[145,6,128]{2,0,1:T(8,128)}, f32[145,6,128]{2,0,1:T(8,128)}, u32[]{:S(2)}, u32[]{:S(2)}) %collective-permute-start) | collective-permute-done | bytes 445472 | tf_op jit(solution)/shard_map/ppermute | solution.py:24
  21.3 2.8 %fusion.18 = f32[144,41,128]{2,1,0:T(8,128)S(1)} fusion(f32[145,44,128]{2,1,0:T(8,128)S(1)} %pad_maximum_fusion, f32[144]{0:T(256)S(1)} %get-tuple-element.39, f32[144]{0:T(256)S(1)} %get-tuple-element.38, f32[144]{0:T(256)S(1)} %get-tuple-element.37, pred[144]{0:T(512)(128)(4,1)S(1)} %get-tuple-element.36), kind=kLoop, calls=%fused_computation.51 | loop fusion | flops 11335680 | bytes 15116112 | tf_op jit(solution)/shard_map/mul | solution.py:56
  25.2 5.4 %fusion.4 = f32[144,40,129]{2,1,0:T(8,128)S(1)} fusion(f32[144,40,128]{2,1,0:T(8,128)S(1)} %fusion.29, f32[144]{0:T(256)S(1)} %get-tuple-element.35, f32[144]{0:T(256)S(1)} %get-tuple-element.34, f32[144]{0:T(256)S(1)} %get-tuple-element.19, pred[144]{0:T(512)(128)(4,1)S(1)} %get-tuple-element.18), kind=kLoop, calls=%fused_computation.18 | loop fusion | flops 11145600 | bytes 5923152 | tf_op jit(solution)/shard_map/mul | solution.py:56
  31.5 2.6 %fusion.26 = f32[144,37,128]{2,1,0:T(8,128)S(1)} fusion(f32[144,40,128]{2,1,0:T(8,128)S(1)} %fusion.28, f32[144]{0:T(256)S(1)} %get-tuple-element.39, f32[144]{0:T(256)S(1)} %get-tuple-element.38, f32[144]{0:T(256)S(1)} %get-tuple-element.37, pred[144]{0:T(512)(128)(4,1)S(1)} %get-tuple-element.36), kind=kLoop, calls=%fused_computation.71 | loop fusion | flops 10229760 | bytes 13641552 | tf_op jit(solution)/shard_map/mul | solution.py:56
  35.0 5.4 %fusion.11 = f32[144,36,129]{2,1,0:T(8,128)S(1)} fusion(f32[144,36,128]{2,1,0:T(8,128)S(1)} %fusion.21, f32[144]{0:T(256)S(1)} %get-tuple-element.35, f32[144]{0:T(256)S(1)} %get-tuple-element.34, f32[144]{0:T(256)S(1)} %get-tuple-element.19, pred[144]{0:T(512)(128)(4,1)S(1)} %get-tuple-element.18), kind=kLoop, calls=%fused_computation.25 | loop fusion | flops 10031040 | bytes 5331024 | tf_op jit(solution)/shard_map/mul | solution.py:56
  41.6 3.9 %fusion.36 = f32[144,32,128]{2,1,0:T(8,128)S(1)} fusion(f32[144,32,128]{2,1,0:T(8,128)S(1)} %slice.218, f32[144,36,128]{2,1,0:T(8,128)S(1)} %fusion.20, f32[32,128]{1,0:T(8,128)S(1)} %copy-done.2, f32[144]{0:T(256)S(1)} %get-tuple-element.33, f32[144]{0:T(256)S(1)} %get-tuple-element.32), kind=kLoop, calls=%fused_computation.84 | loop fusion | flops 11796480 | bytes 14173312 | tf_op jit(solution)/shard_map/mul | solution.py:131
  45.5 3.3 %copy.32 = f32[144,32,128]{0,2,1:T(8,128)} copy(f32[144,32,128]{2,1,0:T(8,128)S(1)} %fusion.36) | data formatting | bytes 4718592 | tf_op jit(solution)/shard_map/mul | solution.py:131
  48.8 12.0 %gather_fusion = f32[3072,144]{1,0:T(8,128)S(1)} fusion(f32[144,4096]{0,1:T(8,128)} %bitcast.26, s32[3072]{0:T(1024)S(1)} %broadcast_clamp_fusion), kind=kCustom, calls=%fused_computation | custom fusion | bytes 3551232 | tf_op jit(solution)/shard_map/jit(_take)/gather | solution.py:136
  60.8 2.0 copy.33
  62.9 2.8 %broadcast_select_fusion = f32[144,8,384]{2,0,1:T(8,128)} fusion(f32[144,8,384]{2,0,1:T(8,128)} %copy.33, pred[8,384]{1,0:T(8,128)(4,1)S(1)} %compare_and_fusion), kind=kLoop, calls=%fused_computation.118 | loop fusion | flops 442368 | bytes 3542016 | tf_op jit(solution)/shard_map/jit(_take)/select_n | solution.py:136
  65.7 5.7 %all-to-all-start = ((f32[144,8,384]{2,0,1:T(8,128)}), f32[144,8,384]{2,0,1:T(8,128)S(1)}, u32[]{:S(2)}, u32[]{:S(2)}) async-start(f32[144,8,384]{2,0,1:T(8,128)} %broadcast_select_fusion), calls=%async_computation | async-start | bytes 3538944 | tf_op jit(solution)/shard_map/all_to_all | solution.py:137
  81.1 32.3 %all-to-all-done = f32[144,8,384]{2,0,1:T(8,128)S(1)} async-done(((f32[144,8,384]{2,0,1:T(8,128)}), f32[144,8,384]{2,0,1:T(8,128)S(1)}, u32[]{:S(2)}, u32[]{:S(2)}) %all-to-all-start) | async-done | bytes 1769504 | tf_op jit(solution)/shard_map/all_to_all | solution.py:137
  114.6 1.5 reshape.190
  116.7 5.0 %subtract_multiply_fusion.1 = (f32[32,36,384]{2,1,0:T(8,128)S(1)}, f32[32,36,384]{2,1,0:T(8,128)S(1)}) fusion(s32[]{:T(128)S(6)} %select_n.151, f32[32,36,384]{2,1,0:T(8,128)S(1)} %get-tuple-element.25, s32[]{:T(128)S(6)} %select_n.147, f32[32,36,384]{2,1,0:T(8,128)S(1)} %get-tuple-element.24, f32[32,36,384]{2,1,0:T(8,128)S(1)} %reshape.190, ...), kind=kLoop, calls=%fused_computation.117 | loop fusion | flops 9732096 | bytes 8847504 | tf_op jit(solution)/shard_map/mul | solution.py:87
  121.7 4.2 %fusion.62 = (f32[32,36,384]{2,1,0:T(8,128)S(1)}, f32[32,36,384]{2,1,0:T(8,128)}, f32[32,36,384]{2,1,0:T(8,128)}, f32[32,36,384]{2,1,0:T(8,128)}) fusion(s32[]{:T(128)S(6)} %select_n.153, f32[32,36,384]{2,1,0:T(8,128)S(1)} %get-tuple-element.23, s32[]{:T(128)S(6)} %select_n.157, f32[32,36,384]{2,1,0:T(8,128)S(1)} %get-tuple-element.22), kind=kLoop, calls=%fused_computation.113 | loop fusion | flops 1769472 | bytes 10616840 | tf_op jit(solution)/shard_map/jit(_roll_dynamic)/concatenate | solution.py:92
  125.9 6.4 %fusion.78 = (bf16[32,36,384]{2,1,0:T(8,128)(2,1)S(1)}, f32[32,36,384]{2,1,0:T(8,128)S(1)}) fusion(s32[]{:T(128)S(6)} %select_n.151, f32[32,36,384]{2,1,0:T(8,128)} %get-tuple-element.31, s32[]{:T(128)S(6)} %select_n.147, f32[32,36,384]{2,1,0:T(8,128)S(1)} %get-tuple-element.30, f32[32,36,384]{2,1,0:T(8,128)S(1)} %get-tuple-element.23, s32[]{:T(128)S(6)} %select_n.159, ...), kind=kLoop, calls=%fused_computation.159 | loop fusion | flops 5750784 | bytes 13271056 | tf_op jit(solution)/shard_map/convert_element_type | solution.py:142
  133.6 3.6 %all-to-all-start.1 = ((f32[384,8,144]{0,2,1:T(8,128)}), f32[384,8,144]{0,2,1:T(8,128)S(1)}, u32[]{:S(2)}, u32[]{:S(2)}) async-start(f32[384,8,144]{0,2,1:T(8,128)} %bitcast.30), calls=%async_computation.1 | async-start | bytes 3538944 | tf_op jit(solution)/shard_map/all_to_all | solution.py:139
  138.3 40.9 %all-to-all-done.1 = f32[384,8,144]{0,2,1:T(8,128)S(1)} async-done(((f32[384,8,144]{0,2,1:T(8,128)}), f32[384,8,144]{0,2,1:T(8,128)S(1)}, u32[]{:S(2)}, u32[]{:S(2)}) %all-to-all-start.1) | async-done | bytes 1769504 | tf_op jit(solution)/shard_map/all_to_all | solution.py:139
  179.2 2.3 %copy.34 = f32[8,384,144]{2,1,0:T(8,128)} copy(f32[8,384,144]{1,2,0:T(8,128)S(1)} %bitcast.31) | data formatting | bytes 3538944 | tf_op jit(solution)/shard_map/all_to_all | solution.py:139
  181.5 15.8 %scatter_custom_fusion = f32[4096,144]{1,0:T(8,128)} fusion(s32[3072]{0:T(1024)S(1)} %bitcast.39, f32[3072,144]{1,0:T(8,128)} %bitcast.32, f32[]{:T(128)} %constant.68.clone.1), kind=kCustom, calls=%fused_computation.97 | custom fusion | bytes 2359808 | tf_op jit(solution)/shard_map/scatter | solution.py:140
  197.3 6.0 %bitcast_add_fusion = f32[144,4096]{0,1:T(8,128)} fusion(f32[4096,144]{1,0:T(8,128)} %scatter_custom_fusion, f32[144,32,128]{0,2,1:T(8,128)} %copy.32), kind=kLoop, calls=%fused_computation.36 | loop fusion | flops 589824 | bytes 7077888 | tf_op jit(solution)/shard_map/add | solution.py:141
  203.3 4.8 %copy.35 = f32[144,32,128]{2,1,0:T(8,128)} copy(f32[144,32,128]{0,2,1:T(8,128)} %bitcast.27) | data formatting | bytes 4718592
  (48 shorter events, 15.8 us)
Async XLA Ops:
  0.6 9.5 %copy-start.6 = (f32[32]{0:T(128)S(1)}, f32[32]{0:T(128)}, u32[]{:S(2)}) copy-start(f32[32]{0:T(128)} %param.15) | copy-start | bytes 388
  0.6 9.5 %copy-start.7 = (f32[32]{0:T(128)S(1)}, f32[32]{0:T(128)}, u32[]{:S(2)}) copy-start(f32[32]{0:T(128)} %param.14) | copy-start | bytes 388
  0.7 9.7 %copy-start.3 = (s32[32,128]{1,0:T(8,128)S(1)}, s32[32,128]{1,0:T(8,128)}, u32[]{:S(2)}) copy-start(s32[32,128]{1,0:T(8,128)} %param.13) | copy-start | bytes 49156
  2.0 18.7 %copy-start = (f32[144,32,128]{2,1,0:T(8,128)S(1)}, f32[144,32,128]{2,1,0:T(8,128)}, u32[]{:S(2)}) copy-start(f32[144,32,128]{2,1,0:T(8,128)} %param.11) | copy-start | bytes 7077892
  2.0 18.7 %copy-start.2 = (f32[32,128]{1,0:T(8,128)S(1)}, f32[32,128]{1,0:T(8,128)}, u32[]{:S(2)}) copy-start(f32[32,128]{1,0:T(8,128)} %param.12) | copy-start | bytes 49156
  2.1 15.1 %collective-permute-start.1 = (f32[145,6,128]{2,0,1:T(8,128)S(1)}, f32[145,6,128]{2,0,1:T(8,128)S(1)}, u32[]{:S(2)}, u32[]{:S(2)}) collective-permute-start(f32[145,6,128]{2,0,1:T(8,128)S(1)} %copy.29), channel_id=1, source_target_pairs={{1,0},{3,2},{5,4},{7,6},{9,8},{11,10},{13,12},{15,14},{17,16},{19,... | collective-permute-start | bytes 1336328 | tf_op jit(solution)/shard_map/ppermute | solution.py:27
  4.4 15.2 %collective-permute-start = (f32[145,6,128]{2,0,1:T(8,128)}, f32[145,6,128]{2,0,1:T(8,128)}, u32[]{:S(2)}, u32[]{:S(2)}) collective-permute-start(f32[145,6,128]{2,0,1:T(8,128)} %copy.28), channel_id=1, source_target_pairs={{0,1},{2,3},{4,5},{6,7},{8,9},{10,11},{12,13},{14,15},{16,17},{18,... | collective-permute-start | bytes 1336328 | tf_op jit(solution)/shard_map/ppermute | solution.py:24
  62.9 8.5 %copy-start.4 = (s32[4]{0:T(128)S(1)}, s32[4]{0:T(128)}, u32[]{:S(2)}) copy-start(s32[4]{0:T(128)} %param.17) | copy-start | bytes 52
  62.9 16.9 %copy-start.5 = (f32[32]{0:T(128)S(1)}, f32[32]{0:T(128)}, u32[]{:S(2)}) copy-start(f32[32]{0:T(128)} %param.16) | copy-start | bytes 388
  65.7 47.7 %all-to-all-start = ((f32[144,8,384]{2,0,1:T(8,128)}), f32[144,8,384]{2,0,1:T(8,128)S(1)}, u32[]{:S(2)}, u32[]{:S(2)}) async-start(f32[144,8,384]{2,0,1:T(8,128)} %broadcast_select_fusion), calls=%async_computation | async-start | bytes 3538944 | tf_op jit(solution)/shard_map/all_to_all | solution.py:137
  113.4 1.2 copy-start.1
  133.6 45.5 %all-to-all-start.1 = ((f32[384,8,144]{0,2,1:T(8,128)}), f32[384,8,144]{0,2,1:T(8,128)S(1)}, u32[]{:S(2)}, u32[]{:S(2)}) async-start(f32[384,8,144]{0,2,1:T(8,128)} %bitcast.30), calls=%async_computation.1 | async-start | bytes 3538944 | tf_op jit(solution)/shard_map/all_to_all | solution.py:139

commit v2 on v0

--- a/solution.py
+++ b/solution.py
@@ -3,6 +3,8 @@
 import jax
 import jax.numpy as jnp
 from jax import lax
+from jax.experimental import pallas as pl
+from jax.experimental.pallas import tpu as pltpu
 from jax.sharding import PartitionSpec as P
 
 NDIR = 36
@@ -69,29 +71,60 @@
     return 4.0 / 3.0 * near_sum - 1.0 / 12.0 * far_sum
 
 
-def interact(columns, coupling, quad_offsets):
-    initial = columns.shape
-    spectra = columns.reshape(NFREQ, NDIR, -1)
-    up_freq = quad_offsets[0]
-    down_freq = quad_offsets[1]
-    dir_one = quad_offsets[2]
-    dir_two = quad_offsets[3]
-    freq_index = lax.iota(jnp.int32, NFREQ)[:, None, None]
-    inside = ((freq_index + up_freq < NFREQ) & (freq_index - down_freq >= 0)).astype(jnp.float32)
-    weight = coupling[:, None, None] * inside
-    source_sum = jnp.zeros_like(spectra)
-    for mirror in (1, -1):
-        upper_bin = jnp.roll(jnp.roll(spectra, -up_freq, 0), -mirror * dir_one, 1)
-        lower_bin = jnp.roll(jnp.roll(spectra, down_freq, 0), mirror * dir_two, 1)
+def interact_kernel(off_ref, w_ref, e_ref, s_ref, t_ref):
+    up_freq = off_ref[0]
+    down_freq = off_ref[1]
+    dir_one = off_ref[2]
+    dir_two = off_ref[3]
+    weight = w_ref[...]
+    up_shift = (NFREQ - up_freq) % NFREQ
+    down_shift = down_freq % NFREQ
+
+    def transfers(d, carry):
+        spectra = e_ref[d]
         squared = spectra * spectra
-        transfer = weight * (
-            squared * (upper_bin * gain_up + lower_bin * gain_down)
-            - 2.0 * gain_cross * spectra * upper_bin * lower_bin
-        )
-        source_sum = source_sum - 2.0 * transfer
-        source_sum = source_sum + jnp.roll(jnp.roll(transfer, up_freq, 0), mirror * dir_one, 1)
-        source_sum = source_sum + jnp.roll(jnp.roll(transfer, -down_freq, 0), -mirror * dir_two, 1)
-    return source_sum.reshape(initial)
+        for slot, mirror in enumerate((1, -1)):
+            upper_bin = pltpu.roll(e_ref[(d + mirror * dir_one) % NDIR], up_shift, 0)
+            lower_bin = pltpu.roll(e_ref[(d - mirror * dir_two) % NDIR], down_shift, 0)
+            t_ref[slot, d] = weight * (
+                squared * (upper_bin * gain_up + lower_bin * gain_down)
+                - 2.0 * gain_cross * spectra * upper_bin * lower_bin
+            )
+        return carry
+
+    lax.fori_loop(0, NDIR, transfers, 0)
+
+    def sources(d, carry):
+        total = -2.0 * t_ref[0, d] - 2.0 * t_ref[1, d]
+        for slot, mirror in enumerate((1, -1)):
+            total = total + pltpu.roll(t_ref[slot, (d - mirror * dir_one) % NDIR], up_freq % NFREQ, 0)
+            total = total + pltpu.roll(
+                t_ref[slot, (d + mirror * dir_two) % NDIR], (NFREQ - down_freq) % NFREQ, 0
+            )
+        s_ref[d] = total
+        return carry
+
+    lax.fori_loop(0, NDIR, sources, 0)
+
+
+def interact_pallas(columns, coupling, quad_offsets):
+    comps, points = columns.shape
+    spectra = columns.reshape(NFREQ, NDIR, points).transpose(1, 0, 2)
+    freq_index = lax.iota(jnp.int32, NFREQ)
+    inside = ((freq_index + quad_offsets[0] < NFREQ) & (freq_index - quad_offsets[1] >= 0)).astype(jnp.float32)
+    weight = (coupling * inside)[:, None]
+    out = pl.pallas_call(
+        interact_kernel,
+        out_shape=jax.ShapeDtypeStruct((NDIR, NFREQ, points), jnp.float32),
+        in_specs=[
+            pl.BlockSpec(memory_space=pltpu.SMEM),
+            pl.BlockSpec(memory_space=pltpu.VMEM),
+            pl.BlockSpec(memory_space=pltpu.VMEM),
+        ],
+        out_specs=pl.BlockSpec(memory_space=pltpu.VMEM),
+        scratch_shapes=[pltpu.VMEM((2, NDIR, NFREQ, points), jnp.float32)],
+    )(quad_offsets, weight, spectra)
+    return out.transpose(1, 0, 2).reshape(comps, points)
 
 
 def per_component(lookup, freq_index):
@@ -135,7 +168,7 @@
     sea_cells = sea_order.reshape(-1)[:SEA_MAX]
     columns = jnp.take(flat_cells, sea_cells, axis=1)
     gathered = lax.all_to_all(columns, "spec", split_axis=1, concat_axis=0, tiled=True)
-    source_terms = interact(gathered, coupling, quad_offsets)
+    source_terms = interact_pallas(gathered, coupling, quad_offsets)
     returned = lax.all_to_all(source_terms, "spec", split_axis=0, concat_axis=1, tiled=True)
     new_cells = flat_cells.at[:, sea_cells].add(returned)
     updated = new_cells.reshape(smoothed.shape)

time: 206 us -> 207 us (level)
  other arithmetic: 63.4 us -> 51.3 us
  between operations: 8.97 us -> 0.94 us
  Pallas kernels: 0 us -> 7.27 us
  local copies, waits for them, and re-layouts: 34.7 us -> 41.8 us
  waiting for transfers between devices: 81.7 us -> 88.8 us
    all_to_all x1, waiting for transfers between devices: 32 us -> 39.3 us  [on_device(): lax.all_to_all(columns, 'spec', split_axis=1, concat_axis=0, tiled=True)]
    pallas_call x0 -> x1, Pallas kernels: none -> 7.27 us  [interact_pallas(): pl.pallas_call(interact_kernel, out_shape=jax.ShapeDtypeStruct((NDIR, NFR...]
    mul x2 -> x0, other arithmetic: 6.36 us -> none  [the longest x1 5.03 us: interact(): weight * (squared * (upper_bin * gain_up + lower_bin * gain_down) - 2.0 *...]
    convert_element_type x1, other arithmetic: 4.28 us -> 0.11 us  [on_device(): return (updated, source_terms.astype(jnp.bfloat16)[None])]
    transpose x0 -> x1, local copies, waits for them, and re-layouts: none -> 3.78 us  [interact_pallas(): return out.transpose(1, 0, 2).reshape(comps, points)]
    concatenate x2 -> x0, other arithmetic: 2.88 us -> none  [interact(): jnp.roll(transfer, up_freq, 0)]
    unnamed x18 -> x19, local copies, waits for them, and re-layouts: 6.19 us -> 6.07 us
  transfers between devices with their start and end apart: 4 -> 4, of which waited for: 4 -> 4; matrix products, arithmetic and copies ran while one was open for 2% -> 3% of each run, Pallas kernels for 0% -> 0%
where the time goes in v2:
time: 207 us; the launch traced here: 206 us
  waiting for transfers between devices  88.8 us (43%)
  other arithmetic  51.3 us (25%)
  local copies, waits for them, and re-layouts  41.8 us (20%)
  starting transfers between devices  16.4 us (8%)
  Pallas kernels  7.27 us (4%)
    all_to_all x1, waiting for transfers between devices, on_device(): lax.all_to_all(source_terms, 'spec', split_axis=0, concat_axis=1, tiled=T...  40.4 us
    all_to_all x1, waiting for transfers between devices, on_device(): lax.all_to_all(columns, 'spec', split_axis=1, concat_axis=0, tiled=True)  39.3 us
    scatter-add x1, other arithmetic, on_device(): new_cells = flat_cells.at[:, sea_cells].add(returned)  21.1 us
    mul x4, other arithmetic, quickest(): face_flux = courant * face_value  16.3 us
    gather x2, local copies, waits for them, and re-layouts, on_device(): columns = jnp.take(flat_cells, sea_cells, axis=1)  14 us
    pallas_call x1, Pallas kernels, interact_pallas(): pl.pallas_call(interact_kernel, out_shape=jax.ShapeDtypeStruct((NDIR, NFR...  7.27 us
    ppermute x1, waiting for transfers between devices, extended_2(): lax.ppermute(lax.slice_in_dim(block, 0, width, axis=dim), axis, backward)  6.8 us
    all_to_all x3, local copies, waits for them, and re-layouts, on_device(): lax.all_to_all(source_terms, 'spec', split_axis=0, concat_axis=1, tiled=T...  6.21 us
  transfers between devices with their start and end apart: 4, of which 4 were waited for; matrix products, arithmetic and copies ran while one was open for 3% of the time, Pallas kernels for 0%

profile of v2, /device:TPU:0, one launch (start us, length us, event | category | flops | bytes accessed | tf_op | source)
XLA Modules:
  0.0 206.5 jit_solution(3040604123179642178)
XLA Ops:
  4.4 5.7 %collective-permute-start = (f32[145,6,128]{2,0,1:T(8,128)}, f32[145,6,128]{2,0,1:T(8,128)}, u32[]{:S(2)}, u32[]{:S(2)}) collective-permute-start(f32[145,6,128]{2,0,1:T(8,128)} %copy.51), channel_id=1, source_target_pairs={{0,1},{2,3},{4,5},{6,7},{8,9},{10,11},{12,13},{14,15},{16,17},{18,... | collective-permute-start | bytes 1336328 | tf_op jit(solution)/shard_map/ppermute | solution.py:26
  10.4 6.8 %collective-permute-done.1 = f32[145,6,128]{2,0,1:T(8,128)S(1)} collective-permute-done((f32[145,6,128]{2,0,1:T(8,128)S(1)}, f32[145,6,128]{2,0,1:T(8,128)S(1)}, u32[]{:S(2)}, u32[]{:S(2)}) %collective-permute-start.1) | collective-permute-done | bytes 445472 | tf_op jit(solution)/shard_map/ppermute | solution.py:29
  17.4 2.2 %collective-permute-done = f32[145,6,128]{2,0,1:T(8,128)} collective-permute-done((f32[145,6,128]{2,0,1:T(8,128)}, f32[145,6,128]{2,0,1:T(8,128)}, u32[]{:S(2)}, u32[]{:S(2)}) %collective-permute-start) | collective-permute-done | bytes 445472 | tf_op jit(solution)/shard_map/ppermute | solution.py:26
  21.3 2.8 %fusion.18 = f32[144,41,128]{2,1,0:T(8,128)S(1)} fusion(f32[145,44,128]{2,1,0:T(8,128)S(1)} %pad_maximum_fusion, f32[144]{0:T(256)S(1)} %get-tuple-element.32, f32[144]{0:T(256)S(1)} %get-tuple-element.33, f32[144]{0:T(256)S(1)} %get-tuple-element.27, pred[144]{0:T(512)(128)(4,1)S(1)} %get-tuple-element.26), kind=kLoop, calls=%fused_computation.34 | loop fusion | flops 11335680 | bytes 15116112 | tf_op jit(solution)/shard_map/mul | solution.py:58
  25.2 5.4 %fusion.4 = f32[144,40,129]{2,1,0:T(8,128)S(1)} fusion(f32[144,40,128]{2,1,0:T(8,128)S(1)} %fusion.29, f32[144]{0:T(256)S(1)} %get-tuple-element.25, f32[144]{0:T(256)S(1)} %get-tuple-element.24, f32[144]{0:T(256)S(1)} %get-tuple-element.17, pred[144]{0:T(512)(128)(4,1)S(1)} %get-tuple-element.16), kind=kLoop, calls=%fused_computation.18 | loop fusion | flops 11145600 | bytes 5923152 | tf_op jit(solution)/shard_map/mul | solution.py:58
  31.5 2.6 %fusion.26 = f32[144,37,128]{2,1,0:T(8,128)S(1)} fusion(f32[144,40,128]{2,1,0:T(8,128)S(1)} %fusion.28, f32[144]{0:T(256)S(1)} %get-tuple-element.32, f32[144]{0:T(256)S(1)} %get-tuple-element.33, f32[144]{0:T(256)S(1)} %get-tuple-element.27, pred[144]{0:T(512)(128)(4,1)S(1)} %get-tuple-element.26), kind=kLoop, calls=%fused_computation.46 | loop fusion | flops 10229760 | bytes 13641552 | tf_op jit(solution)/shard_map/mul | solution.py:58
  35.0 5.4 %fusion.11 = f32[144,36,129]{2,1,0:T(8,128)S(1)} fusion(f32[144,36,128]{2,1,0:T(8,128)S(1)} %fusion.21, f32[144]{0:T(256)S(1)} %get-tuple-element.25, f32[144]{0:T(256)S(1)} %get-tuple-element.24, f32[144]{0:T(256)S(1)} %get-tuple-element.17, pred[144]{0:T(512)(128)(4,1)S(1)} %get-tuple-element.16), kind=kLoop, calls=%fused_computation.25 | loop fusion | flops 10031040 | bytes 5331024 | tf_op jit(solution)/shard_map/mul | solution.py:58
  41.6 3.9 %fusion.36 = f32[144,32,128]{2,1,0:T(8,128)S(1)} fusion(f32[144,32,128]{2,1,0:T(8,128)S(1)} %slice.210, f32[144,36,128]{2,1,0:T(8,128)S(1)} %fusion.20, f32[32,128]{1,0:T(8,128)S(1)} %copy-done.3, f32[144]{0:T(256)S(1)} %get-tuple-element.23, f32[144]{0:T(256)S(1)} %get-tuple-element.22), kind=kLoop, calls=%fused_computation.59 | loop fusion | flops 11796480 | bytes 14173312 | tf_op jit(solution)/shard_map/mul | solution.py:164
  45.6 3.3 %copy.55 = f32[144,32,128]{0,2,1:T(8,128)} copy(f32[144,32,128]{2,1,0:T(8,128)S(1)} %fusion.36) | data formatting | bytes 4718592 | tf_op jit(solution)/shard_map/mul | solution.py:164
  48.8 12.0 %gather_fusion = f32[3072,144]{1,0:T(8,128)S(1)} fusion(f32[144,4096]{0,1:T(8,128)} %bitcast.27, s32[3072]{0:T(1024)S(1)} %broadcast_clamp_fusion), kind=kCustom, calls=%fused_computation | custom fusion | bytes 3551232 | tf_op jit(solution)/shard_map/jit(_take)/gather | solution.py:169
  60.8 2.0 copy.56
  62.9 2.8 %broadcast_select_fusion = f32[144,8,384]{2,0,1:T(8,128)} fusion(f32[144,8,384]{2,0,1:T(8,128)} %copy.56, pred[8,384]{1,0:T(8,128)(4,1)S(1)} %compare_and_fusion), kind=kLoop, calls=%fused_computation.73 | loop fusion | flops 442368 | bytes 3542016 | tf_op jit(solution)/shard_map/jit(_take)/select_n | solution.py:169
  65.7 5.7 %all-to-all-start = ((f32[144,8,384]{2,0,1:T(8,128)}), f32[144,8,384]{2,0,1:T(8,128)S(1)}, u32[]{:S(2)}, u32[]{:S(2)}) async-start(f32[144,8,384]{2,0,1:T(8,128)} %broadcast_select_fusion), calls=%async_computation | async-start | bytes 3538944 | tf_op jit(solution)/shard_map/all_to_all | solution.py:170
  74.1 39.3 %all-to-all-done = f32[144,8,384]{2,0,1:T(8,128)S(1)} async-done(((f32[144,8,384]{2,0,1:T(8,128)}), f32[144,8,384]{2,0,1:T(8,128)S(1)}, u32[]{:S(2)}, u32[]{:S(2)}) %all-to-all-start) | async-done | bytes 1769504 | tf_op jit(solution)/shard_map/all_to_all | solution.py:170
  114.6 1.5 reshape.180
  116.2 1.5 copy.66
  117.7 7.3 %shard_map.86 = f32[36,32,384]{2,1,0:T(8,128)} custom-call(s32[4]{0:T(128)} %off_ref.1, f32[32,1]{1,0:T(8,128)} %copy.58.w_ref, f32[36,32,384]{2,1,0:T(8,128)} %bitcast.34), custom_call_target="tpu_custom_call" | custom-call | tf_op jit(solution)/shard_map/pallas_call | solution.py:116
  125.0 3.8 %copy.59 = f32[32,36,384]{2,1,0:T(8,128)} copy(f32[32,36,384]{2,0,1:T(8,128)} %bitcast.30) | data formatting | bytes 3538944 | tf_op jit(solution)/shard_map/transpose | solution.py:127
  128.8 2.7 %all_to_all.26 = f32[8,144,384]{2,1,0:T(8,128)} reshape(f32[32,36,384]{2,1,0:T(8,128)} %copy.59) | data formatting | bytes 3538944 | tf_op jit(solution)/shard_map/all_to_all | solution.py:172
  131.4 3.6 %all-to-all-start.1 = ((f32[8,144,384]{2,1,0:T(8,128)}), f32[8,144,384]{2,1,0:T(8,128)S(1)}, u32[]{:S(2)}, u32[]{:S(2)}) async-start(f32[8,144,384]{2,1,0:T(8,128)} %all_to_all.26), calls=%async_computation.1 | async-start | bytes 3538944 | tf_op jit(solution)/shard_map/all_to_all | solution.py:172
  136.5 40.4 %all-to-all-done.1 = f32[8,144,384]{2,1,0:T(8,128)S(1)} async-done(((f32[8,144,384]{2,1,0:T(8,128)}), f32[8,144,384]{2,1,0:T(8,128)S(1)}, u32[]{:S(2)}, u32[]{:S(2)}) %all-to-all-start.1) | async-done | bytes 1769504 | tf_op jit(solution)/shard_map/all_to_all | solution.py:172
  178.4 2.1 %copy.61 = f32[3072,144]{1,0:T(8,128)S(1)} copy(f32[3072,144]{0,1:T(8,128)} %bitcast.35) | data formatting | bytes 3538944 | tf_op jit(solution)/shard_map/all_to_all | solution.py:172
  180.5 21.1 %scatter_fusion = f32[144,4096]{0,1:T(8,128)} fusion(f32[144,4096]{0,1:T(8,128)} %bitcast.28, s32[3072]{0:T(1024)S(1)} %bitcast.41, f32[3072,144]{1,0:T(8,128)S(1)} %copy.61), kind=kCustom, calls=%fused_computation.1 | custom fusion | flops 442368 | bytes 5320704 | tf_op jit(solution)/shard_map/scatter-add | solution.py:173
  201.6 4.8 %copy.63 = f32[144,32,128]{2,1,0:T(8,128)} copy(f32[144,32,128]{0,2,1:T(8,128)} %bitcast.29) | data formatting | bytes 4718592
  (49 shorter events, 16.5 us)
Async XLA Ops:
  0.6 9.5 %copy-start.7 = (f32[32]{0:T(128)S(1)}, f32[32]{0:T(128)}, u32[]{:S(2)}) copy-start(f32[32]{0:T(128)} %param.11) | copy-start | bytes 388
  0.6 9.5 %copy-start.8 = (f32[32]{0:T(128)S(1)}, f32[32]{0:T(128)}, u32[]{:S(2)}) copy-start(f32[32]{0:T(128)} %param.10) | copy-start | bytes 388
  0.7 9.6 %copy-start.4 = (s32[32,128]{1,0:T(8,128)S(1)}, s32[32,128]{1,0:T(8,128)}, u32[]{:S(2)}) copy-start(s32[32,128]{1,0:T(8,128)} %param.9) | copy-start | bytes 49156
  2.0 18.7 %copy-start = (f32[144,32,128]{2,1,0:T(8,128)S(1)}, f32[144,32,128]{2,1,0:T(8,128)}, u32[]{:S(2)}) copy-start(f32[144,32,128]{2,1,0:T(8,128)} %param.7) | copy-start | bytes 7077892
  2.0 18.7 %copy-start.3 = (f32[32,128]{1,0:T(8,128)S(1)}, f32[32,128]{1,0:T(8,128)}, u32[]{:S(2)}) copy-start(f32[32,128]{1,0:T(8,128)} %param.8) | copy-start | bytes 49156
  2.1 15.1 %collective-permute-start.1 = (f32[145,6,128]{2,0,1:T(8,128)S(1)}, f32[145,6,128]{2,0,1:T(8,128)S(1)}, u32[]{:S(2)}, u32[]{:S(2)}) collective-permute-start(f32[145,6,128]{2,0,1:T(8,128)S(1)} %copy.52), channel_id=1, source_target_pairs={{1,0},{3,2},{5,4},{7,6},{9,8},{11,10},{13,12},{15,14},{17,16},{19,... | collective-permute-start | bytes 1336328 | tf_op jit(solution)/shard_map/ppermute | solution.py:29
  4.4 15.2 %collective-permute-start = (f32[145,6,128]{2,0,1:T(8,128)}, f32[145,6,128]{2,0,1:T(8,128)}, u32[]{:S(2)}, u32[]{:S(2)}) collective-permute-start(f32[145,6,128]{2,0,1:T(8,128)} %copy.51), channel_id=1, source_target_pairs={{0,1},{2,3},{4,5},{6,7},{8,9},{10,11},{12,13},{14,15},{16,17},{18,... | collective-permute-start | bytes 1336328 | tf_op jit(solution)/shard_map/ppermute | solution.py:26
  62.9 8.5 %copy-start.5 = (s32[4]{0:T(128)S(1)}, s32[4]{0:T(128)}, u32[]{:S(2)}) copy-start(s32[4]{0:T(128)} %off_ref.1) | copy-start | bytes 52
  62.9 9.2 %copy-start.6 = (f32[32]{0:T(128)S(1)}, f32[32]{0:T(128)}, u32[]{:S(2)}) copy-start(f32[32]{0:T(128)} %param.12) | copy-start | bytes 388
  65.7 47.7 %all-to-all-start = ((f32[144,8,384]{2,0,1:T(8,128)}), f32[144,8,384]{2,0,1:T(8,128)S(1)}, u32[]{:S(2)}, u32[]{:S(2)}) async-start(f32[144,8,384]{2,0,1:T(8,128)} %broadcast_select_fusion), calls=%async_computation | async-start | bytes 3538944 | tf_op jit(solution)/shard_map/all_to_all | solution.py:170
  113.4 1.2 copy-start.2
  128.8 6.3 %copy-start.1 = (f32[36,32,384]{2,1,0:T(8,128)S(1)}, f32[36,32,384]{2,1,0:T(8,128)}, u32[]{:S(2)}) copy-start(f32[36,32,384]{2,1,0:T(8,128)} %shard_map.86) | copy-start | bytes 5308420
  131.4 45.5 %all-to-all-start.1 = ((f32[8,144,384]{2,1,0:T(8,128)}), f32[8,144,384]{2,1,0:T(8,128)S(1)}, u32[]{:S(2)}, u32[]{:S(2)}) async-start(f32[8,144,384]{2,1,0:T(8,128)} %all_to_all.26), calls=%async_computation.1 | async-start | bytes 3538944 | tf_op jit(solution)/shard_map/all_to_all | solution.py:172

commit v3 on v2

--- a/solution.py
+++ b/solution.py
@@ -166,11 +166,13 @@
     ) * transparency
     flat_cells = smoothed.reshape(local_comps, -1)
     sea_cells = sea_order.reshape(-1)[:SEA_MAX]
-    columns = jnp.take(flat_cells, sea_cells, axis=1)
+    columns = flat_cells.at[:, sea_cells].get(mode="promise_in_bounds", unique_indices=True)
     gathered = lax.all_to_all(columns, "spec", split_axis=1, concat_axis=0, tiled=True)
     source_terms = interact_pallas(gathered, coupling, quad_offsets)
     returned = lax.all_to_all(source_terms, "spec", split_axis=0, concat_axis=1, tiled=True)
-    new_cells = flat_cells.at[:, sea_cells].add(returned)
+    new_cells = flat_cells.at[:, sea_cells].add(
+        returned, mode="promise_in_bounds", unique_indices=True
+    )
     updated = new_cells.reshape(smoothed.shape)
     return (updated, source_terms.astype(jnp.bfloat16)[None])
 

time: 207 us -> 203 us (0.981)
  other arithmetic: 51.3 us -> 48.1 us
    select_n x2 -> x1, other arithmetic: 2.85 us -> 0.02 us  [on_device(): flat_cells.at[:, sea_cells]]
    gather x2 -> x1, local copies, waits for them, and re-layouts: 14 us -> 12 us  [on_device(): flat_cells.at[:, sea_cells]]
    unnamed x19 -> x15, local copies, waits for them, and re-layouts: 6.07 us -> 4.86 us
where the time goes in v3:
time: 203 us; the launch traced here: 202 us
  waiting for transfers between devices  89 us (44%)
  other arithmetic  48.1 us (24%)
  local copies, waits for them, and re-layouts  40.5 us (20%)
  starting transfers between devices  16.5 us (8%)
  Pallas kernels  7.27 us (4%)
    all_to_all x1, waiting for transfers between devices, on_device(): lax.all_to_all(source_terms, 'spec', split_axis=0, concat_axis=1, tiled=T...  40.4 us
    all_to_all x1, waiting for transfers between devices, on_device(): lax.all_to_all(columns, 'spec', split_axis=1, concat_axis=0, tiled=True)  39.5 us
    scatter-add x1, other arithmetic, on_device(): flat_cells.at[:, sea_cells]  21.1 us
    mul x4, other arithmetic, quickest(): face_flux = courant * face_value  16.2 us
    gather x1, local copies, waits for them, and re-layouts, on_device(): flat_cells.at[:, sea_cells]  12 us
    pallas_call x1, Pallas kernels, interact_pallas(): pl.pallas_call(interact_kernel, out_shape=jax.ShapeDtypeStruct((NDIR, NFR...  7.27 us
    ppermute x1, waiting for transfers between devices, extended_2(): lax.ppermute(lax.slice_in_dim(block, 0, width, axis=dim), axis, backward)  6.84 us
    all_to_all x3, local copies, waits for them, and re-layouts, on_device(): lax.all_to_all(source_terms, 'spec', split_axis=0, concat_axis=1, tiled=T...  6.21 us
  transfers between devices with their start and end apart: 4, of which 4 were waited for; matrix products, arithmetic and copies ran while one was open for 3% of the time, Pallas kernels for 0%

profile of v3, /device:TPU:0, one launch (start us, length us, event | category | flops | bytes accessed | tf_op | source)
XLA Modules:
  0.0 202.3 jit_solution(8548259314337500120)
XLA Ops:
  2.1 1.4 collective-permute-start.1
  4.4 5.7 %collective-permute-start = (f32[145,6,128]{2,0,1:T(8,128)}, f32[145,6,128]{2,0,1:T(8,128)}, u32[]{:S(2)}, u32[]{:S(2)}) collective-permute-start(f32[145,6,128]{2,0,1:T(8,128)} %copy.51), channel_id=1, source_target_pairs={{0,1},{2,3},{4,5},{6,7},{8,9},{10,11},{12,13},{14,15},{16,17},{18,... | collective-permute-start | bytes 1336328 | tf_op jit(solution)/shard_map/ppermute | solution.py:26
  10.4 6.8 %collective-permute-done.1 = f32[145,6,128]{2,0,1:T(8,128)S(1)} collective-permute-done((f32[145,6,128]{2,0,1:T(8,128)S(1)}, f32[145,6,128]{2,0,1:T(8,128)S(1)}, u32[]{:S(2)}, u32[]{:S(2)}) %collective-permute-start.1) | collective-permute-done | bytes 445472 | tf_op jit(solution)/shard_map/ppermute | solution.py:29
  17.4 2.2 %collective-permute-done = f32[145,6,128]{2,0,1:T(8,128)} collective-permute-done((f32[145,6,128]{2,0,1:T(8,128)}, f32[145,6,128]{2,0,1:T(8,128)}, u32[]{:S(2)}, u32[]{:S(2)}) %collective-permute-start) | collective-permute-done | bytes 445472 | tf_op jit(solution)/shard_map/ppermute | solution.py:26
  21.3 2.8 %fusion.18 = f32[144,41,128]{2,1,0:T(8,128)S(1)} fusion(f32[145,44,128]{2,1,0:T(8,128)S(1)} %pad_maximum_fusion, f32[144]{0:T(256)S(1)} %get-tuple-element.32, f32[144]{0:T(256)S(1)} %get-tuple-element.33, f32[144]{0:T(256)S(1)} %get-tuple-element.27, pred[144]{0:T(512)(128)(4,1)S(1)} %get-tuple-element.26), kind=kLoop, calls=%fused_computation.34 | loop fusion | flops 11335680 | bytes 15116112 | tf_op jit(solution)/shard_map/mul | solution.py:58
  25.0 5.3 %fusion.4 = f32[144,40,129]{2,1,0:T(8,128)S(1)} fusion(f32[144,40,128]{2,1,0:T(8,128)S(1)} %fusion.29, f32[144]{0:T(256)S(1)} %get-tuple-element.25, f32[144]{0:T(256)S(1)} %get-tuple-element.24, f32[144]{0:T(256)S(1)} %get-tuple-element.17, pred[144]{0:T(512)(128)(4,1)S(1)} %get-tuple-element.16), kind=kLoop, calls=%fused_computation.18 | loop fusion | flops 11145600 | bytes 5923152 | tf_op jit(solution)/shard_map/mul | solution.py:58
  31.2 2.6 %fusion.26 = f32[144,37,128]{2,1,0:T(8,128)S(1)} fusion(f32[144,40,128]{2,1,0:T(8,128)S(1)} %fusion.28, f32[144]{0:T(256)S(1)} %get-tuple-element.32, f32[144]{0:T(256)S(1)} %get-tuple-element.33, f32[144]{0:T(256)S(1)} %get-tuple-element.27, pred[144]{0:T(512)(128)(4,1)S(1)} %get-tuple-element.26), kind=kLoop, calls=%fused_computation.46 | loop fusion | flops 10229760 | bytes 13641552 | tf_op jit(solution)/shard_map/mul | solution.py:58
  34.7 5.4 %fusion.11 = f32[144,36,129]{2,1,0:T(8,128)S(1)} fusion(f32[144,36,128]{2,1,0:T(8,128)S(1)} %fusion.21, f32[144]{0:T(256)S(1)} %get-tuple-element.25, f32[144]{0:T(256)S(1)} %get-tuple-element.24, f32[144]{0:T(256)S(1)} %get-tuple-element.17, pred[144]{0:T(512)(128)(4,1)S(1)} %get-tuple-element.16), kind=kLoop, calls=%fused_computation.25 | loop fusion | flops 10031040 | bytes 5331024 | tf_op jit(solution)/shard_map/mul | solution.py:58
  41.3 3.9 %fusion.36 = f32[144,32,128]{2,1,0:T(8,128)S(1)} fusion(f32[144,32,128]{2,1,0:T(8,128)S(1)} %slice.207, f32[144,36,128]{2,1,0:T(8,128)S(1)} %fusion.20, f32[32,128]{1,0:T(8,128)S(1)} %copy-done.2, f32[144]{0:T(256)S(1)} %get-tuple-element.23, f32[144]{0:T(256)S(1)} %get-tuple-element.22), kind=kLoop, calls=%fused_computation.59 | loop fusion | flops 11796480 | bytes 14173312 | tf_op jit(solution)/shard_map/mul | solution.py:164
  45.2 3.3 %copy.55 = f32[144,32,128]{0,2,1:T(8,128)} copy(f32[144,32,128]{2,1,0:T(8,128)S(1)} %fusion.36) | data formatting | bytes 4718592 | tf_op jit(solution)/shard_map/mul | solution.py:164
  48.5 12.0 %gather_fusion = f32[3072,144]{1,0:T(8,128)S(1)} fusion(f32[144,4096]{0,1:T(8,128)} %bitcast.27, s32[3072]{0:T(1024)S(1)} %broadcast_clamp_fusion), kind=kCustom, calls=%fused_computation | custom fusion | bytes 3551232 | tf_op jit(solution)/shard_map/gather | solution.py:169
  60.5 2.0 %copy.56 = f32[144,8,384]{2,0,1:T(8,128)} copy(f32[144,8,384]{0,2,1:T(8,128)S(1)} %bitcast.31) | data formatting | bytes 3538944 | tf_op jit(solution)/shard_map/all_to_all | solution.py:170
  62.5 5.8 %all-to-all-start = ((f32[144,8,384]{2,0,1:T(8,128)}), f32[144,8,384]{2,0,1:T(8,128)}, u32[]{:S(2)}, u32[]{:S(2)}) async-start(f32[144,8,384]{2,0,1:T(8,128)} %copy.56), calls=%async_computation | async-start | bytes 3538944 | tf_op jit(solution)/shard_map/all_to_all | solution.py:170
  70.9 39.5 %all-to-all-done = f32[144,8,384]{2,0,1:T(8,128)} async-done(((f32[144,8,384]{2,0,1:T(8,128)}), f32[144,8,384]{2,0,1:T(8,128)}, u32[]{:S(2)}, u32[]{:S(2)}) %all-to-all-start) | async-done | bytes 1769504 | tf_op jit(solution)/shard_map/all_to_all | solution.py:170
  110.5 1.5 reshape.168
  112.0 1.5 copy.66
  113.5 7.3 %shard_map.86 = f32[36,32,384]{2,1,0:T(8,128)} custom-call(s32[4]{0:T(128)} %off_ref.1, f32[32,1]{1,0:T(8,128)} %copy.58.w_ref, f32[36,32,384]{2,1,0:T(8,128)} %bitcast.33), custom_call_target="tpu_custom_call" | custom-call | tf_op jit(solution)/shard_map/pallas_call | solution.py:116
  120.8 3.8 %copy.59 = f32[32,36,384]{2,1,0:T(8,128)} copy(f32[32,36,384]{2,0,1:T(8,128)} %bitcast.30) | data formatting | bytes 3538944 | tf_op jit(solution)/shard_map/transpose | solution.py:127
  124.6 2.7 %all_to_all.29 = f32[8,144,384]{2,1,0:T(8,128)} reshape(f32[32,36,384]{2,1,0:T(8,128)} %copy.59) | data formatting | bytes 3538944 | tf_op jit(solution)/shard_map/all_to_all | solution.py:172
  127.3 3.6 %all-to-all-start.1 = ((f32[8,144,384]{2,1,0:T(8,128)}), f32[8,144,384]{2,1,0:T(8,128)S(1)}, u32[]{:S(2)}, u32[]{:S(2)}) async-start(f32[8,144,384]{2,1,0:T(8,128)} %all_to_all.29), calls=%async_computation.1 | async-start | bytes 3538944 | tf_op jit(solution)/shard_map/all_to_all | solution.py:172
  132.4 40.4 %all-to-all-done.1 = f32[8,144,384]{2,1,0:T(8,128)S(1)} async-done(((f32[8,144,384]{2,1,0:T(8,128)}), f32[8,144,384]{2,1,0:T(8,128)S(1)}, u32[]{:S(2)}, u32[]{:S(2)}) %all-to-all-start.1) | async-done | bytes 1769504 | tf_op jit(solution)/shard_map/all_to_all | solution.py:172
  174.2 2.1 %copy.61 = f32[3072,144]{1,0:T(8,128)S(1)} copy(f32[3072,144]{0,1:T(8,128)} %bitcast.34) | data formatting | bytes 3538944 | tf_op jit(solution)/shard_map/all_to_all | solution.py:172
  176.4 21.1 %scatter_fusion = f32[144,4096]{0,1:T(8,128)} fusion(f32[144,4096]{0,1:T(8,128)} %bitcast.28, s32[3072]{0:T(1024)S(1)} %bitcast.40, f32[3072,144]{1,0:T(8,128)S(1)} %copy.61), kind=kCustom, calls=%fused_computation.1 | custom fusion | flops 442368 | bytes 5320704 | tf_op jit(solution)/shard_map/scatter-add | solution.py:173
  197.5 4.8 %copy.63 = f32[144,32,128]{2,1,0:T(8,128)} copy(f32[144,32,128]{0,2,1:T(8,128)} %bitcast.29) | data formatting | bytes 4718592
  (43 shorter events, 13.5 us)
Async XLA Ops:
  0.6 9.5 %copy-start.5 = (f32[32]{0:T(128)S(1)}, f32[32]{0:T(128)}, u32[]{:S(2)}) copy-start(f32[32]{0:T(128)} %param.11) | copy-start | bytes 388
  0.6 9.5 %copy-start.6 = (f32[32]{0:T(128)S(1)}, f32[32]{0:T(128)}, u32[]{:S(2)}) copy-start(f32[32]{0:T(128)} %param.10) | copy-start | bytes 388
  0.7 9.6 %slice-start = ((s32[32,128]{1,0:T(8,128)}), s32[24,128]{1,0:T(8,128)S(1)}, s32[]{:S(2)}) async-start(s32[32,128]{1,0:T(8,128)} %param.9), calls=%async_computation.2 | async-start | bytes 24576 | tf_op jit(solution)/shard_map/slice | solution.py:168
  2.0 18.7 %copy-start = (f32[144,32,128]{2,1,0:T(8,128)S(1)}, f32[144,32,128]{2,1,0:T(8,128)}, u32[]{:S(2)}) copy-start(f32[144,32,128]{2,1,0:T(8,128)} %param.7) | copy-start | bytes 7077892
  2.0 18.7 %copy-start.2 = (f32[32,128]{1,0:T(8,128)S(1)}, f32[32,128]{1,0:T(8,128)}, u32[]{:S(2)}) copy-start(f32[32,128]{1,0:T(8,128)} %param.8) | copy-start | bytes 49156
  2.1 15.1 %collective-permute-start.1 = (f32[145,6,128]{2,0,1:T(8,128)S(1)}, f32[145,6,128]{2,0,1:T(8,128)S(1)}, u32[]{:S(2)}, u32[]{:S(2)}) collective-permute-start(f32[145,6,128]{2,0,1:T(8,128)S(1)} %copy.52), channel_id=1, source_target_pairs={{1,0},{3,2},{5,4},{7,6},{9,8},{11,10},{13,12},{15,14},{17,16},{19,... | collective-permute-start | bytes 1336328 | tf_op jit(solution)/shard_map/ppermute | solution.py:29
  4.4 15.2 %collective-permute-start = (f32[145,6,128]{2,0,1:T(8,128)}, f32[145,6,128]{2,0,1:T(8,128)}, u32[]{:S(2)}, u32[]{:S(2)}) collective-permute-start(f32[145,6,128]{2,0,1:T(8,128)} %copy.51), channel_id=1, source_target_pairs={{0,1},{2,3},{4,5},{6,7},{8,9},{10,11},{12,13},{14,15},{16,17},{18,... | collective-permute-start | bytes 1336328 | tf_op jit(solution)/shard_map/ppermute | solution.py:26
  62.5 5.8 %copy-start.3 = (s32[4]{0:T(128)S(1)}, s32[4]{0:T(128)}, u32[]{:S(2)}) copy-start(s32[4]{0:T(128)} %off_ref.1) | copy-start | bytes 52
  62.5 6.4 %copy-start.4 = (f32[32]{0:T(128)S(1)}, f32[32]{0:T(128)}, u32[]{:S(2)}) copy-start(f32[32]{0:T(128)} %param.12) | copy-start | bytes 388
  62.5 47.9 %all-to-all-start = ((f32[144,8,384]{2,0,1:T(8,128)}), f32[144,8,384]{2,0,1:T(8,128)}, u32[]{:S(2)}, u32[]{:S(2)}) async-start(f32[144,8,384]{2,0,1:T(8,128)} %copy.56), calls=%async_computation | async-start | bytes 3538944 | tf_op jit(solution)/shard_map/all_to_all | solution.py:170
  124.6 6.3 %copy-start.1 = (f32[36,32,384]{2,1,0:T(8,128)S(1)}, f32[36,32,384]{2,1,0:T(8,128)}, u32[]{:S(2)}) copy-start(f32[36,32,384]{2,1,0:T(8,128)} %shard_map.86) | copy-start | bytes 5308420
  127.3 45.5 %all-to-all-start.1 = ((f32[8,144,384]{2,1,0:T(8,128)}), f32[8,144,384]{2,1,0:T(8,128)S(1)}, u32[]{:S(2)}, u32[]{:S(2)}) async-start(f32[8,144,384]{2,1,0:T(8,128)} %all_to_all.29), calls=%async_computation.1 | async-start | bytes 3538944 | tf_op jit(solution)/shard_map/all_to_all | solution.py:172

commit v4 on v2

--- a/solution.py
+++ b/solution.py
@@ -165,12 +165,34 @@
         centre + spread_y * laplace(with_rim, 1) + spread_x * laplace(pad_along(centre), 2)
     ) * transparency
     flat_cells = smoothed.reshape(local_comps, -1)
-    sea_cells = sea_order.reshape(-1)[:SEA_MAX]
-    columns = jnp.take(flat_cells, sea_cells, axis=1)
-    gathered = lax.all_to_all(columns, "spec", split_axis=1, concat_axis=0, tiled=True)
+    spec_size = lax.axis_size("spec")
+    me = lax.axis_index("spec")
+    per_dest = SEA_MAX // spec_size
+    cells = sea_order.reshape(-1)[:SEA_MAX].reshape(spec_size, per_dest)
+    pieces = []
+    for shift in range(spec_size):
+        dest = (me + shift) % spec_size
+        block_cells = lax.dynamic_index_in_dim(cells, dest, 0, keepdims=False)
+        block = flat_cells.at[:, block_cells].get(mode="promise_in_bounds", unique_indices=True)
+        if shift:
+            pairs = [(s, (s + shift) % spec_size) for s in range(spec_size)]
+            block = lax.ppermute(block, "spec", pairs)
+        pieces.append(block)
+    by_shift = jnp.stack(pieces[:1] + pieces[:0:-1])
+    gathered = jnp.roll(by_shift, me, axis=0).reshape(-1, per_dest)
     source_terms = interact_pallas(gathered, coupling, quad_offsets)
-    returned = lax.all_to_all(source_terms, "spec", split_axis=0, concat_axis=1, tiled=True)
-    new_cells = flat_cells.at[:, sea_cells].add(returned)
+    new_cells = flat_cells
+    for shift in range(spec_size):
+        dest = (me + shift) % spec_size
+        src = (me - shift) % spec_size
+        block = lax.dynamic_slice_in_dim(source_terms, dest * local_comps, local_comps, 0)
+        if shift:
+            pairs = [(s, (s + shift) % spec_size) for s in range(spec_size)]
+            block = lax.ppermute(block, "spec", pairs)
+        block_cells = lax.dynamic_index_in_dim(cells, src, 0, keepdims=False)
+        new_cells = new_cells.at[:, block_cells].add(
+            block, mode="promise_in_bounds", unique_indices=True
+        )
     updated = new_cells.reshape(smoothed.shape)
     return (updated, source_terms.astype(jnp.bfloat16)[None])
 

time: 207 us -> 244 us (1.18)
  the two profiles are of different devices: /device:TPU:0 before, /device:TPU:9 now
where the time goes in v4:
time: 244 us
  other arithmetic  80.4 us (33%)
  waiting for transfers between devices  71.6 us (29%)
  local copies, waits for them, and re-layouts  61.1 us (25%)
  starting transfers between devices  21.7 us (9%)
  Pallas kernels  7.26 us (3%)
    ppermute x14, waiting for transfers between devices, on_device(): block = lax.ppermute(block, 'spec', pairs)  64.1 us
    scatter-add x8, other arithmetic, on_device(): new_cells.at[:, block_cells]  51.9 us
    gather x8, local copies, waits for them, and re-layouts, on_device(): flat_cells.at[:, block_cells]  32.9 us
    ppermute x14, starting transfers between devices, on_device(): block = lax.ppermute(block, 'spec', pairs)  17.2 us
    mul x4, other arithmetic, quickest(): face_flux = courant * face_value  16.2 us
    pallas_call x1, Pallas kernels, interact_pallas(): pl.pallas_call(interact_kernel, out_shape=jax.ShapeDtypeStruct((NDIR, NFR...  7.26 us
    unnamed x46, local copies, waits for them, and re-layouts  5.31 us
    ppermute x1, waiting for transfers between devices, extended_2(): lax.ppermute(lax.slice_in_dim(block, 0, width, axis=dim), axis, backward)  4.9 us
  transfers between devices with their start and end apart: 16, of which 10 were waited for; matrix products, arithmetic and copies ran while one was open for 16% of the time, Pallas kernels for 0%

profile of v4, /device:TPU:9, one launch (start us, length us, event | category | flops | bytes accessed | tf_op | source)
XLA Modules:
  0.0 243.5 jit_solution(5920247861643013901)
XLA Ops:
  14.9 4.9 %collective-permute-done.1 = f32[145,6,128]{2,0,1:T(8,128)} collective-permute-done((f32[145,6,128]{2,0,1:T(8,128)}, f32[145,6,128]{2,0,1:T(8,128)}, u32[]{:S(2)}, u32[]{:S(2)}) %collective-permute-start.1) | collective-permute-done | bytes 445472 | tf_op jit(solution)/shard_map/ppermute | solution.py:29
  25.2 5.3 %fusion.4 = f32[144,40,129]{2,1,0:T(8,128)S(1)} fusion(f32[144,40,128]{2,1,0:T(8,128)S(1)} %fusion.29, f32[144]{0:T(256)S(1)} %get-tuple-element.46, f32[144]{0:T(256)S(1)} %get-tuple-element.45, f32[144]{0:T(256)S(1)} %get-tuple-element.30, pred[144]{0:T(512)(128)(4,1)S(1)} %get-tuple-element.29), kind=kLoop, calls=%fused_computation.32 | loop fusion | flops 11145600 | bytes 5923152 | tf_op jit(solution)/shard_map/mul | solution.py:58
  34.9 5.4 %fusion.11 = f32[144,36,129]{2,1,0:T(8,128)S(1)} fusion(f32[144,36,128]{2,1,0:T(8,128)S(1)} %fusion.21, f32[144]{0:T(256)S(1)} %get-tuple-element.46, f32[144]{0:T(256)S(1)} %get-tuple-element.45, f32[144]{0:T(256)S(1)} %get-tuple-element.30, pred[144]{0:T(512)(128)(4,1)S(1)} %get-tuple-element.29), kind=kLoop, calls=%fused_computation.39 | loop fusion | flops 10031040 | bytes 5331024 | tf_op jit(solution)/shard_map/mul | solution.py:58
  41.5 3.9 %fusion.36 = f32[144,32,128]{2,1,0:T(8,128)S(1)} fusion(f32[144,32,128]{2,1,0:T(8,128)S(1)} %slice.218, f32[144,36,128]{2,1,0:T(8,128)S(1)} %fusion.20, f32[32,128]{1,0:T(8,128)S(1)} %copy-done.2, f32[144]{0:T(256)S(1)} %get-tuple-element.44, f32[144]{0:T(256)S(1)} %get-tuple-element.43), kind=kLoop, calls=%fused_computation.73 | loop fusion | flops 11796480 | bytes 14173312 | tf_op jit(solution)/shard_map/mul | solution.py:164
  52.5 4.4 %gather_fusion.1 = f32[384,144]{1,0:T(8,128)} fusion(f32[144,4096]{0,1:T(8,128)} %bitcast.119, s32[1024]{0:T(1024)S(1)} %pad_clamp_fusion.6), kind=kCustom, calls=%fused_computation.1 | custom fusion | bytes 443904 | tf_op jit(solution)/shard_map/gather | solution.py:176
  58.7 4.4 %gather_fusion.2 = f32[384,144]{1,0:T(8,128)} fusion(f32[144,4096]{0,1:T(8,128)} %bitcast.120, s32[1024]{0:T(1024)S(1)} %get-tuple-element.60), kind=kCustom, calls=%fused_computation.2 | custom fusion | bytes 443904 | tf_op jit(solution)/shard_map/gather | solution.py:176
  74.6 4.4 %gather_fusion.5 = f32[384,144]{1,0:T(8,128)} fusion(f32[144,4096]{0,1:T(8,128)} %bitcast.123, s32[1024]{0:T(1024)S(1)} %get-tuple-element.57), kind=kCustom, calls=%fused_computation.5 | custom fusion | bytes 443904 | tf_op jit(solution)/shard_map/gather | solution.py:176
  80.7 4.4 %gather_fusion.6 = f32[384,144]{1,0:T(8,128)} fusion(f32[144,4096]{0,1:T(8,128)} %bitcast.124, s32[1024]{0:T(1024)S(1)} %get-tuple-element.56), kind=kCustom, calls=%fused_computation.6 | custom fusion | bytes 443904 | tf_op jit(solution)/shard_map/gather | solution.py:176
  91.6 13.5 %collective-permute-done.5 = f32[144,384]{0,1:T(8,128)S(1)} collective-permute-done((f32[144,384]{0,1:T(8,128)S(1)}, f32[144,384]{0,1:T(8,128)S(1)}, u32[]{:S(2)}, u32[]{:S(2)}) %collective-permute-start.5) | collective-permute-done | bytes 221216 | tf_op jit(solution)/shard_map/ppermute | solution.py:179
  105.1 8.5 %collective-permute-done.6 = f32[144,384]{0,1:T(8,128)S(1)} collective-permute-done((f32[144,384]{0,1:T(8,128)}, f32[144,384]{0,1:T(8,128)S(1)}, u32[]{:S(2)}, u32[]{:S(2)}) %collective-permute-start.6) | collective-permute-done | bytes 221216 | tf_op jit(solution)/shard_map/ppermute | solution.py:179
  113.6 8.4 %collective-permute-done.7 = f32[144,384]{0,1:T(8,128)S(1)} collective-permute-done((f32[144,384]{0,1:T(8,128)}, f32[144,384]{0,1:T(8,128)S(1)}, u32[]{:S(2)}, u32[]{:S(2)}) %collective-permute-start.7) | collective-permute-done | bytes 221216 | tf_op jit(solution)/shard_map/ppermute | solution.py:179
  122.1 8.3 %collective-permute-done.8 = f32[144,384]{0,1:T(8,128)S(1)} collective-permute-done((f32[144,384]{0,1:T(8,128)S(1)}, f32[144,384]{0,1:T(8,128)S(1)}, u32[]{:S(2)}, u32[]{:S(2)}) %collective-permute-start.8) | collective-permute-done | bytes 221216 | tf_op jit(solution)/shard_map/ppermute | solution.py:179
  136.1 7.3 %shard_map.86 = f32[36,32,384]{2,1,0:T(8,128)} custom-call(s32[4]{0:T(128)} %off_ref.1, f32[32,1]{1,0:T(8,128)} %copy.69.w_ref, f32[36,32,384]{2,1,0:T(8,128)} %bitcast.129), custom_call_target="tpu_custom_call" | custom-call | tf_op jit(solution)/shard_map/pallas_call | solution.py:116
  152.6 6.5 %scatter_fusion = f32[144,4096]{0,1:T(8,128)} fusion(f32[144,4096]{0,1:T(8,128)} %bitcast.126, s32[384]{0:T(512)S(1)} %get-tuple-element.26, f32[384,144]{1,0:T(8,128)S(1)} %copy.71), kind=kCustom, calls=%fused_computation.8 | custom fusion | flops 55296 | bytes 665088 | tf_op jit(solution)/shard_map/scatter-add | solution.py:193
  166.0 17.5 %collective-permute-done.11 = f32[144,384]{1,0:T(8,128)S(1)} collective-permute-done((f32[144,384]{1,0:T(8,128)}, f32[144,384]{1,0:T(8,128)S(1)}, u32[]{:S(2)}, u32[]{:S(2)}) %collective-permute-start.11) | collective-permute-done | bytes 221216 | tf_op jit(solution)/shard_map/ppermute | solution.py:191
  183.6 4.6 %collective-permute-done.12 = f32[144,384]{1,0:T(8,128)S(1)} collective-permute-done((f32[144,384]{1,0:T(8,128)}, f32[144,384]{1,0:T(8,128)S(1)}, u32[]{:S(2)}, u32[]{:S(2)}) %collective-permute-start.12) | collective-permute-done | bytes 221216 | tf_op jit(solution)/shard_map/ppermute | solution.py:191
  193.2 6.5 %scatter_fusion.1 = f32[144,4096]{0,1:T(8,128)} fusion(f32[144,4096]{0,1:T(8,128)} %scatter_fusion, s32[384]{0:T(512)S(1)} %copy-done.10, f32[384,144]{1,0:T(8,128)S(1)} %copy.72), kind=kCustom, calls=%fused_computation.9 | custom fusion | flops 55296 | bytes 665088 | tf_op jit(solution)/shard_map/scatter-add | solution.py:193
  199.7 6.5 %scatter_fusion.2 = f32[144,4096]{0,1:T(8,128)} fusion(f32[144,4096]{0,1:T(8,128)} %scatter_fusion.1, s32[384]{0:T(512)S(1)} %copy-done.9, f32[384,144]{1,0:T(8,128)S(1)} %copy.73), kind=kCustom, calls=%fused_computation.10 | custom fusion | flops 55296 | bytes 665088 | tf_op jit(solution)/shard_map/scatter-add | solution.py:193
  206.2 6.5 %scatter_fusion.3 = f32[144,4096]{0,1:T(8,128)} fusion(f32[144,4096]{0,1:T(8,128)} %scatter_fusion.2, s32[384]{0:T(512)S(1)} %copy-done.8, f32[384,144]{1,0:T(8,128)S(1)} %copy.74), kind=kCustom, calls=%fused_computation.11 | custom fusion | flops 55296 | bytes 665088 | tf_op jit(solution)/shard_map/scatter-add | solution.py:193
  212.7 6.5 %scatter_fusion.4 = f32[144,4096]{0,1:T(8,128)} fusion(f32[144,4096]{0,1:T(8,128)} %scatter_fusion.3, s32[384]{0:T(512)S(1)} %copy-done.7, f32[384,144]{1,0:T(8,128)S(1)} %copy.75), kind=kCustom, calls=%fused_computation.12 | custom fusion | flops 55296 | bytes 665088 | tf_op jit(solution)/shard_map/scatter-add | solution.py:193
  219.2 6.5 %scatter_fusion.5 = f32[144,4096]{0,1:T(8,128)} fusion(f32[144,4096]{0,1:T(8,128)} %scatter_fusion.4, s32[384]{0:T(512)S(1)} %copy-done.6, f32[384,144]{1,0:T(8,128)S(1)} %copy.76), kind=kCustom, calls=%fused_computation.13 | custom fusion | flops 55296 | bytes 665088 | tf_op jit(solution)/shard_map/scatter-add | solution.py:193
  225.7 6.5 %scatter_fusion.6 = f32[144,4096]{0,1:T(8,128)} fusion(f32[144,4096]{0,1:T(8,128)} %scatter_fusion.5, s32[384]{0:T(512)S(1)} %copy-done.5, f32[384,144]{1,0:T(8,128)S(1)} %copy.77), kind=kCustom, calls=%fused_computation.14 | custom fusion | flops 55296 | bytes 665088 | tf_op jit(solution)/shard_map/scatter-add | solution.py:193
  232.2 6.5 %scatter_fusion.7 = f32[144,4096]{0,1:T(8,128)} fusion(f32[144,4096]{0,1:T(8,128)} %scatter_fusion.6, s32[384]{0:T(512)S(1)} %copy-done.4, f32[384,144]{1,0:T(8,128)S(1)} %copy.78), kind=kCustom, calls=%fused_computation.15 | custom fusion | flops 55296 | bytes 665088 | tf_op jit(solution)/shard_map/scatter-add | solution.py:193
  238.7 4.8 %copy.80 = f32[144,32,128]{2,1,0:T(8,128)} copy(f32[144,32,128]{0,2,1:T(8,128)} %bitcast.127) | data formatting | bytes 4718592
  (126 shorter events, 80.2 us)
Async XLA Ops:
  0.7 20.3 %copy-start = (f32[144,32,128]{2,1,0:T(8,128)S(1)}, f32[144,32,128]{2,1,0:T(8,128)}, u32[]{:S(2)}) copy-start(f32[144,32,128]{2,1,0:T(8,128)} %param.7) | copy-start | bytes 7077892
  0.7 20.3 %copy-start.2 = (f32[32,128]{1,0:T(8,128)S(1)}, f32[32,128]{1,0:T(8,128)}, u32[]{:S(2)}) copy-start(f32[32,128]{1,0:T(8,128)} %param.8) | copy-start | bytes 49156
  2.3 12.5 %collective-permute-start = (f32[145,6,128]{2,0,1:T(8,128)S(1)}, f32[145,6,128]{2,0,1:T(8,128)S(1)}, u32[]{:S(2)}, u32[]{:S(2)}) collective-permute-start(f32[145,6,128]{2,0,1:T(8,128)S(1)} %copy.62), channel_id=1, source_target_pairs={{0,1},{2,3},{4,5},{6,7},{8,9},{10,11},{12,13},{14,15},{16,17},{18,... | collective-permute-start | bytes 1336328 | tf_op jit(solution)/shard_map/ppermute | solution.py:26
  6.3 13.5 %collective-permute-start.1 = (f32[145,6,128]{2,0,1:T(8,128)}, f32[145,6,128]{2,0,1:T(8,128)}, u32[]{:S(2)}, u32[]{:S(2)}) collective-permute-start(f32[145,6,128]{2,0,1:T(8,128)} %copy.63), channel_id=1, source_target_pairs={{1,0},{3,2},{5,4},{7,6},{9,8},{11,10},{13,12},{15,14},{17,16},{19,... | collective-permute-start | bytes 1336328 | tf_op jit(solution)/shard_map/ppermute | solution.py:29
  48.7 22.0 %copy-start.3 = (s32[1024]{0:T(1024)S(1)}, s32[1024]{0:T(1024)}, u32[]{:S(2)}) copy-start(s32[1024]{0:T(1024)} %get-tuple-element.58) | copy-start | bytes 12292
  56.9 32.1 %collective-permute-start.2 = (f32[144,384]{0,1:T(8,128)}, f32[144,384]{0,1:T(8,128)S(1)}, u32[]{:S(2)}, u32[]{:S(2)}) collective-permute-start(f32[144,384]{0,1:T(8,128)} %bitcast.11), channel_id=1, source_target_pairs={{0,14},{2,0},{4,2},{6,4},{8,6},{10,8},{12,10},{14,12},{1,15},{3,1}... | collective-permute-start | bytes 663560 | tf_op jit(solution)/shard_map/ppermute | solution.py:179
  63.1 28.2 %collective-permute-start.3 = (f32[144,384]{0,1:T(8,128)}, f32[144,384]{0,1:T(8,128)S(1)}, u32[]{:S(2)}, u32[]{:S(2)}) collective-permute-start(f32[144,384]{0,1:T(8,128)} %bitcast.14), channel_id=1, source_target_pairs={{0,12},{2,14},{4,0},{6,2},{8,4},{10,6},{12,8},{14,10},{1,13},{3,15... | collective-permute-start | bytes 663560 | tf_op jit(solution)/shard_map/ppermute | solution.py:179
  67.1 24.4 %collective-permute-start.4 = (f32[144,384]{0,1:T(8,128)S(1)}, f32[144,384]{0,1:T(8,128)S(1)}, u32[]{:S(2)}, u32[]{:S(2)}) collective-permute-start(f32[144,384]{0,1:T(8,128)S(1)} %bitcast.141), channel_id=1, source_target_pairs={{0,10},{2,12},{4,14},{6,0},{8,2},{10,4},{12,6},{14,8},{1,11},{3,13... | collective-permute-start | bytes 663560 | tf_op jit(solution)/shard_map/ppermute | solution.py:179
  74.5 30.6 %collective-permute-start.5 = (f32[144,384]{0,1:T(8,128)S(1)}, f32[144,384]{0,1:T(8,128)S(1)}, u32[]{:S(2)}, u32[]{:S(2)}) collective-permute-start(f32[144,384]{0,1:T(8,128)S(1)} %bitcast.142), channel_id=1, source_target_pairs={{0,8},{2,10},{4,12},{6,14},{8,0},{10,2},{12,4},{14,6},{1,9},{3,11}... | collective-permute-start | bytes 663560 | tf_op jit(solution)/shard_map/ppermute | solution.py:179
  79.0 34.6 %collective-permute-start.6 = (f32[144,384]{0,1:T(8,128)}, f32[144,384]{0,1:T(8,128)S(1)}, u32[]{:S(2)}, u32[]{:S(2)}) collective-permute-start(f32[144,384]{0,1:T(8,128)} %bitcast.23), channel_id=1, source_target_pairs={{0,6},{2,8},{4,10},{6,12},{8,14},{10,0},{12,2},{14,4},{1,7},{3,9},... | collective-permute-start | bytes 663560 | tf_op jit(solution)/shard_map/ppermute | solution.py:179
  89.0 33.1 %collective-permute-start.7 = (f32[144,384]{0,1:T(8,128)}, f32[144,384]{0,1:T(8,128)S(1)}, u32[]{:S(2)}, u32[]{:S(2)}) collective-permute-start(f32[144,384]{0,1:T(8,128)} %bitcast.143), channel_id=1, source_target_pairs={{0,4},{2,6},{4,8},{6,10},{8,12},{10,14},{12,0},{14,2},{1,5},{3,7},... | collective-permute-start | bytes 663560 | tf_op jit(solution)/shard_map/ppermute | solution.py:179
  91.3 39.1 %collective-permute-start.8 = (f32[144,384]{0,1:T(8,128)S(1)}, f32[144,384]{0,1:T(8,128)S(1)}, u32[]{:S(2)}, u32[]{:S(2)}) collective-permute-start(f32[144,384]{0,1:T(8,128)S(1)} %bitcast.140), channel_id=1, source_target_pairs={{0,2},{2,4},{4,6},{6,8},{8,10},{10,12},{12,14},{14,0},{1,3},{3,5},... | collective-permute-start | bytes 663560 | tf_op jit(solution)/shard_map/ppermute | solution.py:179
  147.3 16.8 %copy-start.1 = (f32[36,32,384]{2,1,0:T(8,128)S(1)}, f32[36,32,384]{2,1,0:T(8,128)}, u32[]{:S(2)}) copy-start(f32[36,32,384]{2,1,0:T(8,128)} %shard_map.86) | copy-start | bytes 5308420
  150.0 12.5 %collective-permute-start.9 = (f32[144,384]{1,0:T(8,128)S(1)}, f32[144,384]{1,0:T(8,128)S(1)}, u32[]{:S(2)}, u32[]{:S(2)}) collective-permute-start(f32[144,384]{1,0:T(8,128)S(1)} %get-tuple-element.41), channel_id=1, source_target_pairs={{0,2},{2,4},{4,6},{6,8},{8,10},{10,12},{12,14},{14,0},{1,3},{3,5},... | collective-permute-start | bytes 663560 | tf_op jit(solution)/shard_map/ppermute | solution.py:191
  152.4 11.7 %collective-permute-start.10 = (f32[144,384]{1,0:T(8,128)}, f32[144,384]{1,0:T(8,128)S(1)}, u32[]{:S(2)}, u32[]{:S(2)}) collective-permute-start(f32[144,384]{1,0:T(8,128)} %get-tuple-element.40), channel_id=1, source_target_pairs={{0,4},{2,6},{4,8},{6,10},{8,12},{10,14},{12,0},{14,2},{1,5},{3,7},... | collective-permute-start | bytes 663560 | tf_op jit(solution)/shard_map/ppermute | solution.py:191
  159.1 24.4 %collective-permute-start.11 = (f32[144,384]{1,0:T(8,128)}, f32[144,384]{1,0:T(8,128)S(1)}, u32[]{:S(2)}, u32[]{:S(2)}) collective-permute-start(f32[144,384]{1,0:T(8,128)} %get-tuple-element.39), channel_id=1, source_target_pairs={{0,6},{2,8},{4,10},{6,12},{8,14},{10,0},{12,2},{14,4},{1,7},{3,9},... | collective-permute-start | bytes 663560 | tf_op jit(solution)/shard_map/ppermute | solution.py:191
  159.5 28.7 %collective-permute-start.12 = (f32[144,384]{1,0:T(8,128)}, f32[144,384]{1,0:T(8,128)S(1)}, u32[]{:S(2)}, u32[]{:S(2)}) collective-permute-start(f32[144,384]{1,0:T(8,128)} %get-tuple-element.38), channel_id=1, source_target_pairs={{0,8},{2,10},{4,12},{6,14},{8,0},{10,2},{12,4},{14,6},{1,9},{3,11}... | collective-permute-start | bytes 663560 | tf_op jit(solution)/shard_map/ppermute | solution.py:191
  161.7 26.6 %collective-permute-start.13 = (f32[144,384]{1,0:T(8,128)}, f32[144,384]{1,0:T(8,128)S(1)}, u32[]{:S(2)}, u32[]{:S(2)}) collective-permute-start(f32[144,384]{1,0:T(8,128)} %get-tuple-element.37), channel_id=1, source_target_pairs={{0,10},{2,12},{4,14},{6,0},{8,2},{10,4},{12,6},{14,8},{1,11},{3,13... | collective-permute-start | bytes 663560 | tf_op jit(solution)/shard_map/ppermute | solution.py:191
  162.5 27.7 %collective-permute-start.14 = (f32[144,384]{1,0:T(8,128)}, f32[144,384]{1,0:T(8,128)S(1)}, u32[]{:S(2)}, u32[]{:S(2)}) collective-permute-start(f32[144,384]{1,0:T(8,128)} %get-tuple-element.36), channel_id=1, source_target_pairs={{0,12},{2,14},{4,0},{6,2},{8,4},{10,6},{12,8},{14,10},{1,13},{3,15... | collective-permute-start | bytes 663560 | tf_op jit(solution)/shard_map/ppermute | solution.py:191
  164.1 28.0 %collective-permute-start.15 = (f32[144,384]{1,0:T(8,128)}, f32[144,384]{1,0:T(8,128)}, u32[]{:S(2)}, u32[]{:S(2)}) collective-permute-start(f32[144,384]{1,0:T(8,128)} %get-tuple-element.35), channel_id=1, source_target_pairs={{0,14},{2,0},{4,2},{6,4},{8,6},{10,8},{12,10},{14,12},{1,15},{3,1}... | collective-permute-start | bytes 663560 | tf_op jit(solution)/shard_map/ppermute | solution.py:191
  164.2 29.0 %copy-start.10 = (s32[384]{0:T(512)S(1)}, s32[384]{0:T(512)}, u32[]{:S(2)}) copy-start(s32[384]{0:T(512)} %get-tuple-element.18) | copy-start | bytes 4612
  165.9 33.8 %copy-start.9 = (s32[384]{0:T(512)S(1)}, s32[384]{0:T(512)}, u32[]{:S(2)}) copy-start(s32[384]{0:T(512)} %get-tuple-element.17) | copy-start | bytes 4612
  193.2 13.0 %copy-start.8 = (s32[384]{0:T(512)S(1)}, s32[384]{0:T(512)}, u32[]{:S(2)}) copy-start(s32[384]{0:T(512)} %get-tuple-element.16) | copy-start | bytes 4612
  212.7 13.0 %copy-start.5 = (s32[384]{0:T(512)S(1)}, s32[384]{0:T(512)}, u32[]{:S(2)}) copy-start(s32[384]{0:T(512)} %get-tuple-element.13) | copy-start | bytes 4612
  (8 other events, 78.0 us)

commit v5 on v4

--- a/solution.py
+++ b/solution.py
@@ -169,11 +169,11 @@
     me = lax.axis_index("spec")
     per_dest = SEA_MAX // spec_size
     cells = sea_order.reshape(-1)[:SEA_MAX].reshape(spec_size, per_dest)
+    send_cells = jnp.roll(cells, -me, axis=0).reshape(-1)
+    columns = flat_cells.at[:, send_cells].get(mode="promise_in_bounds", unique_indices=True)
     pieces = []
     for shift in range(spec_size):
-        dest = (me + shift) % spec_size
-        block_cells = lax.dynamic_index_in_dim(cells, dest, 0, keepdims=False)
-        block = flat_cells.at[:, block_cells].get(mode="promise_in_bounds", unique_indices=True)
+        block = lax.slice_in_dim(columns, shift * per_dest, (shift + 1) * per_dest, axis=1)
         if shift:
             pairs = [(s, (s + shift) % spec_size) for s in range(spec_size)]
             block = lax.ppermute(block, "spec", pairs)
@@ -181,18 +181,18 @@
     by_shift = jnp.stack(pieces[:1] + pieces[:0:-1])
     gathered = jnp.roll(by_shift, me, axis=0).reshape(-1, per_dest)
     source_terms = interact_pallas(gathered, coupling, quad_offsets)
-    new_cells = flat_cells
+    by_dest = jnp.roll(source_terms.reshape(spec_size, local_comps, per_dest), -me, axis=0)
+    returned = []
     for shift in range(spec_size):
-        dest = (me + shift) % spec_size
-        src = (me - shift) % spec_size
-        block = lax.dynamic_slice_in_dim(source_terms, dest * local_comps, local_comps, 0)
+        block = by_dest[shift]
         if shift:
             pairs = [(s, (s + shift) % spec_size) for s in range(spec_size)]
             block = lax.ppermute(block, "spec", pairs)
-        block_cells = lax.dynamic_index_in_dim(cells, src, 0, keepdims=False)
-        new_cells = new_cells.at[:, block_cells].add(
-            block, mode="promise_in_bounds", unique_indices=True
-        )
+        returned.append(block)
+    recv_cells = jnp.roll(cells[::-1], me + 1, axis=0).reshape(-1)
+    new_cells = flat_cells.at[:, recv_cells].add(
+        jnp.concatenate(returned, axis=1), mode="promise_in_bounds", unique_indices=True
+    )
     updated = new_cells.reshape(smoothed.shape)
     return (updated, source_terms.astype(jnp.bfloat16)[None])
 

time: 244 us -> 224 us (0.918)
  the two profiles are of different devices: /device:TPU:9 before, /device:TPU:0 now
where the time goes in v5:
time: 224 us; the launch traced here: 223 us
  waiting for transfers between devices  85.1 us (38%)
  other arithmetic  52.3 us (23%)
  local copies, waits for them, and re-layouts  43.4 us (19%)
  starting transfers between devices  34.1 us (15%)
  Pallas kernels  7.26 us (3%)
    ppermute x14, waiting for transfers between devices, on_device(): block = lax.ppermute(block, 'spec', pairs)  78.7 us
    ppermute x14, starting transfers between devices, on_device(): block = lax.ppermute(block, 'spec', pairs)  27 us
    scatter-add x1, other arithmetic, on_device(): flat_cells.at[:, recv_cells]  21.1 us
    mul x4, other arithmetic, quickest(): face_flux = courant * face_value  16.3 us
    unnamed x31, local copies, waits for them, and re-layouts  12.1 us
    gather x1, local copies, waits for them, and re-layouts, on_device(): flat_cells.at[:, send_cells]  12 us
    pallas_call x1, Pallas kernels, interact_pallas(): pl.pallas_call(interact_kernel, out_shape=jax.ShapeDtypeStruct((NDIR, NFR...  7.26 us
    ppermute x1, starting transfers between devices, extended_2(): lax.ppermute(lax.slice_in_dim(block, block.shape[dim] - width, None, axis...  5.67 us
  transfers between devices with their start and end apart: 16, of which 8 were waited for; matrix products, arithmetic and copies ran while one was open for 5% of the time, Pallas kernels for 0%

profile of v5, /device:TPU:0, one launch (start us, length us, event | category | flops | bytes accessed | tf_op | source)
XLA Modules:
  0.0 223.2 jit_solution(3672511832580032261)
XLA Ops:
  4.5 5.7 %collective-permute-start = (f32[145,6,128]{2,0,1:T(8,128)}, f32[145,6,128]{2,0,1:T(8,128)}, u32[]{:S(2)}, u32[]{:S(2)}) collective-permute-start(f32[145,6,128]{2,0,1:T(8,128)} %copy.41), channel_id=1, source_target_pairs={{0,1},{2,3},{4,5},{6,7},{8,9},{10,11},{12,13},{14,15},{16,17},{18,... | collective-permute-start | bytes 1336328 | tf_op jit(solution)/shard_map/ppermute | solution.py:26
  13.1 4.2 %collective-permute-done.1 = f32[145,6,128]{2,0,1:T(8,128)S(1)} collective-permute-done((f32[145,6,128]{2,0,1:T(8,128)S(1)}, f32[145,6,128]{2,0,1:T(8,128)S(1)}, u32[]{:S(2)}, u32[]{:S(2)}) %collective-permute-start.1) | collective-permute-done | bytes 445472 | tf_op jit(solution)/shard_map/ppermute | solution.py:29
  17.4 2.2 %collective-permute-done = f32[145,6,128]{2,0,1:T(8,128)} collective-permute-done((f32[145,6,128]{2,0,1:T(8,128)}, f32[145,6,128]{2,0,1:T(8,128)}, u32[]{:S(2)}, u32[]{:S(2)}) %collective-permute-start) | collective-permute-done | bytes 445472 | tf_op jit(solution)/shard_map/ppermute | solution.py:26
  21.4 2.8 %fusion.18 = f32[144,41,128]{2,1,0:T(8,128)S(1)} fusion(f32[145,44,128]{2,1,0:T(8,128)S(1)} %pad_maximum_fusion, f32[144]{0:T(256)S(1)} %get-tuple-element.46, f32[144]{0:T(256)S(1)} %get-tuple-element.47, f32[144]{0:T(256)S(1)} %get-tuple-element.41, pred[144]{0:T(512)(128)(4,1)S(1)} %get-tuple-element.40), kind=kLoop, calls=%fused_computation.36 | loop fusion | flops 11335680 | bytes 15116112 | tf_op jit(solution)/shard_map/mul | solution.py:58
  25.3 5.4 %fusion.4 = f32[144,40,129]{2,1,0:T(8,128)S(1)} fusion(f32[144,40,128]{2,1,0:T(8,128)S(1)} %fusion.30, f32[144]{0:T(256)S(1)} %get-tuple-element.39, f32[144]{0:T(256)S(1)} %get-tuple-element.38, f32[144]{0:T(256)S(1)} %get-tuple-element.17, pred[144]{0:T(512)(128)(4,1)S(1)} %get-tuple-element.16), kind=kLoop, calls=%fused_computation.20 | loop fusion | flops 11145600 | bytes 5923152 | tf_op jit(solution)/shard_map/mul | solution.py:58
  31.5 2.6 %fusion.27 = f32[144,37,128]{2,1,0:T(8,128)S(1)} fusion(f32[144,40,128]{2,1,0:T(8,128)S(1)} %fusion.29, f32[144]{0:T(256)S(1)} %get-tuple-element.46, f32[144]{0:T(256)S(1)} %get-tuple-element.47, f32[144]{0:T(256)S(1)} %get-tuple-element.41, pred[144]{0:T(512)(128)(4,1)S(1)} %get-tuple-element.40), kind=kLoop, calls=%fused_computation.51 | loop fusion | flops 10229760 | bytes 13641552 | tf_op jit(solution)/shard_map/mul | solution.py:58
  35.0 5.4 %fusion.11 = f32[144,36,129]{2,1,0:T(8,128)S(1)} fusion(f32[144,36,128]{2,1,0:T(8,128)S(1)} %fusion.22, f32[144]{0:T(256)S(1)} %get-tuple-element.39, f32[144]{0:T(256)S(1)} %get-tuple-element.38, f32[144]{0:T(256)S(1)} %get-tuple-element.17, pred[144]{0:T(512)(128)(4,1)S(1)} %get-tuple-element.16), kind=kLoop, calls=%fused_computation.27 | loop fusion | flops 10031040 | bytes 5331024 | tf_op jit(solution)/shard_map/mul | solution.py:58
  41.7 3.9 %fusion.37 = f32[144,32,128]{2,1,0:T(8,128)S(1)} fusion(f32[144,32,128]{2,1,0:T(8,128)S(1)} %slice.268, f32[144,36,128]{2,1,0:T(8,128)S(1)} %fusion.21, f32[32,128]{1,0:T(8,128)S(1)} %copy-done.2, f32[144]{0:T(256)S(1)} %get-tuple-element.37, f32[144]{0:T(256)S(1)} %get-tuple-element.36), kind=kLoop, calls=%fused_computation.64 | loop fusion | flops 11796480 | bytes 14173312 | tf_op jit(solution)/shard_map/mul | solution.py:164
  45.6 3.2 %copy.45 = f32[144,32,128]{0,2,1:T(8,128)} copy(f32[144,32,128]{2,1,0:T(8,128)S(1)} %fusion.37) | data formatting | bytes 4718592 | tf_op jit(solution)/shard_map/mul | solution.py:164
  48.8 12.0 %gather_fusion = f32[3072,144]{1,0:T(8,128)S(1)} fusion(f32[144,4096]{0,1:T(8,128)} %bitcast.66, s32[3072]{0:T(1024)S(1)} %broadcast_clamp_fusion), kind=kCustom, calls=%fused_computation | custom fusion | bytes 3551232 | tf_op jit(solution)/shard_map/gather | solution.py:173
  61.1 2.4 %collective-permute-start.7 = (f32[144,384]{0,1:T(8,128)S(1)}, f32[144,384]{0,1:T(8,128)S(1)}, u32[]{:S(2)}, u32[]{:S(2)}) collective-permute-start(f32[144,384]{0,1:T(8,128)S(1)} %get-tuple-element.21), channel_id=1, source_target_pairs={{0,4},{2,6},{4,8},{6,10},{8,12},{10,14},{12,0},{14,2},{1,5},{3,7},... | collective-permute-start | bytes 663560 | tf_op jit(solution)/shard_map/ppermute | solution.py:179
  63.6 2.5 %collective-permute-start.6 = (f32[144,384]{0,1:T(8,128)S(1)}, f32[144,384]{0,1:T(8,128)S(1)}, u32[]{:S(2)}, u32[]{:S(2)}) collective-permute-start(f32[144,384]{0,1:T(8,128)S(1)} %get-tuple-element.22), channel_id=1, source_target_pairs={{0,6},{2,8},{4,10},{6,12},{8,14},{10,0},{12,2},{14,4},{1,7},{3,9},... | collective-permute-start | bytes 663560 | tf_op jit(solution)/shard_map/ppermute | solution.py:179
  68.2 29.6 %collective-permute-done.2 = f32[144,384]{0,1:T(8,128)S(1)} collective-permute-done((f32[144,384]{0,1:T(8,128)S(1)}, f32[144,384]{0,1:T(8,128)S(1)}, u32[]{:S(2)}, u32[]{:S(2)}) %collective-permute-start.2) | collective-permute-done | bytes 221216 | tf_op jit(solution)/shard_map/ppermute | solution.py:179
  99.3 13.0 %collective-permute-done.3 = f32[144,384]{0,1:T(8,128)S(1)} collective-permute-done((f32[144,384]{0,1:T(8,128)S(1)}, f32[144,384]{0,1:T(8,128)S(1)}, u32[]{:S(2)}, u32[]{:S(2)}) %collective-permute-start.3) | collective-permute-done | bytes 221216 | tf_op jit(solution)/shard_map/ppermute | solution.py:179
  112.3 8.8 %collective-permute-start.4 = (f32[144,384]{0,1:T(8,128)S(1)}, f32[144,384]{0,1:T(8,128)S(1)}, u32[]{:S(2)}, u32[]{:S(2)}) collective-permute-start(f32[144,384]{0,1:T(8,128)S(1)} %get-tuple-element.24), channel_id=1, source_target_pairs={{0,10},{2,12},{4,14},{6,0},{8,2},{10,4},{12,6},{14,8},{1,11},{3,13... | collective-permute-start | bytes 663560 | tf_op jit(solution)/shard_map/ppermute | solution.py:179
  121.1 8.2 %collective-permute-done.4 = f32[144,384]{0,1:T(8,128)S(1)} collective-permute-done((f32[144,384]{0,1:T(8,128)S(1)}, f32[144,384]{0,1:T(8,128)S(1)}, u32[]{:S(2)}, u32[]{:S(2)}) %collective-permute-start.4) | collective-permute-done | bytes 221216 | tf_op jit(solution)/shard_map/ppermute | solution.py:179
  135.3 7.3 %shard_map.86 = f32[36,32,384]{2,1,0:T(8,128)} custom-call(s32[4]{0:T(128)} %off_ref.1, f32[32,1]{1,0:T(8,128)} %copy.48.w_ref, f32[36,32,384]{2,1,0:T(8,128)} %bitcast.72), custom_call_target="tpu_custom_call" | custom-call | tf_op jit(solution)/shard_map/pallas_call | solution.py:116
  148.8 5.7 %collective-permute-start.10 = (f32[144,384]{1,0:T(8,128)S(1)}, f32[144,384]{1,0:T(8,128)}, u32[]{:S(2)}, u32[]{:S(2)}) collective-permute-start(f32[144,384]{1,0:T(8,128)S(1)} %get-tuple-element.34), channel_id=1, source_target_pairs={{0,4},{2,6},{4,8},{6,10},{8,12},{10,14},{12,0},{14,2},{1,5},{3,7},... | collective-permute-start | bytes 663560 | tf_op jit(solution)/shard_map/ppermute | solution.py:190
  156.5 3.5 %collective-permute-start.15 = (f32[144,384]{1,0:T(8,128)S(1)}, f32[144,384]{1,0:T(8,128)S(1)}, u32[]{:S(2)}, u32[]{:S(2)}) collective-permute-start(f32[144,384]{1,0:T(8,128)S(1)} %get-tuple-element.29), channel_id=1, source_target_pairs={{0,14},{2,0},{4,2},{6,4},{8,6},{10,8},{12,10},{14,12},{1,15},{3,1}... | collective-permute-start | bytes 663560 | tf_op jit(solution)/shard_map/ppermute | solution.py:190
  160.1 2.9 %collective-permute-done.9 = f32[144,384]{1,0:T(8,128)} collective-permute-done((f32[144,384]{1,0:T(8,128)S(1)}, f32[144,384]{1,0:T(8,128)}, u32[]{:S(2)}, u32[]{:S(2)}) %collective-permute-start.9) | collective-permute-done | bytes 221216 | tf_op jit(solution)/shard_map/ppermute | solution.py:190
  166.7 20.8 %collective-permute-done.11 = f32[144,384]{1,0:T(8,128)S(1)} collective-permute-done((f32[144,384]{1,0:T(8,128)S(1)}, f32[144,384]{1,0:T(8,128)S(1)}, u32[]{:S(2)}, u32[]{:S(2)}) %collective-permute-start.11) | collective-permute-done | bytes 221216 | tf_op jit(solution)/shard_map/ppermute | solution.py:190
  188.1 4.2 %collective-permute-done.12 = f32[144,384]{1,0:T(8,128)S(1)} collective-permute-done((f32[144,384]{1,0:T(8,128)S(1)}, f32[144,384]{1,0:T(8,128)S(1)}, u32[]{:S(2)}, u32[]{:S(2)}) %collective-permute-start.12) | collective-permute-done | bytes 221216 | tf_op jit(solution)/shard_map/ppermute | solution.py:190
  197.3 21.1 %scatter_fusion = f32[144,4096]{0,1:T(8,128)} fusion(f32[144,4096]{0,1:T(8,128)} %bitcast.67, s32[3072]{0:T(1024)S(1)} %bitcast.78, f32[3072,144]{1,0:T(8,128)S(1)} %copy.50), kind=kCustom, calls=%fused_computation.1 | custom fusion | flops 442368 | bytes 5320704 | tf_op jit(solution)/shard_map/scatter-add | solution.py:193
  218.4 4.8 %copy.52 = f32[144,32,128]{2,1,0:T(8,128)} copy(f32[144,32,128]{0,2,1:T(8,128)} %bitcast.68) | data formatting | bytes 4718592
  (93 shorter events, 39.6 us)
Async XLA Ops:
  0.6 9.5 %copy-start.3 = (s32[4]{0:T(128)S(1)}, s32[4]{0:T(128)}, u32[]{:S(2)}) copy-start(s32[4]{0:T(128)} %off_ref.1) | copy-start | bytes 52
  0.6 10.1 %copy-start.5 = (f32[32]{0:T(128)S(1)}, f32[32]{0:T(128)}, u32[]{:S(2)}) copy-start(f32[32]{0:T(128)} %param.15) | copy-start | bytes 388
  0.7 10.1 %copy-start.6 = (f32[32]{0:T(128)S(1)}, f32[32]{0:T(128)}, u32[]{:S(2)}) copy-start(f32[32]{0:T(128)} %param.14) | copy-start | bytes 388
  0.7 10.2 %slice-start = ((s32[32,128]{1,0:T(8,128)}), s32[24,128]{1,0:T(8,128)S(1)}, s32[]{:S(2)}) async-start(s32[32,128]{1,0:T(8,128)} %param.13), calls=%async_computation | async-start | bytes 24576 | tf_op jit(solution)/shard_map/slice | solution.py:171
  0.7 10.5 %copy-start.4 = (f32[32]{0:T(128)S(1)}, f32[32]{0:T(128)}, u32[]{:S(2)}) copy-start(f32[32]{0:T(128)} %param.16) | copy-start | bytes 388
  2.0 18.7 %copy-start = (f32[144,32,128]{2,1,0:T(8,128)S(1)}, f32[144,32,128]{2,1,0:T(8,128)}, u32[]{:S(2)}) copy-start(f32[144,32,128]{2,1,0:T(8,128)} %param.11) | copy-start | bytes 7077892
  2.1 18.7 %copy-start.2 = (f32[32,128]{1,0:T(8,128)S(1)}, f32[32,128]{1,0:T(8,128)}, u32[]{:S(2)}) copy-start(f32[32,128]{1,0:T(8,128)} %param.12) | copy-start | bytes 49156
  2.2 15.1 %collective-permute-start.1 = (f32[145,6,128]{2,0,1:T(8,128)S(1)}, f32[145,6,128]{2,0,1:T(8,128)S(1)}, u32[]{:S(2)}, u32[]{:S(2)}) collective-permute-start(f32[145,6,128]{2,0,1:T(8,128)S(1)} %copy.42), channel_id=1, source_target_pairs={{1,0},{3,2},{5,4},{7,6},{9,8},{11,10},{13,12},{15,14},{17,16},{19,... | collective-permute-start | bytes 1336328 | tf_op jit(solution)/shard_map/ppermute | solution.py:29
  4.5 15.2 %collective-permute-start = (f32[145,6,128]{2,0,1:T(8,128)}, f32[145,6,128]{2,0,1:T(8,128)}, u32[]{:S(2)}, u32[]{:S(2)}) collective-permute-start(f32[145,6,128]{2,0,1:T(8,128)} %copy.41), channel_id=1, source_target_pairs={{0,1},{2,3},{4,5},{6,7},{8,9},{10,11},{12,13},{14,15},{16,17},{18,... | collective-permute-start | bytes 1336328 | tf_op jit(solution)/shard_map/ppermute | solution.py:26
  61.1 68.5 %collective-permute-start.8 = (f32[144,384]{0,1:T(8,128)S(1)}, f32[144,384]{0,1:T(8,128)S(1)}, u32[]{:S(2)}, u32[]{:S(2)}) collective-permute-start(f32[144,384]{0,1:T(8,128)S(1)} %get-tuple-element.20), channel_id=1, source_target_pairs={{0,2},{2,4},{4,6},{6,8},{8,10},{10,12},{12,14},{14,0},{1,3},{3,5},... | collective-permute-start | bytes 663560 | tf_op jit(solution)/shard_map/ppermute | solution.py:179
  61.1 68.4 %collective-permute-start.7 = (f32[144,384]{0,1:T(8,128)S(1)}, f32[144,384]{0,1:T(8,128)S(1)}, u32[]{:S(2)}, u32[]{:S(2)}) collective-permute-start(f32[144,384]{0,1:T(8,128)S(1)} %get-tuple-element.21), channel_id=1, source_target_pairs={{0,4},{2,6},{4,8},{6,10},{8,12},{10,14},{12,0},{14,2},{1,5},{3,7},... | collective-permute-start | bytes 663560 | tf_op jit(solution)/shard_map/ppermute | solution.py:179
  63.6 65.9 %collective-permute-start.6 = (f32[144,384]{0,1:T(8,128)S(1)}, f32[144,384]{0,1:T(8,128)S(1)}, u32[]{:S(2)}, u32[]{:S(2)}) collective-permute-start(f32[144,384]{0,1:T(8,128)S(1)} %get-tuple-element.22), channel_id=1, source_target_pairs={{0,6},{2,8},{4,10},{6,12},{8,14},{10,0},{12,2},{14,4},{1,7},{3,9},... | collective-permute-start | bytes 663560 | tf_op jit(solution)/shard_map/ppermute | solution.py:179
  66.1 63.3 %collective-permute-start.5 = (f32[144,384]{0,1:T(8,128)S(1)}, f32[144,384]{0,1:T(8,128)S(1)}, u32[]{:S(2)}, u32[]{:S(2)}) collective-permute-start(f32[144,384]{0,1:T(8,128)S(1)} %get-tuple-element.23), channel_id=1, source_target_pairs={{0,8},{2,10},{4,12},{6,14},{8,0},{10,2},{12,4},{14,6},{1,9},{3,11}... | collective-permute-start | bytes 663560 | tf_op jit(solution)/shard_map/ppermute | solution.py:179
  67.3 30.4 %collective-permute-start.2 = (f32[144,384]{0,1:T(8,128)S(1)}, f32[144,384]{0,1:T(8,128)S(1)}, u32[]{:S(2)}, u32[]{:S(2)}) collective-permute-start(f32[144,384]{0,1:T(8,128)S(1)} %get-tuple-element.26), channel_id=1, source_target_pairs={{0,14},{2,0},{4,2},{6,4},{8,6},{10,8},{12,10},{14,12},{1,15},{3,1}... | collective-permute-start | bytes 663560 | tf_op jit(solution)/shard_map/ppermute | solution.py:179
  97.8 14.5 %collective-permute-start.3 = (f32[144,384]{0,1:T(8,128)S(1)}, f32[144,384]{0,1:T(8,128)S(1)}, u32[]{:S(2)}, u32[]{:S(2)}) collective-permute-start(f32[144,384]{0,1:T(8,128)S(1)} %get-tuple-element.25), channel_id=1, source_target_pairs={{0,12},{2,14},{4,0},{6,2},{8,4},{10,6},{12,8},{14,10},{1,13},{3,15... | collective-permute-start | bytes 663560 | tf_op jit(solution)/shard_map/ppermute | solution.py:179
  112.3 17.1 %collective-permute-start.4 = (f32[144,384]{0,1:T(8,128)S(1)}, f32[144,384]{0,1:T(8,128)S(1)}, u32[]{:S(2)}, u32[]{:S(2)}) collective-permute-start(f32[144,384]{0,1:T(8,128)S(1)} %get-tuple-element.24), channel_id=1, source_target_pairs={{0,10},{2,12},{4,14},{6,0},{8,2},{10,4},{12,6},{14,8},{1,11},{3,13... | collective-permute-start | bytes 663560 | tf_op jit(solution)/shard_map/ppermute | solution.py:179
  142.5 2.0 copy-start.1
  148.8 15.9 %collective-permute-start.10 = (f32[144,384]{1,0:T(8,128)S(1)}, f32[144,384]{1,0:T(8,128)}, u32[]{:S(2)}, u32[]{:S(2)}) collective-permute-start(f32[144,384]{1,0:T(8,128)S(1)} %get-tuple-element.34), channel_id=1, source_target_pairs={{0,4},{2,6},{4,8},{6,10},{8,12},{10,14},{12,0},{14,2},{1,5},{3,7},... | collective-permute-start | bytes 663560 | tf_op jit(solution)/shard_map/ppermute | solution.py:190
  154.4 8.6 %collective-permute-start.9 = (f32[144,384]{1,0:T(8,128)S(1)}, f32[144,384]{1,0:T(8,128)}, u32[]{:S(2)}, u32[]{:S(2)}) collective-permute-start(f32[144,384]{1,0:T(8,128)S(1)} %get-tuple-element.35), channel_id=1, source_target_pairs={{0,2},{2,4},{4,6},{6,8},{8,10},{10,12},{12,14},{14,0},{1,3},{3,5},... | collective-permute-start | bytes 663560 | tf_op jit(solution)/shard_map/ppermute | solution.py:190
  156.5 37.9 %collective-permute-start.15 = (f32[144,384]{1,0:T(8,128)S(1)}, f32[144,384]{1,0:T(8,128)S(1)}, u32[]{:S(2)}, u32[]{:S(2)}) collective-permute-start(f32[144,384]{1,0:T(8,128)S(1)} %get-tuple-element.29), channel_id=1, source_target_pairs={{0,14},{2,0},{4,2},{6,4},{8,6},{10,8},{12,10},{14,12},{1,15},{3,1}... | collective-permute-start | bytes 663560 | tf_op jit(solution)/shard_map/ppermute | solution.py:190
  160.1 33.7 %collective-permute-start.14 = (f32[144,384]{1,0:T(8,128)S(1)}, f32[144,384]{1,0:T(8,128)S(1)}, u32[]{:S(2)}, u32[]{:S(2)}) collective-permute-start(f32[144,384]{1,0:T(8,128)S(1)} %get-tuple-element.30), channel_id=1, source_target_pairs={{0,12},{2,14},{4,0},{6,2},{8,4},{10,6},{12,8},{14,10},{1,13},{3,15... | collective-permute-start | bytes 663560 | tf_op jit(solution)/shard_map/ppermute | solution.py:190
  160.1 33.0 %collective-permute-start.13 = (f32[144,384]{1,0:T(8,128)S(1)}, f32[144,384]{1,0:T(8,128)S(1)}, u32[]{:S(2)}, u32[]{:S(2)}) collective-permute-start(f32[144,384]{1,0:T(8,128)S(1)} %get-tuple-element.31), channel_id=1, source_target_pairs={{0,10},{2,12},{4,14},{6,0},{8,2},{10,4},{12,6},{14,8},{1,11},{3,13... | collective-permute-start | bytes 663560 | tf_op jit(solution)/shard_map/ppermute | solution.py:190
  163.0 24.4 %collective-permute-start.11 = (f32[144,384]{1,0:T(8,128)S(1)}, f32[144,384]{1,0:T(8,128)S(1)}, u32[]{:S(2)}, u32[]{:S(2)}) collective-permute-start(f32[144,384]{1,0:T(8,128)S(1)} %get-tuple-element.33), channel_id=1, source_target_pairs={{0,6},{2,8},{4,10},{6,12},{8,14},{10,0},{12,2},{14,4},{1,7},{3,9},... | collective-permute-start | bytes 663560 | tf_op jit(solution)/shard_map/ppermute | solution.py:190
  164.7 27.7 %collective-permute-start.12 = (f32[144,384]{1,0:T(8,128)S(1)}, f32[144,384]{1,0:T(8,128)S(1)}, u32[]{:S(2)}, u32[]{:S(2)}) collective-permute-start(f32[144,384]{1,0:T(8,128)S(1)} %get-tuple-element.32), channel_id=1, source_target_pairs={{0,8},{2,10},{4,12},{6,14},{8,0},{10,2},{12,4},{14,6},{1,9},{3,11}... | collective-permute-start | bytes 663560 | tf_op jit(solution)/shard_map/ppermute | solution.py:190

commit v6 on v3

--- a/solution.py
+++ b/solution.py
@@ -21,12 +21,18 @@
 def extended_2(block, sides, width):
     for axis, dim in sides:
         count = lax.axis_size(axis)
-        forward = [(i, i + 1) for i in range(count - 1)]
-        backward = [(target, source) for source, target in forward]
-        low = lax.ppermute(
-            lax.slice_in_dim(block, block.shape[dim] - width, None, axis=dim), axis, forward
-        )
-        high = lax.ppermute(lax.slice_in_dim(block, 0, width, axis=dim), axis, backward)
+        bottom = lax.slice_in_dim(block, block.shape[dim] - width, None, axis=dim)
+        top = lax.slice_in_dim(block, 0, width, axis=dim)
+        if count == 2:
+            first = lax.axis_index(axis) == 0
+            swapped = lax.ppermute(jnp.where(first, bottom, top), axis, [(0, 1), (1, 0)])
+            low = jnp.where(first, 0.0, swapped)
+            high = jnp.where(first, swapped, 0.0)
+        else:
+            forward = [(i, i + 1) for i in range(count - 1)]
+            backward = [(target, source) for source, target in forward]
+            low = lax.ppermute(bottom, axis, forward)
+            high = lax.ppermute(top, axis, backward)
         block = jnp.concatenate([low, block, high], axis=dim)
     return block
 

time: 203 us -> 198 us (0.975)
  starting transfers between devices: 16.5 us -> 11.9 us
  local copies, waits for them, and re-layouts: 40.5 us -> 38.4 us
    ppermute x2 -> x1, starting transfers between devices: 7.11 us -> 3.03 us  [extended_2(): lax.ppermute(jnp.where(first, bottom, top), axis, [(0, 1), (1, 0)])]
    ppermute x2 -> x1, waiting for transfers between devices: 9.09 us -> 10.4 us  [extended_2(): lax.ppermute(jnp.where(first, bottom, top), axis, [(0, 1), (1, 0)])]
  transfers between devices with their start and end apart: 4 -> 3, of which waited for: 4 -> 3; matrix products, arithmetic and copies ran while one was open for 3% -> 2% of each run, Pallas kernels for 0% -> 0%
where the time goes in v6:
time: 198 us; the launch traced here: 197 us
  waiting for transfers between devices  90.3 us (46%)
  other arithmetic  48.4 us (24%)
  local copies, waits for them, and re-layouts  38.4 us (19%)
  starting transfers between devices  11.9 us (6%)
  Pallas kernels  7.27 us (4%)
    all_to_all x1, waiting for transfers between devices, on_device(): lax.all_to_all(source_terms, 'spec', split_axis=0, concat_axis=1, tiled=T...  40.4 us
    all_to_all x1, waiting for transfers between devices, on_device(): lax.all_to_all(columns, 'spec', split_axis=1, concat_axis=0, tiled=True)  39.5 us
    scatter-add x1, other arithmetic, on_device(): flat_cells.at[:, sea_cells]  21.1 us
    mul x4, other arithmetic, quickest(): face_flux = courant * face_value  16.2 us
    gather x1, local copies, waits for them, and re-layouts, on_device(): flat_cells.at[:, sea_cells]  12 us
    ppermute x1, waiting for transfers between devices, extended_2(): lax.ppermute(jnp.where(first, bottom, top), axis, [(0, 1), (1, 0)])  10.4 us
    pallas_call x1, Pallas kernels, interact_pallas(): pl.pallas_call(interact_kernel, out_shape=jax.ShapeDtypeStruct((NDIR, NFR...  7.27 us
    all_to_all x3, local copies, waits for them, and re-layouts, on_device(): lax.all_to_all(source_terms, 'spec', split_axis=0, concat_axis=1, tiled=T...  6.21 us
  transfers between devices with their start and end apart: 3, of which 3 were waited for; matrix products, arithmetic and copies ran while one was open for 2% of the time, Pallas kernels for 0%

profile of v6, /device:TPU:0, one launch (start us, length us, event | category | flops | bytes accessed | tf_op | source)
XLA Modules:
  0.0 197.1 jit_solution(5652467778666909799)
XLA Ops:
  0.7 1.5 fusion.46
  2.3 3.0 %collective-permute-start = (f32[145,6,128]{2,0,1:T(8,128)S(1)}, f32[145,6,128]{2,0,1:T(8,128)S(1)}, u32[]{:S(2)}, u32[]{:S(2)}) collective-permute-start(f32[145,6,128]{2,0,1:T(8,128)S(1)} %copy.50), channel_id=1, source_target_pairs={{0,1},{1,0},{2,3},{3,2},{4,5},{5,4},{6,7},{7,6},{8,9},{9,8},{10,11... | collective-permute-start | bytes 1336328 | tf_op jit(solution)/shard_map/ppermute | solution.py:28
  5.6 10.4 %collective-permute-done = f32[145,6,128]{2,0,1:T(8,128)S(1)} collective-permute-done((f32[145,6,128]{2,0,1:T(8,128)S(1)}, f32[145,6,128]{2,0,1:T(8,128)S(1)}, u32[]{:S(2)}, u32[]{:S(2)}) %collective-permute-start) | collective-permute-done | bytes 445472 | tf_op jit(solution)/shard_map/ppermute | solution.py:28
  16.7 2.8 %fusion.18 = f32[144,41,128]{2,1,0:T(8,128)S(1)} fusion(f32[145,44,128]{2,1,0:T(8,128)S(1)} %pad_maximum_fusion, f32[144]{0:T(256)S(1)} %get-tuple-element.29, f32[144]{0:T(256)S(1)} %get-tuple-element.28, f32[144]{0:T(256)S(1)} %get-tuple-element.27, pred[144]{0:T(512)(128)(4,1)S(1)} %get-tuple-element.26), kind=kLoop, calls=%fused_computation.34 | loop fusion | flops 11335680 | bytes 15116112 | tf_op jit(solution)/shard_map/mul | solution.py:64
  20.4 5.3 %fusion.4 = f32[144,40,129]{2,1,0:T(8,128)S(1)} fusion(f32[144,40,128]{2,1,0:T(8,128)S(1)} %fusion.29, f32[144]{0:T(256)S(1)} %get-tuple-element.25, f32[144]{0:T(256)S(1)} %get-tuple-element.24, f32[144]{0:T(256)S(1)} %get-tuple-element.17, pred[144]{0:T(512)(128)(4,1)S(1)} %get-tuple-element.16), kind=kLoop, calls=%fused_computation.18 | loop fusion | flops 11145600 | bytes 5923152 | tf_op jit(solution)/shard_map/mul | solution.py:64
  26.6 2.6 %fusion.26 = f32[144,37,128]{2,1,0:T(8,128)S(1)} fusion(f32[144,40,128]{2,1,0:T(8,128)S(1)} %fusion.28, f32[144]{0:T(256)S(1)} %get-tuple-element.29, f32[144]{0:T(256)S(1)} %get-tuple-element.28, f32[144]{0:T(256)S(1)} %get-tuple-element.27, pred[144]{0:T(512)(128)(4,1)S(1)} %get-tuple-element.26), kind=kLoop, calls=%fused_computation.46 | loop fusion | flops 10229760 | bytes 13641552 | tf_op jit(solution)/shard_map/mul | solution.py:64
  30.1 5.4 %fusion.11 = f32[144,36,129]{2,1,0:T(8,128)S(1)} fusion(f32[144,36,128]{2,1,0:T(8,128)S(1)} %fusion.21, f32[144]{0:T(256)S(1)} %get-tuple-element.25, f32[144]{0:T(256)S(1)} %get-tuple-element.24, f32[144]{0:T(256)S(1)} %get-tuple-element.17, pred[144]{0:T(512)(128)(4,1)S(1)} %get-tuple-element.16), kind=kLoop, calls=%fused_computation.25 | loop fusion | flops 10031040 | bytes 5331024 | tf_op jit(solution)/shard_map/mul | solution.py:64
  36.7 3.9 %fusion.36 = f32[144,32,128]{2,1,0:T(8,128)S(1)} fusion(f32[144,32,128]{2,1,0:T(8,128)S(1)} %slice.207, f32[144,36,128]{2,1,0:T(8,128)S(1)} %fusion.20, f32[32,128]{1,0:T(8,128)S(1)} %copy-done.2, f32[144]{0:T(256)S(1)} %get-tuple-element.23, f32[144]{0:T(256)S(1)} %get-tuple-element.22), kind=kLoop, calls=%fused_computation.59 | loop fusion | flops 11796480 | bytes 14173312 | tf_op jit(solution)/shard_map/mul | solution.py:170
  40.6 3.3 %copy.53 = f32[144,32,128]{0,2,1:T(8,128)} copy(f32[144,32,128]{2,1,0:T(8,128)S(1)} %fusion.36) | data formatting | bytes 4718592 | tf_op jit(solution)/shard_map/mul | solution.py:170
  43.9 12.0 %gather_fusion = f32[3072,144]{1,0:T(8,128)S(1)} fusion(f32[144,4096]{0,1:T(8,128)} %bitcast.27, s32[3072]{0:T(1024)S(1)} %broadcast_clamp_fusion), kind=kCustom, calls=%fused_computation | custom fusion | bytes 3551232 | tf_op jit(solution)/shard_map/gather | solution.py:175
  55.9 2.0 %copy.54 = f32[144,8,384]{2,0,1:T(8,128)} copy(f32[144,8,384]{0,2,1:T(8,128)S(1)} %bitcast.31) | data formatting | bytes 3538944 | tf_op jit(solution)/shard_map/all_to_all | solution.py:176
  57.9 5.3 %all-to-all-start = ((f32[144,8,384]{2,0,1:T(8,128)}), f32[144,8,384]{2,0,1:T(8,128)}, u32[]{:S(2)}, u32[]{:S(2)}) async-start(f32[144,8,384]{2,0,1:T(8,128)} %copy.54), calls=%async_computation | async-start | bytes 3538944 | tf_op jit(solution)/shard_map/all_to_all | solution.py:176
  65.8 39.5 %all-to-all-done = f32[144,8,384]{2,0,1:T(8,128)} async-done(((f32[144,8,384]{2,0,1:T(8,128)}), f32[144,8,384]{2,0,1:T(8,128)}, u32[]{:S(2)}, u32[]{:S(2)}) %all-to-all-start) | async-done | bytes 1769504 | tf_op jit(solution)/shard_map/all_to_all | solution.py:176
  105.3 1.5 reshape.168
  106.8 1.5 copy.66
  108.4 7.3 %shard_map.86 = f32[36,32,384]{2,1,0:T(8,128)} custom-call(s32[4]{0:T(128)} %off_ref.1, f32[32,1]{1,0:T(8,128)} %copy.56.w_ref, f32[36,32,384]{2,1,0:T(8,128)} %bitcast.33), custom_call_target="tpu_custom_call" | custom-call | tf_op jit(solution)/shard_map/pallas_call | solution.py:122
  115.6 3.8 %copy.57 = f32[32,36,384]{2,1,0:T(8,128)} copy(f32[32,36,384]{2,0,1:T(8,128)} %bitcast.30) | data formatting | bytes 3538944 | tf_op jit(solution)/shard_map/transpose | solution.py:133
  119.4 2.7 %all_to_all.29 = f32[8,144,384]{2,1,0:T(8,128)} reshape(f32[32,36,384]{2,1,0:T(8,128)} %copy.57) | data formatting | bytes 3538944 | tf_op jit(solution)/shard_map/all_to_all | solution.py:178
  122.1 3.6 %all-to-all-start.1 = ((f32[8,144,384]{2,1,0:T(8,128)}), f32[8,144,384]{2,1,0:T(8,128)S(1)}, u32[]{:S(2)}, u32[]{:S(2)}) async-start(f32[8,144,384]{2,1,0:T(8,128)} %all_to_all.29), calls=%async_computation.1 | async-start | bytes 3538944 | tf_op jit(solution)/shard_map/all_to_all | solution.py:178
  127.2 40.4 %all-to-all-done.1 = f32[8,144,384]{2,1,0:T(8,128)S(1)} async-done(((f32[8,144,384]{2,1,0:T(8,128)}), f32[8,144,384]{2,1,0:T(8,128)S(1)}, u32[]{:S(2)}, u32[]{:S(2)}) %all-to-all-start.1) | async-done | bytes 1769504 | tf_op jit(solution)/shard_map/all_to_all | solution.py:178
  167.6 1.4 copy.62
  169.0 2.1 %copy.59 = f32[3072,144]{1,0:T(8,128)S(1)} copy(f32[3072,144]{0,1:T(8,128)} %bitcast.34) | data formatting | bytes 3538944 | tf_op jit(solution)/shard_map/all_to_all | solution.py:178
  171.2 21.1 %scatter_fusion = f32[144,4096]{0,1:T(8,128)} fusion(f32[144,4096]{0,1:T(8,128)} %bitcast.28, s32[3072]{0:T(1024)S(1)} %bitcast.40, f32[3072,144]{1,0:T(8,128)S(1)} %copy.59), kind=kCustom, calls=%fused_computation.1 | custom fusion | flops 442368 | bytes 5320704 | tf_op jit(solution)/shard_map/scatter-add | solution.py:179
  192.3 4.8 %copy.61 = f32[144,32,128]{2,1,0:T(8,128)} copy(f32[144,32,128]{0,2,1:T(8,128)} %bitcast.29) | data formatting | bytes 4718592
  (40 shorter events, 8.8 us)
Async XLA Ops:
  0.6 15.5 %copy-start = (f32[144,32,128]{2,1,0:T(8,128)S(1)}, f32[144,32,128]{2,1,0:T(8,128)}, u32[]{:S(2)}) copy-start(f32[144,32,128]{2,1,0:T(8,128)} %param.7) | copy-start | bytes 7077892
  0.6 15.5 %copy-start.2 = (f32[32,128]{1,0:T(8,128)S(1)}, f32[32,128]{1,0:T(8,128)}, u32[]{:S(2)}) copy-start(f32[32,128]{1,0:T(8,128)} %param.8) | copy-start | bytes 49156
  0.7 4.7 %copy-start.5 = (f32[32]{0:T(128)S(1)}, f32[32]{0:T(128)}, u32[]{:S(2)}) copy-start(f32[32]{0:T(128)} %param.11) | copy-start | bytes 388
  0.7 4.7 %copy-start.6 = (f32[32]{0:T(128)S(1)}, f32[32]{0:T(128)}, u32[]{:S(2)}) copy-start(f32[32]{0:T(128)} %param.10) | copy-start | bytes 388
  0.7 4.9 %slice-start = ((s32[32,128]{1,0:T(8,128)}), s32[24,128]{1,0:T(8,128)S(1)}, s32[]{:S(2)}) async-start(s32[32,128]{1,0:T(8,128)} %param.9), calls=%async_computation.2 | async-start | bytes 24576 | tf_op jit(solution)/shard_map/slice | solution.py:174
  2.3 13.7 %collective-permute-start = (f32[145,6,128]{2,0,1:T(8,128)S(1)}, f32[145,6,128]{2,0,1:T(8,128)S(1)}, u32[]{:S(2)}, u32[]{:S(2)}) collective-permute-start(f32[145,6,128]{2,0,1:T(8,128)S(1)} %copy.50), channel_id=1, source_target_pairs={{0,1},{1,0},{2,3},{3,2},{4,5},{5,4},{6,7},{7,6},{8,9},{9,8},{10,11... | collective-permute-start | bytes 1336328 | tf_op jit(solution)/shard_map/ppermute | solution.py:28
  57.9 5.3 %copy-start.3 = (s32[4]{0:T(128)S(1)}, s32[4]{0:T(128)}, u32[]{:S(2)}) copy-start(s32[4]{0:T(128)} %off_ref.1) | copy-start | bytes 52
  57.9 5.9 %copy-start.4 = (f32[32]{0:T(128)S(1)}, f32[32]{0:T(128)}, u32[]{:S(2)}) copy-start(f32[32]{0:T(128)} %param.12) | copy-start | bytes 388
  57.9 47.4 %all-to-all-start = ((f32[144,8,384]{2,0,1:T(8,128)}), f32[144,8,384]{2,0,1:T(8,128)}, u32[]{:S(2)}, u32[]{:S(2)}) async-start(f32[144,8,384]{2,0,1:T(8,128)} %copy.54), calls=%async_computation | async-start | bytes 3538944 | tf_op jit(solution)/shard_map/all_to_all | solution.py:176
  119.4 6.3 %copy-start.1 = (f32[36,32,384]{2,1,0:T(8,128)S(1)}, f32[36,32,384]{2,1,0:T(8,128)}, u32[]{:S(2)}) copy-start(f32[36,32,384]{2,1,0:T(8,128)} %shard_map.86) | copy-start | bytes 5308420
  122.1 45.5 %all-to-all-start.1 = ((f32[8,144,384]{2,1,0:T(8,128)}), f32[8,144,384]{2,1,0:T(8,128)S(1)}, u32[]{:S(2)}, u32[]{:S(2)}) async-start(f32[8,144,384]{2,1,0:T(8,128)} %all_to_all.29), calls=%async_computation.1 | async-start | bytes 3538944 | tf_op jit(solution)/shard_map/all_to_all | solution.py:178

commit v7 on v3

--- a/solution.py
+++ b/solution.py
@@ -18,17 +18,17 @@
 gain_cross = 0.9375 ** (-4)
 
 
-def extended_2(block, sides, width):
-    for axis, dim in sides:
-        count = lax.axis_size(axis)
-        forward = [(i, i + 1) for i in range(count - 1)]
-        backward = [(target, source) for source, target in forward]
-        low = lax.ppermute(
-            lax.slice_in_dim(block, block.shape[dim] - width, None, axis=dim), axis, forward
-        )
-        high = lax.ppermute(lax.slice_in_dim(block, 0, width, axis=dim), axis, backward)
-        block = jnp.concatenate([low, block, high], axis=dim)
-    return block
+def border_rows(block, axis, dim, width):
+    count = lax.axis_size(axis)
+    bottom = lax.slice_in_dim(block, block.shape[dim] - width, None, axis=dim)
+    top = lax.slice_in_dim(block, 0, width, axis=dim)
+    if count == 2:
+        first = lax.axis_index(axis) == 0
+        swapped = lax.ppermute(jnp.where(first, bottom, top), axis, [(0, 1), (1, 0)])
+        return jnp.where(first, 0.0, swapped), jnp.where(first, swapped, 0.0)
+    forward = [(i, i + 1) for i in range(count - 1)]
+    backward = [(target, source) for source, target in forward]
+    return lax.ppermute(bottom, axis, forward), lax.ppermute(top, axis, backward)
 
 
 def cut_slab(values, offset, length, along):
@@ -157,13 +157,24 @@
     spread_y = (spread * (sines * sines + 0.25 * cosines * cosines))[:, None, None]
     spread_x = (spread * (cosines * cosines + 0.25 * sines * sines))[:, None, None]
     stacked = jnp.concatenate([transparency[None], spectrum], axis=0)
-    reach = 2 * SUBSTEPS
-    extended = extended_2(stacked, (("lat", 1),), reach + 2)
-    with_rim = propagate(extended[1:], extended[0], courant_y, courant_x)
-    centre = cut_slab(with_rim, 2, band_rows, 1)
-    smoothed = (
-        centre + spread_y * laplace(with_rim, 1) + spread_x * laplace(pad_along(centre), 2)
-    ) * transparency
+    width = 2 * SUBSTEPS + 2
+
+    def smooth_window(window):
+        rows = window.shape[1] - 2 * width
+        with_rim = propagate(window[1:], window[0], courant_y, courant_x)
+        centre = cut_slab(with_rim, 2, rows, 1)
+        return (
+            centre + spread_y * laplace(with_rim, 1) + spread_x * laplace(pad_along(centre), 2)
+        ) * cut_slab(window[0], width, rows, 0)
+
+    low, high = border_rows(stacked, "lat", 1, width)
+    if band_rows > 2 * width:
+        inner = smooth_window(stacked)
+        top = smooth_window(jnp.concatenate([low, stacked[:, : 2 * width]], axis=1))
+        bottom = smooth_window(jnp.concatenate([stacked[:, band_rows - 2 * width :], high], axis=1))
+        smoothed = jnp.concatenate([top, inner, bottom], axis=1)
+    else:
+        smoothed = smooth_window(jnp.concatenate([low, stacked, high], axis=1))
     flat_cells = smoothed.reshape(local_comps, -1)
     sea_cells = sea_order.reshape(-1)[:SEA_MAX]
     columns = flat_cells.at[:, sea_cells].get(mode="promise_in_bounds", unique_indices=True)

time: 203 us -> 205 us (level)
  other arithmetic: 48.1 us -> 63.4 us
  waiting for transfers between devices: 89 us -> 79.9 us
  starting transfers between devices: 16.5 us -> 11.7 us
    mul x4 -> x8, other arithmetic: 16.2 us -> 25.6 us  [quickest(): face_flux = courant * face_value]
    ppermute x2 -> x1, waiting for transfers between devices: 9.09 us -> 0.01 us  [border_rows(): lax.ppermute(jnp.where(first, bottom, top), axis, [(0, 1), (1, 0)])]
    ppermute x2 -> x1, starting transfers between devices: 7.11 us -> 2.97 us  [border_rows(): lax.ppermute(jnp.where(first, bottom, top), axis, [(0, 1), (1, 0)])]
    mul x1, local copies, waits for them, and re-layouts: 3.28 us -> 0.01 us  [smooth_window(): (centre + spread_y * laplace(with_rim, 1) + spread_x * laplace(pad_along(...]
    concatenate x0 -> x1, local copies, waits for them, and re-layouts: none -> 3.24 us  [on_device(): smoothed = jnp.concatenate([top, inner, bottom], axis=1)]
    select_n x0 -> x2, other arithmetic: none -> 2.65 us  [the longest x1 1.47 us: border_rows(): jnp.where(first, bottom, top)]
    unnamed x15 -> x27, local copies, waits for them, and re-layouts: 4.86 us -> 6.59 us
    mul x1 -> x2, other arithmetic: 3.91 us -> 4.35 us  [smooth_window(): (centre + spread_y * laplace(with_rim, 1) + spread_x * laplace(pad_along(...]
  transfers between devices with their start and end apart: 4 -> 3, of which waited for: 4 -> 2; matrix products, arithmetic and copies ran while one was open for 3% -> 13% of each run, Pallas kernels for 0% -> 0%
where the time goes in v7:
time: 205 us; the launch traced here: 204 us
  waiting for transfers between devices  79.9 us (39%)
  other arithmetic  63.4 us (31%)
  local copies, waits for them, and re-layouts  40.7 us (20%)
  starting transfers between devices  11.7 us (6%)
  Pallas kernels  7.25 us (4%)
    all_to_all x1, waiting for transfers between devices, on_device(): lax.all_to_all(source_terms, 'spec', split_axis=0, concat_axis=1, tiled=T...  40.4 us
    all_to_all x1, waiting for transfers between devices, on_device(): lax.all_to_all(columns, 'spec', split_axis=1, concat_axis=0, tiled=True)  39.5 us
    mul x8, other arithmetic, quickest(): face_flux = courant * face_value  25.6 us
    scatter-add x1, other arithmetic, on_device(): flat_cells.at[:, sea_cells]  21.1 us
    gather x1, local copies, waits for them, and re-layouts, on_device(): flat_cells.at[:, sea_cells]  12 us
    pallas_call x1, Pallas kernels, interact_pallas(): pl.pallas_call(interact_kernel, out_shape=jax.ShapeDtypeStruct((NDIR, NFR...  7.25 us
    unnamed x27, local copies, waits for them, and re-layouts  6.59 us
    all_to_all x1, starting transfers between devices, on_device(): lax.all_to_all(columns, 'spec', split_axis=1, concat_axis=0, tiled=True)  5.01 us
  transfers between devices with their start and end apart: 3, of which 2 were waited for; matrix products, arithmetic and copies ran while one was open for 13% of the time, Pallas kernels for 0%

profile of v7, /device:TPU:0, one launch (start us, length us, event | category | flops | bytes accessed | tf_op | source)
XLA Modules:
  0.0 204.0 jit_solution(16641203749441840563)
XLA Ops:
  3.0 3.0 %collective-permute-start = (f32[145,6,128]{2,0,1:T(8,128)}, f32[145,6,128]{2,0,1:T(8,128)}, u32[]{:S(2)}, u32[]{:S(2)}) collective-permute-start(f32[145,6,128]{2,0,1:T(8,128)} %copy.52), channel_id=1, source_target_pairs={{0,1},{1,0},{2,3},{3,2},{4,5},{5,4},{6,7},{7,6},{8,9},{9,8},{10,11... | collective-permute-start | bytes 1336328 | tf_op jit(solution)/shard_map/ppermute | solution.py:27
  10.9 2.2 %subtract_multiply_fusion = f32[144,29,128]{2,1,0:T(8,128)S(1)} fusion(f32[144,32,128]{2,1,0:T(8,128)S(1)} %copy-done, f32[144]{0:T(256)S(1)} %get-tuple-element.48, f32[144]{0:T(256)S(1)} %get-tuple-element.49, f32[144]{0:T(256)S(1)} %get-tuple-element.39, pred[144]{0:T(512)(128)(4,1)S(1)} %get-tuple-element.38), kind=kLoop, calls=%fused_computation.100 | loop fusion | flops 8017920 | bytes 10692432 | tf_op jit(solution)/shard_map/mul | solution.py:58
  13.9 4.5 %fusion.4 = f32[144,28,129]{2,1,0:T(8,128)S(1)} fusion(f32[144,28,128]{2,1,0:T(8,128)S(1)} %fusion.49, f32[144]{0:T(256)S(1)} %get-tuple-element.37, f32[144]{0:T(256)S(1)} %get-tuple-element.36, f32[144]{0:T(256)S(1)} %get-tuple-element.17, pred[144]{0:T(512)(128)(4,1)S(1)} %get-tuple-element.16), kind=kLoop, calls=%fused_computation.18 | loop fusion | flops 7801920 | bytes 4146768 | tf_op jit(solution)/shard_map/mul | solution.py:58
  19.1 2.2 %fusion.46 = f32[144,25,128]{2,1,0:T(8,128)S(1)} fusion(f32[144,28,128]{2,1,0:T(8,128)S(1)} %fusion.48, f32[144]{0:T(256)S(1)} %get-tuple-element.48, f32[144]{0:T(256)S(1)} %get-tuple-element.49, f32[144]{0:T(256)S(1)} %get-tuple-element.39, pred[144]{0:T(512)(128)(4,1)S(1)} %get-tuple-element.38), kind=kLoop, calls=%fused_computation.92 | loop fusion | flops 6912000 | bytes 9217872 | tf_op jit(solution)/shard_map/mul | solution.py:58
  21.9 3.5 %fusion.11 = f32[144,24,129]{2,1,0:T(8,128)S(1)} fusion(f32[144,24,128]{2,1,0:T(8,128)S(1)} %fusion.69, f32[144]{0:T(256)S(1)} %get-tuple-element.37, f32[144]{0:T(256)S(1)} %get-tuple-element.36, f32[144]{0:T(256)S(1)} %get-tuple-element.17, pred[144]{0:T(512)(128)(4,1)S(1)} %get-tuple-element.16), kind=kLoop, calls=%fused_computation.50 | loop fusion | flops 6687360 | bytes 3554640 | tf_op jit(solution)/shard_map/mul | solution.py:58
  26.6 2.6 %fusion.57 = f32[144,20,128]{2,1,0:T(8,128)S(1)} fusion(f32[144,20,128]{2,1,0:T(8,128)S(1)} %slice.587, f32[144,24,128]{2,1,0:T(8,128)S(1)} %fusion.68, f32[20,128]{1,0:T(8,128)S(1)} %copy-done.9, f32[144]{0:T(256)S(1)} %get-tuple-element.35, f32[144]{0:T(256)S(1)} %get-tuple-element.34), kind=kLoop, calls=%fused_computation.120 | loop fusion | flops 7372800 | bytes 8858752 | tf_op jit(solution)/shard_map/mul | solution.py:166
  30.8 2.3 %fusion.80 = (f32[144,15,128]{2,1,0:T(8,128)S(1)}, f32[144,15,128]{2,1,0:T(8,128)S(1)}) fusion(f32[145,12,128]{2,1,0:T(8,128)S(1)} %fusion.70, f32[145,6,128]{2,1,0:T(8,128)S(1)} %get-tuple-element.20, f32[144]{0:T(256)S(1)} %get-tuple-element.48, f32[144]{0:T(256)S(1)} %get-tuple-element.49, f32[144]{0:T(256)S(1)} %get-tuple-element.39, ...), kind=kLoop, calls=%fused_computation.149 | loop fusion | flops 9400320 | bytes 7973712 | tf_op jit(solution)/shard_map/mul | solution.py:58
  33.7 4.4 %fusion.18 = (f32[144,14,129]{2,1,0:T(8,128)S(1)}, f32[144,14,129]{2,1,0:T(8,128)S(1)}) fusion(f32[144,14,128]{2,1,0:T(8,128)S(1)} %fusion.72, f32[144]{0:T(256)S(1)} %get-tuple-element.37, f32[144]{0:T(256)S(1)} %get-tuple-element.36, f32[144]{0:T(256)S(1)} %get-tuple-element.17, pred[144]{0:T(512)(128)(4,1)S(1)} %get-tuple-element.16, ...), kind=kLoop, calls=%fused_computation.63 | loop fusion | flops 7801920 | bytes 4146768 | tf_op jit(solution)/shard_map/mul | solution.py:58
  38.9 2.3 %fusion.107 = (f32[144,11,128]{2,1,0:T(8,128)S(1)}, f32[144,11,128]{2,1,0:T(8,128)S(1)}) fusion(f32[144,14,128]{2,1,0:T(8,128)S(1)} %fusion.109, f32[144]{0:T(256)S(1)} %get-tuple-element.48, f32[144]{0:T(256)S(1)} %get-tuple-element.49, f32[144]{0:T(256)S(1)} %get-tuple-element.39, pred[144]{0:T(512)(128)(4,1)S(1)} %get-tuple-element.38, ...), kind=kLoop, calls=%fused_computation.187 | loop fusion | flops 6082560 | bytes 8111952 | tf_op jit(solution)/shard_map/mul | solution.py:58
  41.7 4.3 %fusion.25 = (f32[144,10,129]{2,1,0:T(8,128)S(1)}, f32[144,10,129]{2,1,0:T(8,128)S(1)}) fusion(f32[144,10,128]{2,1,0:T(8,128)S(1)} %fusion.102, f32[144]{0:T(256)S(1)} %get-tuple-element.37, f32[144]{0:T(256)S(1)} %get-tuple-element.36, f32[144]{0:T(256)S(1)} %get-tuple-element.17, pred[144]{0:T(512)(128)(4,1)S(1)} %get-tuple-element.16, ...), kind=kLoop, calls=%fused_computation.70 | loop fusion | flops 5572800 | bytes 2962512 | tf_op jit(solution)/shard_map/mul | solution.py:58
  47.0 1.7 fusion.119
  49.1 3.2 %copy.55 = f32[144,32,128]{0,2,1:T(8,128)} copy(f32[144,32,128]{2,1,0:T(8,128)S(1)} %pad_maximum_fusion) | data formatting | bytes 4718592 | tf_op jit(solution)/shard_map/concatenate | solution.py:175
  52.4 12.0 %gather_fusion = f32[3072,144]{1,0:T(8,128)S(1)} fusion(f32[144,4096]{0,1:T(8,128)} %bitcast.35, s32[3072]{0:T(1024)S(1)} %copy-done.8), kind=kCustom, calls=%fused_computation | custom fusion | bytes 3551232 | tf_op jit(solution)/shard_map/gather | solution.py:180
  64.4 2.0 copy.56
  66.4 5.0 %all-to-all-start = ((f32[144,8,384]{2,0,1:T(8,128)}), f32[144,8,384]{2,0,1:T(8,128)S(1)}, u32[]{:S(2)}, u32[]{:S(2)}) async-start(f32[144,8,384]{2,0,1:T(8,128)} %copy.56), calls=%async_computation | async-start | bytes 3538944 | tf_op jit(solution)/shard_map/all_to_all | solution.py:181
  73.9 39.5 %all-to-all-done = f32[144,8,384]{2,0,1:T(8,128)S(1)} async-done(((f32[144,8,384]{2,0,1:T(8,128)}), f32[144,8,384]{2,0,1:T(8,128)S(1)}, u32[]{:S(2)}, u32[]{:S(2)}) %all-to-all-start) | async-done | bytes 1769504 | tf_op jit(solution)/shard_map/all_to_all | solution.py:181
  116.2 1.5 copy.68
  117.7 7.2 %shard_map.86 = f32[36,32,384]{2,1,0:T(8,128)} custom-call(s32[4]{0:T(128)} %off_ref.1, f32[32,1]{1,0:T(8,128)} %copy.58.w_ref, f32[36,32,384]{2,1,0:T(8,128)} %bitcast.42), custom_call_target="tpu_custom_call" | custom-call | tf_op jit(solution)/shard_map/pallas_call | solution.py:116
  125.0 2.5 %copy.59 = f32[32,36,384]{2,1,0:T(8,128)S(1)} copy(f32[32,36,384]{2,0,1:T(8,128)} %bitcast.38) | data formatting | bytes 3538944 | tf_op jit(solution)/shard_map/transpose | solution.py:127
  128.9 3.7 %all-to-all-start.1 = ((f32[8,144,384]{2,1,0:T(8,128)}), f32[8,144,384]{2,1,0:T(8,128)S(1)}, u32[]{:S(2)}, u32[]{:S(2)}) async-start(f32[8,144,384]{2,1,0:T(8,128)} %all_to_all.29), calls=%async_computation.1 | async-start | bytes 3538944 | tf_op jit(solution)/shard_map/all_to_all | solution.py:183
  134.1 40.4 %all-to-all-done.1 = f32[8,144,384]{2,1,0:T(8,128)S(1)} async-done(((f32[8,144,384]{2,1,0:T(8,128)}), f32[8,144,384]{2,1,0:T(8,128)S(1)}, u32[]{:S(2)}, u32[]{:S(2)}) %all-to-all-start.1) | async-done | bytes 1769504 | tf_op jit(solution)/shard_map/all_to_all | solution.py:183
  175.9 2.1 %copy.61 = f32[3072,144]{1,0:T(8,128)S(1)} copy(f32[3072,144]{0,1:T(8,128)} %bitcast.43) | data formatting | bytes 3538944 | tf_op jit(solution)/shard_map/all_to_all | solution.py:183
  178.1 21.1 %scatter_fusion = f32[144,4096]{0,1:T(8,128)} fusion(f32[144,4096]{0,1:T(8,128)} %bitcast.36, s32[3072]{0:T(1024)S(1)} %bitcast.51, f32[3072,144]{1,0:T(8,128)S(1)} %copy.61), kind=kCustom, calls=%fused_computation.1 | custom fusion | flops 442368 | bytes 5320704 | tf_op jit(solution)/shard_map/scatter-add | solution.py:184
  199.2 4.8 %copy.63 = f32[144,32,128]{2,1,0:T(8,128)} copy(f32[144,32,128]{0,2,1:T(8,128)} %bitcast.37) | data formatting | bytes 4718592
  (71 shorter events, 24.7 us)
Async XLA Ops:
  0.6 5.3 %copy-start.3 = (f32[32,128]{1,0:T(8,128)S(1)}, f32[32,128]{1,0:T(8,128)}, u32[]{:S(2)}) copy-start(f32[32,128]{1,0:T(8,128)} %param.8) | copy-start | bytes 49156
  0.6 7.1 %copy-start = (f32[144,32,128]{2,1,0:T(8,128)S(1)}, f32[144,32,128]{2,1,0:T(8,128)}, u32[]{:S(2)}) copy-start(f32[144,32,128]{2,1,0:T(8,128)} %param.7) | copy-start | bytes 7077892
  3.0 26.3 %collective-permute-start = (f32[145,6,128]{2,0,1:T(8,128)}, f32[145,6,128]{2,0,1:T(8,128)}, u32[]{:S(2)}, u32[]{:S(2)}) collective-permute-start(f32[145,6,128]{2,0,1:T(8,128)} %copy.52), channel_id=1, source_target_pairs={{0,1},{1,0},{2,3},{3,2},{4,5},{5,4},{6,7},{7,6},{8,9},{9,8},{10,11... | collective-permute-start | bytes 1336328 | tf_op jit(solution)/shard_map/ppermute | solution.py:27
  10.2 0.6 copy-start.5
  13.9 4.5 %copy-start.7 = (f32[28,128]{1,0:T(8,128)S(1)}, f32[28,128]{1,0:T(8,128)}, u32[]{:S(2)}) copy-start(f32[28,128]{1,0:T(8,128)} %slice.467) | copy-start | bytes 43012
  21.9 3.5 %copy-start.10 = (f32[24,128]{1,0:T(8,128)S(1)}, f32[24,128]{1,0:T(8,128)}, u32[]{:S(2)}) copy-start(f32[24,128]{1,0:T(8,128)} %slice.481) | copy-start | bytes 36868
  25.9 0.7 copy-start.9
  26.6 3.8 %copy-start.4 = (f32[32,128]{1,0:T(8,128)S(1)}, f32[32,128]{1,0:T(8,128)}, u32[]{:S(2)}) copy-start(f32[32,128]{1,0:T(8,128)} %param.8) | copy-start | bytes 49156
  49.1 3.3 %copy-start.8 = (s32[3072]{0:T(1024)S(1)}, s32[3072]{0:T(1024)}, u32[]{:S(2)}) copy-start(s32[3072]{0:T(1024)} %broadcast_clamp_fusion) | copy-start | bytes 36868
  66.4 5.0 %copy-start.11 = (s32[4]{0:T(128)S(1)}, s32[4]{0:T(128)}, u32[]{:S(2)}) copy-start(s32[4]{0:T(128)} %off_ref.1) | copy-start | bytes 52
  66.4 5.6 %copy-start.12 = (f32[32]{0:T(128)S(1)}, f32[32]{0:T(128)}, u32[]{:S(2)}) copy-start(f32[32]{0:T(128)} %param.12) | copy-start | bytes 388
  66.4 47.0 %all-to-all-start = ((f32[144,8,384]{2,0,1:T(8,128)}), f32[144,8,384]{2,0,1:T(8,128)S(1)}, u32[]{:S(2)}, u32[]{:S(2)}) async-start(f32[144,8,384]{2,0,1:T(8,128)} %copy.56), calls=%async_computation | async-start | bytes 3538944 | tf_op jit(solution)/shard_map/all_to_all | solution.py:181
  113.5 1.2 copy-start.2
  128.9 3.7 %copy-start.1 = (f32[36,32,384]{2,1,0:T(8,128)S(1)}, f32[36,32,384]{2,1,0:T(8,128)}, u32[]{:S(2)}) copy-start(f32[36,32,384]{2,1,0:T(8,128)} %shard_map.86) | copy-start | bytes 5308420
  128.9 45.7 %all-to-all-start.1 = ((f32[8,144,384]{2,1,0:T(8,128)}), f32[8,144,384]{2,1,0:T(8,128)S(1)}, u32[]{:S(2)}, u32[]{:S(2)}) async-start(f32[8,144,384]{2,1,0:T(8,128)} %all_to_all.29), calls=%async_computation.1 | async-start | bytes 3538944 | tf_op jit(solution)/shard_map/all_to_all | solution.py:183
  175.9 2.2 %copy-start.6 = (s32[3072,1]{0,1:T(1,128)S(1)}, s32[3072,1]{0,1:T(1,128)}, u32[]{:S(2)}) copy-start(s32[3072,1]{0,1:T(1,128)} %copy-done.5) | copy-start | bytes 36868

commit v8 on v6

--- a/solution.py
+++ b/solution.py
@@ -41,10 +41,6 @@
     return lax.slice_in_dim(values, offset, offset + length, axis=along)
 
 
-def pad_along(values):
-    return jnp.pad(values, ((0, 0), (0, 0), (2, 2)))
-
-
 def quickest(padded, courant, along):
     length = padded.shape[along] - 4
     before_cell = cut_slab(padded, 0, length + 1, along)
@@ -65,6 +61,42 @@
     return cut_slab(padded, 2, length, along) - (
         cut_slab(face_flux, 1, length, along) - cut_slab(face_flux, 0, length, along)
     )
+
+
+def shifted(values, offset, along):
+    config = [(0, 0, 0)] * values.ndim
+    config[along] = (offset, -offset, 0)
+    return lax.pad(values, jnp.zeros((), values.dtype), config)
+
+
+def face_flux(before_cell, left_cell, right_cell, after_cell, courant):
+    curvature = jnp.where(
+        courant > 0,
+        right_cell - 2.0 * left_cell + before_cell,
+        after_cell - 2.0 * right_cell + left_cell,
+    )
+    face_value = (
+        0.5 * (left_cell + right_cell)
+        - 0.5 * courant * (right_cell - left_cell)
+        - (1.0 - courant * courant) / 6.0 * curvature
+    )
+    return courant * face_value
+
+
+def quickest_x(energy, courant):
+    back_two = shifted(energy, 2, 2)
+    back_one = shifted(energy, 1, 2)
+    ahead_one = shifted(energy, -1, 2)
+    ahead_two = shifted(energy, -2, 2)
+    right_face = face_flux(back_one, energy, ahead_one, ahead_two, courant)
+    left_face = face_flux(back_two, back_one, energy, ahead_one, courant)
+    return energy - (right_face - left_face)
+
+
+def laplace_x(centre):
+    near_sum = shifted(centre, 1, 2) + shifted(centre, -1, 2) - 2.0 * centre
+    far_sum = shifted(centre, 2, 2) + shifted(centre, -2, 2) - 2.0 * centre
+    return 4.0 / 3.0 * near_sum - 1.0 / 12.0 * far_sum
 
 
 def laplace(padded, along):
@@ -142,7 +174,7 @@
     for substep in range(SUBSTEPS):
         energy = quickest(energy, courant_y, 1)
         ext_mask = cut_slab(ext_mask, 2, ext_mask.shape[0] - 4, 0)
-        energy = quickest(pad_along(energy), courant_x, 2) * ext_mask
+        energy = quickest_x(energy, courant_x) * ext_mask
     return energy
 
 
@@ -168,7 +200,7 @@
     with_rim = propagate(extended[1:], extended[0], courant_y, courant_x)
     centre = cut_slab(with_rim, 2, band_rows, 1)
     smoothed = (
-        centre + spread_y * laplace(with_rim, 1) + spread_x * laplace(pad_along(centre), 2)
+        centre + spread_y * laplace(with_rim, 1) + spread_x * laplace_x(centre)
     ) * transparency
     flat_cells = smoothed.reshape(local_comps, -1)
     sea_cells = sea_order.reshape(-1)[:SEA_MAX]

time: 198 us -> 196 us (0.990)
  other arithmetic: 48.4 us -> 45.3 us
    mul x4 -> x2, other arithmetic: 16.2 us -> 5.45 us  [quickest(): face_flux = courant * face_value]
    mul x7 -> x6, other arithmetic: 5.6 us -> 13.2 us  [the longest x4 9.35 us: propagate(): energy = quickest_x(energy, courant_x) * ext_mask]
    unnamed x15 -> x17, local copies, waits for them, and re-layouts: 4.86 us -> 6.06 us
where the time goes in v8:
time: 196 us; the launch traced here: 195 us
  waiting for transfers between devices  89.9 us (46%)
  other arithmetic  45.3 us (23%)
  local copies, waits for them, and re-layouts  39.7 us (20%)
  starting transfers between devices  12.1 us (6%)
  Pallas kernels  7.27 us (4%)
    all_to_all x1, waiting for transfers between devices, on_device(): lax.all_to_all(source_terms, 'spec', split_axis=0, concat_axis=1, tiled=T...  40.2 us
    all_to_all x1, waiting for transfers between devices, on_device(): lax.all_to_all(columns, 'spec', split_axis=1, concat_axis=0, tiled=True)  39.3 us
    scatter-add x1, other arithmetic, on_device(): flat_cells.at[:, sea_cells]  21.1 us
    gather x1, local copies, waits for them, and re-layouts, on_device(): flat_cells.at[:, sea_cells]  12 us
    ppermute x1, waiting for transfers between devices, extended_2(): lax.ppermute(jnp.where(first, bottom, top), axis, [(0, 1), (1, 0)])  10.4 us
    mul x4, other arithmetic, propagate(): energy = quickest_x(energy, courant_x) * ext_mask  9.35 us
    pallas_call x1, Pallas kernels, interact_pallas(): pl.pallas_call(interact_kernel, out_shape=jax.ShapeDtypeStruct((NDIR, NFR...  7.27 us
    all_to_all x3, local copies, waits for them, and re-layouts, on_device(): lax.all_to_all(source_terms, 'spec', split_axis=0, concat_axis=1, tiled=T...  6.21 us
  transfers between devices with their start and end apart: 3, of which 3 were waited for; matrix products, arithmetic and copies ran while one was open for 2% of the time, Pallas kernels for 0%

profile of v8, /device:TPU:0, one launch (start us, length us, event | category | flops | bytes accessed | tf_op | source)
XLA Modules:
  0.0 195.1 jit_solution(9799486464406206711)
XLA Ops:
  0.7 1.5 fusion.56
  2.3 3.0 %collective-permute-start = (f32[145,6,128]{2,0,1:T(8,128)S(1)}, f32[145,6,128]{2,0,1:T(8,128)S(1)}, u32[]{:S(2)}, u32[]{:S(2)}) collective-permute-start(f32[145,6,128]{2,0,1:T(8,128)S(1)} %copy.50), channel_id=1, source_target_pairs={{0,1},{1,0},{2,3},{3,2},{4,5},{5,4},{6,7},{7,6},{8,9},{9,8},{10,11... | collective-permute-start | bytes 1336328 | tf_op jit(solution)/shard_map/ppermute | solution.py:28
  5.6 10.4 %collective-permute-done = f32[145,6,128]{2,0,1:T(8,128)S(1)} collective-permute-done((f32[145,6,128]{2,0,1:T(8,128)S(1)}, f32[145,6,128]{2,0,1:T(8,128)S(1)}, u32[]{:S(2)}, u32[]{:S(2)}) %collective-permute-start) | collective-permute-done | bytes 445472 | tf_op jit(solution)/shard_map/ppermute | solution.py:28
  16.7 2.8 %fusion.4 = f32[144,41,128]{2,1,0:T(8,128)S(1)} fusion(f32[145,44,128]{2,1,0:T(8,128)S(1)} %pad_maximum_fusion, f32[144]{0:T(256)S(1)} %get-tuple-element.32, f32[144]{0:T(256)S(1)} %get-tuple-element.33, f32[144]{0:T(256)S(1)} %get-tuple-element.27, pred[144]{0:T(512)(128)(4,1)S(1)} %get-tuple-element.26), kind=kLoop, calls=%fused_computation.20 | loop fusion | flops 11335680 | bytes 15116112 | tf_op jit(solution)/shard_map/mul | solution.py:60
  20.6 4.7 %fusion.13 = f32[144,40,128]{2,1,0:T(8,128)S(1)} fusion(f32[144,40,128]{2,1,0:T(8,128)S(1)} %fusion.39, f32[40,128]{1,0:T(8,128)S(1)} %maximum_bitcast_fusion.1, f32[144]{0:T(256)S(1)} %get-tuple-element.25, f32[144]{0:T(256)S(1)} %get-tuple-element.24, f32[144]{0:T(256)S(1)} %get-tuple-element.17, pred[144]{0:T(512)(128)(4,1)S(1)} %get-tuple-element.16), kind=kLoop, calls=%fused_computation.30 | loop fusion | flops 22118400 | bytes 5920592 | tf_op jit(solution)/shard_map/mul | solution.py:177
  25.3 2.6 %fusion.38 = f32[144,37,128]{2,1,0:T(8,128)S(1)} fusion(f32[144,40,128]{2,1,0:T(8,128)S(1)} %fusion.13, f32[144]{0:T(256)S(1)} %get-tuple-element.32, f32[144]{0:T(256)S(1)} %get-tuple-element.33, f32[144]{0:T(256)S(1)} %get-tuple-element.27, pred[144]{0:T(512)(128)(4,1)S(1)} %get-tuple-element.26), kind=kLoop, calls=%fused_computation.57 | loop fusion | flops 10229760 | bytes 13641552 | tf_op jit(solution)/shard_map/mul | solution.py:60
  28.5 4.7 %fusion.27 = f32[144,36,128]{2,1,0:T(8,128)S(1)} fusion(f32[144,36,128]{2,1,0:T(8,128)S(1)} %fusion.33, f32[36,128]{1,0:T(8,128)S(1)} %maximum_bitcast_fusion, f32[144]{0:T(256)S(1)} %get-tuple-element.25, f32[144]{0:T(256)S(1)} %get-tuple-element.24, f32[144]{0:T(256)S(1)} %get-tuple-element.17, pred[144]{0:T(512)(128)(4,1)S(1)} %get-tuple-element.16), kind=kLoop, calls=%fused_computation.44 | loop fusion | flops 19906560 | bytes 5328720 | tf_op jit(solution)/shard_map/mul | solution.py:177
  33.6 3.9 %fusion.46 = f32[144,32,128]{2,1,0:T(8,128)S(1)} fusion(f32[144,32,128]{2,1,0:T(8,128)S(1)} %slice.148, f32[144,36,128]{2,1,0:T(8,128)S(1)} %fusion.27, f32[32,128]{1,0:T(8,128)S(1)} %copy-done.3, f32[144]{0:T(256)S(1)} %get-tuple-element.23, f32[144]{0:T(256)S(1)} %get-tuple-element.22), kind=kLoop, calls=%fused_computation.67 | loop fusion | flops 11796480 | bytes 14173312 | tf_op jit(solution)/shard_map/mul | solution.py:202
  37.5 3.3 %copy.53 = f32[144,32,128]{0,2,1:T(8,128)} copy(f32[144,32,128]{2,1,0:T(8,128)S(1)} %fusion.46) | data formatting | bytes 4718592 | tf_op jit(solution)/shard_map/mul | solution.py:202
  40.8 12.0 %gather_fusion = f32[3072,144]{1,0:T(8,128)S(1)} fusion(f32[144,4096]{0,1:T(8,128)} %bitcast.27, s32[3072]{0:T(1024)S(1)} %broadcast_clamp_fusion), kind=kCustom, calls=%fused_computation | custom fusion | bytes 3551232 | tf_op jit(solution)/shard_map/gather | solution.py:207
  52.8 2.0 %copy.54 = f32[144,8,384]{2,0,1:T(8,128)} copy(f32[144,8,384]{0,2,1:T(8,128)S(1)} %bitcast.31) | data formatting | bytes 3538944 | tf_op jit(solution)/shard_map/all_to_all | solution.py:208
  54.8 5.3 %all-to-all-start = ((f32[144,8,384]{2,0,1:T(8,128)}), f32[144,8,384]{2,0,1:T(8,128)S(1)}, u32[]{:S(2)}, u32[]{:S(2)}) async-start(f32[144,8,384]{2,0,1:T(8,128)} %copy.54), calls=%async_computation | async-start | bytes 3538944 | tf_op jit(solution)/shard_map/all_to_all | solution.py:208
  62.8 39.3 %all-to-all-done = f32[144,8,384]{2,0,1:T(8,128)S(1)} async-done(((f32[144,8,384]{2,0,1:T(8,128)}), f32[144,8,384]{2,0,1:T(8,128)S(1)}, u32[]{:S(2)}, u32[]{:S(2)}) %all-to-all-start) | async-done | bytes 1769504 | tf_op jit(solution)/shard_map/all_to_all | solution.py:208
  103.3 1.5 reshape.168
  104.8 1.5 copy.66
  106.4 7.3 %shard_map.86 = f32[36,32,384]{2,1,0:T(8,128)} custom-call(s32[4]{0:T(128)} %off_ref.1, f32[32,1]{1,0:T(8,128)} %copy.56.w_ref, f32[36,32,384]{2,1,0:T(8,128)} %bitcast.34), custom_call_target="tpu_custom_call" | custom-call | tf_op jit(solution)/shard_map/pallas_call | solution.py:154
  113.6 3.8 %copy.57 = f32[32,36,384]{2,1,0:T(8,128)} copy(f32[32,36,384]{2,0,1:T(8,128)} %bitcast.30) | data formatting | bytes 3538944 | tf_op jit(solution)/shard_map/transpose | solution.py:165
  117.4 2.7 %all_to_all.29 = f32[8,144,384]{2,1,0:T(8,128)} reshape(f32[32,36,384]{2,1,0:T(8,128)} %copy.57) | data formatting | bytes 3538944 | tf_op jit(solution)/shard_map/all_to_all | solution.py:210
  120.1 3.8 %all-to-all-start.1 = ((f32[8,144,384]{2,1,0:T(8,128)}), f32[8,144,384]{2,1,0:T(8,128)S(1)}, u32[]{:S(2)}, u32[]{:S(2)}) async-start(f32[8,144,384]{2,1,0:T(8,128)} %all_to_all.29), calls=%async_computation.1 | async-start | bytes 3538944 | tf_op jit(solution)/shard_map/all_to_all | solution.py:210
  125.4 40.2 %all-to-all-done.1 = f32[8,144,384]{2,1,0:T(8,128)S(1)} async-done(((f32[8,144,384]{2,1,0:T(8,128)}), f32[8,144,384]{2,1,0:T(8,128)S(1)}, u32[]{:S(2)}, u32[]{:S(2)}) %all-to-all-start.1) | async-done | bytes 1769504 | tf_op jit(solution)/shard_map/all_to_all | solution.py:210
  165.6 1.4 copy.62
  167.0 2.1 %copy.59 = f32[3072,144]{1,0:T(8,128)S(1)} copy(f32[3072,144]{0,1:T(8,128)} %bitcast.35) | data formatting | bytes 3538944 | tf_op jit(solution)/shard_map/all_to_all | solution.py:210
  169.2 21.1 %scatter_fusion = f32[144,4096]{0,1:T(8,128)} fusion(f32[144,4096]{0,1:T(8,128)} %bitcast.28, s32[3072]{0:T(1024)S(1)} %bitcast.41, f32[3072,144]{1,0:T(8,128)S(1)} %copy.59), kind=kCustom, calls=%fused_computation.1 | custom fusion | flops 442368 | bytes 5320704 | tf_op jit(solution)/shard_map/scatter-add | solution.py:211
  190.3 4.8 %copy.61 = f32[144,32,128]{2,1,0:T(8,128)} copy(f32[144,32,128]{0,2,1:T(8,128)} %bitcast.29) | data formatting | bytes 4718592
  (39 shorter events, 8.5 us)
Async XLA Ops:
  0.6 15.5 %copy-start = (f32[144,32,128]{2,1,0:T(8,128)S(1)}, f32[144,32,128]{2,1,0:T(8,128)}, u32[]{:S(2)}) copy-start(f32[144,32,128]{2,1,0:T(8,128)} %param.7) | copy-start | bytes 7077892
  0.6 15.5 %copy-start.3 = (f32[32,128]{1,0:T(8,128)S(1)}, f32[32,128]{1,0:T(8,128)}, u32[]{:S(2)}) copy-start(f32[32,128]{1,0:T(8,128)} %param.8) | copy-start | bytes 49156
  0.7 4.7 %copy-start.6 = (f32[32]{0:T(128)S(1)}, f32[32]{0:T(128)}, u32[]{:S(2)}) copy-start(f32[32]{0:T(128)} %param.11) | copy-start | bytes 388
  0.7 4.7 %copy-start.7 = (f32[32]{0:T(128)S(1)}, f32[32]{0:T(128)}, u32[]{:S(2)}) copy-start(f32[32]{0:T(128)} %param.10) | copy-start | bytes 388
  0.7 4.8 %slice-start = ((s32[32,128]{1,0:T(8,128)}), s32[24,128]{1,0:T(8,128)S(1)}, s32[]{:S(2)}) async-start(s32[32,128]{1,0:T(8,128)} %param.9), calls=%async_computation.2 | async-start | bytes 24576 | tf_op jit(solution)/shard_map/slice | solution.py:206
  2.3 13.7 %collective-permute-start = (f32[145,6,128]{2,0,1:T(8,128)S(1)}, f32[145,6,128]{2,0,1:T(8,128)S(1)}, u32[]{:S(2)}, u32[]{:S(2)}) collective-permute-start(f32[145,6,128]{2,0,1:T(8,128)S(1)} %copy.50), channel_id=1, source_target_pairs={{0,1},{1,0},{2,3},{3,2},{4,5},{5,4},{6,7},{7,6},{8,9},{9,8},{10,11... | collective-permute-start | bytes 1336328 | tf_op jit(solution)/shard_map/ppermute | solution.py:28
  54.8 5.3 %copy-start.4 = (s32[4]{0:T(128)S(1)}, s32[4]{0:T(128)}, u32[]{:S(2)}) copy-start(s32[4]{0:T(128)} %off_ref.1) | copy-start | bytes 52
  54.8 5.9 %copy-start.5 = (f32[32]{0:T(128)S(1)}, f32[32]{0:T(128)}, u32[]{:S(2)}) copy-start(f32[32]{0:T(128)} %param.12) | copy-start | bytes 388
  54.8 47.3 %all-to-all-start = ((f32[144,8,384]{2,0,1:T(8,128)}), f32[144,8,384]{2,0,1:T(8,128)S(1)}, u32[]{:S(2)}, u32[]{:S(2)}) async-start(f32[144,8,384]{2,0,1:T(8,128)} %copy.54), calls=%async_computation | async-start | bytes 3538944 | tf_op jit(solution)/shard_map/all_to_all | solution.py:208
  102.1 1.2 copy-start.2
  117.4 6.5 %copy-start.1 = (f32[36,32,384]{2,1,0:T(8,128)S(1)}, f32[36,32,384]{2,1,0:T(8,128)}, u32[]{:S(2)}) copy-start(f32[36,32,384]{2,1,0:T(8,128)} %shard_map.86) | copy-start | bytes 5308420
  120.1 45.5 %all-to-all-start.1 = ((f32[8,144,384]{2,1,0:T(8,128)}), f32[8,144,384]{2,1,0:T(8,128)S(1)}, u32[]{:S(2)}, u32[]{:S(2)}) async-start(f32[8,144,384]{2,1,0:T(8,128)} %all_to_all.29), calls=%async_computation.1 | async-start | bytes 3538944 | tf_op jit(solution)/shard_map/all_to_all | solution.py:210

commit v9 on v8

--- a/solution.py
+++ b/solution.py
@@ -41,28 +41,6 @@
     return lax.slice_in_dim(values, offset, offset + length, axis=along)
 
 
-def quickest(padded, courant, along):
-    length = padded.shape[along] - 4
-    before_cell = cut_slab(padded, 0, length + 1, along)
-    left_cell = cut_slab(padded, 1, length + 1, along)
-    right_cell = cut_slab(padded, 2, length + 1, along)
-    after_cell = cut_slab(padded, 3, length + 1, along)
-    curvature = jnp.where(
-        courant > 0,
-        right_cell - 2.0 * left_cell + before_cell,
-        after_cell - 2.0 * right_cell + left_cell,
-    )
-    face_value = (
-        0.5 * (left_cell + right_cell)
-        - 0.5 * courant * (right_cell - left_cell)
-        - (1.0 - courant * courant) / 6.0 * curvature
-    )
-    face_flux = courant * face_value
-    return cut_slab(padded, 2, length, along) - (
-        cut_slab(face_flux, 1, length, along) - cut_slab(face_flux, 0, length, along)
-    )
-
-
 def shifted(values, offset, along):
     config = [(0, 0, 0)] * values.ndim
     config[along] = (offset, -offset, 0)
@@ -91,6 +69,14 @@
     right_face = face_flux(back_one, energy, ahead_one, ahead_two, courant)
     left_face = face_flux(back_two, back_one, energy, ahead_one, courant)
     return energy - (right_face - left_face)
+
+
+def quickest_rows(padded, courant):
+    length = padded.shape[1] - 4
+    cells = [cut_slab(padded, offset, length, 1) for offset in range(5)]
+    right_face = face_flux(cells[1], cells[2], cells[3], cells[4], courant)
+    left_face = face_flux(cells[0], cells[1], cells[2], cells[3], courant)
+    return cells[2] - (right_face - left_face)
 
 
 def laplace_x(centre):
@@ -172,7 +158,7 @@
 
 def propagate(energy, ext_mask, courant_y, courant_x):
     for substep in range(SUBSTEPS):
-        energy = quickest(energy, courant_y, 1)
+        energy = quickest_rows(energy, courant_y)
         ext_mask = cut_slab(ext_mask, 2, ext_mask.shape[0] - 4, 0)
         energy = quickest_x(energy, courant_x) * ext_mask
     return energy

time: 196 us -> 197 us (level)
    sub x2, other arithmetic: 1.64 us -> 8.38 us  [quickest_rows(): return cells[2] - (right_face - left_face)]
    mul x2 -> x0, other arithmetic: 5.45 us -> none  [quickest(): face_flux = courant * face_value]
where the time goes in v9:
time: 197 us; the launch traced here: 196 us
  waiting for transfers between devices  89.9 us (46%)
  other arithmetic  46.6 us (24%)
  local copies, waits for them, and re-layouts  39.7 us (20%)
  starting transfers between devices  12.1 us (6%)
  Pallas kernels  7.27 us (4%)
    all_to_all x1, waiting for transfers between devices, on_device(): lax.all_to_all(source_terms, 'spec', split_axis=0, concat_axis=1, tiled=T...  40.2 us
    all_to_all x1, waiting for transfers between devices, on_device(): lax.all_to_all(columns, 'spec', split_axis=1, concat_axis=0, tiled=True)  39.3 us
    scatter-add x1, other arithmetic, on_device(): flat_cells.at[:, sea_cells]  21.1 us
    gather x1, local copies, waits for them, and re-layouts, on_device(): flat_cells.at[:, sea_cells]  12 us
    ppermute x1, waiting for transfers between devices, extended_2(): lax.ppermute(jnp.where(first, bottom, top), axis, [(0, 1), (1, 0)])  10.4 us
    mul x4, other arithmetic, propagate(): energy = quickest_x(energy, courant_x) * ext_mask  9.33 us
    sub x2, other arithmetic, quickest_rows(): return cells[2] - (right_face - left_face)  8.38 us
    pallas_call x1, Pallas kernels, interact_pallas(): pl.pallas_call(interact_kernel, out_shape=jax.ShapeDtypeStruct((NDIR, NFR...  7.27 us
  transfers between devices with their start and end apart: 3, of which 3 were waited for; matrix products, arithmetic and copies ran while one was open for 2% of the time, Pallas kernels for 0%

profile of v9, /device:TPU:0, one launch (start us, length us, event | category | flops | bytes accessed | tf_op | source)
XLA Modules:
  0.0 196.4 jit_solution(8955667249275660855)
XLA Ops:
  0.7 1.5 fusion.66
  2.3 3.0 %collective-permute-start = (f32[145,6,128]{2,0,1:T(8,128)S(1)}, f32[145,6,128]{2,0,1:T(8,128)S(1)}, u32[]{:S(2)}, u32[]{:S(2)}) collective-permute-start(f32[145,6,128]{2,0,1:T(8,128)S(1)} %copy.50), channel_id=1, source_target_pairs={{0,1},{1,0},{2,3},{3,2},{4,5},{5,4},{6,7},{7,6},{8,9},{9,8},{10,11... | collective-permute-start | bytes 1336328 | tf_op jit(solution)/shard_map/ppermute | solution.py:28
  5.6 10.4 %collective-permute-done = f32[145,6,128]{2,0,1:T(8,128)S(1)} collective-permute-done((f32[145,6,128]{2,0,1:T(8,128)S(1)}, f32[145,6,128]{2,0,1:T(8,128)S(1)}, u32[]{:S(2)}, u32[]{:S(2)}) %collective-permute-start) | collective-permute-done | bytes 445472 | tf_op jit(solution)/shard_map/ppermute | solution.py:28
  16.7 4.1 %fusion.44 = f32[144,40,128]{2,1,0:T(8,128)S(1)} fusion(f32[145,44,128]{2,1,0:T(8,128)S(1)} %pad_maximum_fusion, f32[144]{0:T(256)S(1)} %get-tuple-element.32, f32[144]{0:T(256)S(1)} %get-tuple-element.33, f32[144]{0:T(256)S(1)} %get-tuple-element.27, pred[144]{0:T(512)(128)(4,1)S(1)} %get-tuple-element.26), kind=kLoop, calls=%fused_computation.62 | loop fusion | flops 21381120 | bytes 17696592 | tf_op jit(solution)/shard_map/sub | solution.py:79
  20.8 4.7 %fusion.8 = f32[144,40,128]{2,1,0:T(8,128)S(1)} fusion(f32[144,40,128]{2,1,0:T(8,128)S(1)} %fusion.44, f32[40,128]{1,0:T(8,128)S(1)} %maximum_bitcast_fusion.1, f32[144]{0:T(256)S(1)} %get-tuple-element.25, f32[144]{0:T(256)S(1)} %get-tuple-element.24, f32[144]{0:T(256)S(1)} %get-tuple-element.17, pred[144]{0:T(512)(128)(4,1)S(1)} %get-tuple-element.16), kind=kLoop, calls=%fused_computation.23 | loop fusion | flops 22118400 | bytes 5920592 | tf_op jit(solution)/shard_map/mul | solution.py:163
  25.5 4.3 %fusion.33 = f32[144,36,128]{2,1,0:T(8,128)S(1)} fusion(f32[144,40,128]{2,1,0:T(8,128)S(1)} %fusion.8, f32[144]{0:T(256)S(1)} %get-tuple-element.32, f32[144]{0:T(256)S(1)} %get-tuple-element.33, f32[144]{0:T(256)S(1)} %get-tuple-element.27, pred[144]{0:T(512)(128)(4,1)S(1)} %get-tuple-element.26), kind=kLoop, calls=%fused_computation.49 | loop fusion | flops 19243008 | bytes 15927120 | tf_op jit(solution)/shard_map/sub | solution.py:79
  29.8 4.7 %fusion.22 = f32[144,36,128]{2,1,0:T(8,128)S(1)} fusion(f32[144,36,128]{2,1,0:T(8,128)S(1)} %fusion.33, f32[36,128]{1,0:T(8,128)S(1)} %maximum_bitcast_fusion, f32[144]{0:T(256)S(1)} %get-tuple-element.25, f32[144]{0:T(256)S(1)} %get-tuple-element.24, f32[144]{0:T(256)S(1)} %get-tuple-element.17, pred[144]{0:T(512)(128)(4,1)S(1)} %get-tuple-element.16), kind=kLoop, calls=%fused_computation.37 | loop fusion | flops 19906560 | bytes 5328720 | tf_op jit(solution)/shard_map/mul | solution.py:163
  34.8 3.9 %fusion.56 = f32[144,32,128]{2,1,0:T(8,128)S(1)} fusion(f32[144,32,128]{2,1,0:T(8,128)S(1)} %slice.128, f32[144,36,128]{2,1,0:T(8,128)S(1)} %fusion.22, f32[32,128]{1,0:T(8,128)S(1)} %copy-done.3, f32[144]{0:T(256)S(1)} %get-tuple-element.23, f32[144]{0:T(256)S(1)} %get-tuple-element.22), kind=kLoop, calls=%fused_computation.75 | loop fusion | flops 11796480 | bytes 14173312 | tf_op jit(solution)/shard_map/mul | solution.py:188
  38.7 3.3 %copy.53 = f32[144,32,128]{0,2,1:T(8,128)} copy(f32[144,32,128]{2,1,0:T(8,128)S(1)} %fusion.56) | data formatting | bytes 4718592 | tf_op jit(solution)/shard_map/mul | solution.py:188
  42.0 12.0 %gather_fusion = f32[3072,144]{1,0:T(8,128)S(1)} fusion(f32[144,4096]{0,1:T(8,128)} %bitcast.27, s32[3072]{0:T(1024)S(1)} %broadcast_clamp_fusion), kind=kCustom, calls=%fused_computation | custom fusion | bytes 3551232 | tf_op jit(solution)/shard_map/gather | solution.py:193
  54.0 2.0 %copy.54 = f32[144,8,384]{2,0,1:T(8,128)} copy(f32[144,8,384]{0,2,1:T(8,128)S(1)} %bitcast.31) | data formatting | bytes 3538944 | tf_op jit(solution)/shard_map/all_to_all | solution.py:194
  56.1 5.3 %all-to-all-start = ((f32[144,8,384]{2,0,1:T(8,128)}), f32[144,8,384]{2,0,1:T(8,128)S(1)}, u32[]{:S(2)}, u32[]{:S(2)}) async-start(f32[144,8,384]{2,0,1:T(8,128)} %copy.54), calls=%async_computation | async-start | bytes 3538944 | tf_op jit(solution)/shard_map/all_to_all | solution.py:194
  64.0 39.3 %all-to-all-done = f32[144,8,384]{2,0,1:T(8,128)S(1)} async-done(((f32[144,8,384]{2,0,1:T(8,128)}), f32[144,8,384]{2,0,1:T(8,128)S(1)}, u32[]{:S(2)}, u32[]{:S(2)}) %all-to-all-start) | async-done | bytes 1769504 | tf_op jit(solution)/shard_map/all_to_all | solution.py:194
  104.5 1.5 reshape.168
  106.1 1.5 copy.66
  107.6 7.3 %shard_map.86 = f32[36,32,384]{2,1,0:T(8,128)} custom-call(s32[4]{0:T(128)} %off_ref.1, f32[32,1]{1,0:T(8,128)} %copy.56.w_ref, f32[36,32,384]{2,1,0:T(8,128)} %bitcast.34), custom_call_target="tpu_custom_call" | custom-call | tf_op jit(solution)/shard_map/pallas_call | solution.py:140
  114.9 3.8 %copy.57 = f32[32,36,384]{2,1,0:T(8,128)} copy(f32[32,36,384]{2,0,1:T(8,128)} %bitcast.30) | data formatting | bytes 3538944 | tf_op jit(solution)/shard_map/transpose | solution.py:151
  118.7 2.7 %all_to_all.29 = f32[8,144,384]{2,1,0:T(8,128)} reshape(f32[32,36,384]{2,1,0:T(8,128)} %copy.57) | data formatting | bytes 3538944 | tf_op jit(solution)/shard_map/all_to_all | solution.py:196
  121.3 3.8 %all-to-all-start.1 = ((f32[8,144,384]{2,1,0:T(8,128)}), f32[8,144,384]{2,1,0:T(8,128)S(1)}, u32[]{:S(2)}, u32[]{:S(2)}) async-start(f32[8,144,384]{2,1,0:T(8,128)} %all_to_all.29), calls=%async_computation.1 | async-start | bytes 3538944 | tf_op jit(solution)/shard_map/all_to_all | solution.py:196
  126.6 40.2 %all-to-all-done.1 = f32[8,144,384]{2,1,0:T(8,128)S(1)} async-done(((f32[8,144,384]{2,1,0:T(8,128)}), f32[8,144,384]{2,1,0:T(8,128)S(1)}, u32[]{:S(2)}, u32[]{:S(2)}) %all-to-all-start.1) | async-done | bytes 1769504 | tf_op jit(solution)/shard_map/all_to_all | solution.py:196
  166.9 1.4 copy.62
  168.3 2.1 %copy.59 = f32[3072,144]{1,0:T(8,128)S(1)} copy(f32[3072,144]{0,1:T(8,128)} %bitcast.35) | data formatting | bytes 3538944 | tf_op jit(solution)/shard_map/all_to_all | solution.py:196
  170.4 21.1 %scatter_fusion = f32[144,4096]{0,1:T(8,128)} fusion(f32[144,4096]{0,1:T(8,128)} %bitcast.28, s32[3072]{0:T(1024)S(1)} %bitcast.41, f32[3072,144]{1,0:T(8,128)S(1)} %copy.59), kind=kCustom, calls=%fused_computation.1 | custom fusion | flops 442368 | bytes 5320704 | tf_op jit(solution)/shard_map/scatter-add | solution.py:197
  191.6 4.8 %copy.61 = f32[144,32,128]{2,1,0:T(8,128)} copy(f32[144,32,128]{0,2,1:T(8,128)} %bitcast.29) | data formatting | bytes 4718592
  (37 shorter events, 6.9 us)
Async XLA Ops:
  0.6 15.5 %copy-start = (f32[144,32,128]{2,1,0:T(8,128)S(1)}, f32[144,32,128]{2,1,0:T(8,128)}, u32[]{:S(2)}) copy-start(f32[144,32,128]{2,1,0:T(8,128)} %param.7) | copy-start | bytes 7077892
  0.6 15.5 %copy-start.3 = (f32[32,128]{1,0:T(8,128)S(1)}, f32[32,128]{1,0:T(8,128)}, u32[]{:S(2)}) copy-start(f32[32,128]{1,0:T(8,128)} %param.8) | copy-start | bytes 49156
  0.7 4.7 %copy-start.6 = (f32[32]{0:T(128)S(1)}, f32[32]{0:T(128)}, u32[]{:S(2)}) copy-start(f32[32]{0:T(128)} %param.11) | copy-start | bytes 388
  0.7 4.7 %copy-start.7 = (f32[32]{0:T(128)S(1)}, f32[32]{0:T(128)}, u32[]{:S(2)}) copy-start(f32[32]{0:T(128)} %param.10) | copy-start | bytes 388
  0.7 4.8 %slice-start = ((s32[32,128]{1,0:T(8,128)}), s32[24,128]{1,0:T(8,128)S(1)}, s32[]{:S(2)}) async-start(s32[32,128]{1,0:T(8,128)} %param.9), calls=%async_computation.2 | async-start | bytes 24576 | tf_op jit(solution)/shard_map/slice | solution.py:192
  2.3 13.7 %collective-permute-start = (f32[145,6,128]{2,0,1:T(8,128)S(1)}, f32[145,6,128]{2,0,1:T(8,128)S(1)}, u32[]{:S(2)}, u32[]{:S(2)}) collective-permute-start(f32[145,6,128]{2,0,1:T(8,128)S(1)} %copy.50), channel_id=1, source_target_pairs={{0,1},{1,0},{2,3},{3,2},{4,5},{5,4},{6,7},{7,6},{8,9},{9,8},{10,11... | collective-permute-start | bytes 1336328 | tf_op jit(solution)/shard_map/ppermute | solution.py:28
  56.1 5.3 %copy-start.4 = (s32[4]{0:T(128)S(1)}, s32[4]{0:T(128)}, u32[]{:S(2)}) copy-start(s32[4]{0:T(128)} %off_ref.1) | copy-start | bytes 52
  56.1 5.9 %copy-start.5 = (f32[32]{0:T(128)S(1)}, f32[32]{0:T(128)}, u32[]{:S(2)}) copy-start(f32[32]{0:T(128)} %param.12) | copy-start | bytes 388
  56.1 47.3 %all-to-all-start = ((f32[144,8,384]{2,0,1:T(8,128)}), f32[144,8,384]{2,0,1:T(8,128)S(1)}, u32[]{:S(2)}, u32[]{:S(2)}) async-start(f32[144,8,384]{2,0,1:T(8,128)} %copy.54), calls=%async_computation | async-start | bytes 3538944 | tf_op jit(solution)/shard_map/all_to_all | solution.py:194
  103.3 1.2 copy-start.2
  118.7 6.5 %copy-start.1 = (f32[36,32,384]{2,1,0:T(8,128)S(1)}, f32[36,32,384]{2,1,0:T(8,128)}, u32[]{:S(2)}) copy-start(f32[36,32,384]{2,1,0:T(8,128)} %shard_map.86) | copy-start | bytes 5308420
  121.3 45.5 %all-to-all-start.1 = ((f32[8,144,384]{2,1,0:T(8,128)}), f32[8,144,384]{2,1,0:T(8,128)S(1)}, u32[]{:S(2)}, u32[]{:S(2)}) async-start(f32[8,144,384]{2,1,0:T(8,128)} %all_to_all.29), calls=%async_computation.1 | async-start | bytes 3538944 | tf_op jit(solution)/shard_map/all_to_all | solution.py:196

commit v10 on v8

--- a/solution.py
+++ b/solution.py
@@ -194,14 +194,29 @@
     courant_x = (speed_comp * cosines)[:, None, None]
     spread_y = (spread * (sines * sines + 0.25 * cosines * cosines))[:, None, None]
     spread_x = (spread * (cosines * cosines + 0.25 * sines * sines))[:, None, None]
-    stacked = jnp.concatenate([transparency[None], spectrum], axis=0)
-    reach = 2 * SUBSTEPS
-    extended = extended_2(stacked, (("lat", 1),), reach + 2)
-    with_rim = propagate(extended[1:], extended[0], courant_y, courant_x)
-    centre = cut_slab(with_rim, 2, band_rows, 1)
-    smoothed = (
-        centre + spread_y * laplace(with_rim, 1) + spread_x * laplace_x(centre)
-    ) * transparency
+    width = 2 * SUBSTEPS + 2
+    split = local_comps // 2 if local_comps % 2 == 0 else local_comps
+    parts = [
+        jnp.concatenate([transparency[None], spectrum[start : start + split]], axis=0)
+        for start in range(0, local_comps, split)
+    ]
+    extended = [extended_2(part, (("lat", 1),), width) for part in parts]
+    pieces = []
+    start = 0
+    for part in extended:
+        stop = start + part.shape[0] - 1
+        with_rim = propagate(part[1:], part[0], courant_y[start:stop], courant_x[start:stop])
+        centre = cut_slab(with_rim, 2, band_rows, 1)
+        pieces.append(
+            (
+                centre
+                + spread_y[start:stop] * laplace(with_rim, 1)
+                + spread_x[start:stop] * laplace_x(centre)
+            )
+            * transparency
+        )
+        start = stop
+    smoothed = jnp.concatenate(pieces, axis=0)
     flat_cells = smoothed.reshape(local_comps, -1)
     sea_cells = sea_order.reshape(-1)[:SEA_MAX]
     columns = flat_cells.at[:, sea_cells].get(mode="promise_in_bounds", unique_indices=True)

time: 196 us -> 197 us (level)
    mul x1 -> x2, local copies, waits for them, and re-layouts: 3.28 us -> 0.01 us  [propagate(): energy = quickest_x(energy, courant_x) * ext_mask]
    concatenate x0 -> x1, local copies, waits for them, and re-layouts: none -> 3.26 us  [on_device(): smoothed = jnp.concatenate(pieces, axis=0)]
    slice x0 -> x3, local copies, waits for them, and re-layouts: none -> 1.98 us  [the longest x1 1.84 us: on_device(): spectrum[start:start + split]]
    ppermute x1 -> x2, waiting for transfers between devices: 10.4 us -> 10.7 us  [extended_2(): lax.ppermute(jnp.where(first, bottom, top), axis, [(0, 1), (1, 0)])]
    mul x2 -> x4, other arithmetic: 5.45 us -> 5.49 us  [quickest(): face_flux = courant * face_value]
    unnamed x17 -> x19, local copies, waits for them, and re-layouts: 6.06 us -> 6.07 us
  transfers between devices with their start and end apart: 3 -> 4, of which waited for: 3 -> 4; matrix products, arithmetic and copies ran while one was open for 2% -> 3% of each run, Pallas kernels for 0% -> 0%
where the time goes in v10:
time: 197 us; the launch traced here: 196 us
  waiting for transfers between devices  90.5 us (46%)
  other arithmetic  45.7 us (23%)
  local copies, waits for them, and re-layouts  39.7 us (20%)
  starting transfers between devices  12.1 us (6%)
  Pallas kernels  7.25 us (4%)
    all_to_all x1, waiting for transfers between devices, on_device(): lax.all_to_all(source_terms, 'spec', split_axis=0, concat_axis=1, tiled=T...  40.4 us
    all_to_all x1, waiting for transfers between devices, on_device(): lax.all_to_all(columns, 'spec', split_axis=1, concat_axis=0, tiled=True)  39.3 us
    scatter-add x1, other arithmetic, on_device(): flat_cells.at[:, sea_cells]  21.1 us
    gather x1, local copies, waits for them, and re-layouts, on_device(): flat_cells.at[:, sea_cells]  12 us
    ppermute x2, waiting for transfers between devices, extended_2(): lax.ppermute(jnp.where(first, bottom, top), axis, [(0, 1), (1, 0)])  10.7 us
    mul x4, other arithmetic, propagate(): energy = quickest_x(energy, courant_x) * ext_mask  9.31 us
    pallas_call x1, Pallas kernels, interact_pallas(): pl.pallas_call(interact_kernel, out_shape=jax.ShapeDtypeStruct((NDIR, NFR...  7.25 us
    unnamed x19, local copies, waits for them, and re-layouts  6.07 us
  transfers between devices with their start and end apart: 4, of which 4 were waited for; matrix products, arithmetic and copies ran while one was open for 3% of the time, Pallas kernels for 0%

profile of v10, /device:TPU:0, one launch (start us, length us, event | category | flops | bytes accessed | tf_op | source)
XLA Modules:
  0.0 196.1 jit_solution(7908096098827128686)
XLA Ops:
  0.6 1.8 fusion.134
  2.6 3.0 %collective-permute-start = (f32[73,6,128]{2,1,0:T(8,128)S(1)}, f32[73,6,128]{2,1,0:T(8,128)S(1)}, u32[]{:S(2)}, u32[]{:S(2)}) collective-permute-start(f32[73,6,128]{2,1,0:T(8,128)S(1)} %get-tuple-element.20), channel_id=1, source_target_pairs={{0,1},{1,0},{2,3},{3,2},{4,5},{5,4},{6,7},{7,6},{8,9},{9,8},{10,11... | collective-permute-start | bytes 672776 | tf_op jit(solution)/shard_map/ppermute | solution.py:28
  8.3 5.2 %collective-permute-done = f32[73,6,128]{2,1,0:T(8,128)S(1)} collective-permute-done((f32[73,6,128]{2,1,0:T(8,128)S(1)}, f32[73,6,128]{2,1,0:T(8,128)S(1)}, u32[]{:S(2)}, u32[]{:S(2)}) %collective-permute-start) | collective-permute-done | bytes 224288 | tf_op jit(solution)/shard_map/ppermute | solution.py:28
  13.6 5.5 %collective-permute-done.1 = f32[73,6,128]{2,1,0:T(8,128)S(1)} collective-permute-done((f32[73,6,128]{2,1,0:T(8,128)S(1)}, f32[73,6,128]{2,1,0:T(8,128)S(1)}, u32[]{:S(2)}, u32[]{:S(2)}) %collective-permute-start.1) | collective-permute-done | bytes 224288 | tf_op jit(solution)/shard_map/ppermute | solution.py:28
  21.7 2.3 %fusion.22 = f32[72,40,128]{2,1,0:T(8,128)S(1)} fusion(f32[72,40,128]{2,1,0:T(8,128)S(1)} %fusion.83, f32[40,128]{1,0:T(8,128)S(1)} %get-tuple-element.53, f32[72]{0:T(128)S(1)} %get-tuple-element.30, f32[72]{0:T(128)S(1)} %get-tuple-element.29, f32[72]{0:T(128)S(1)} %get-tuple-element.28, pred[72]{0:T(512)(128)(4,1)S(1)} %get-tuple-element.26), kind=kLoop, calls=%fused_computation.56 | loop fusion | flops 11059200 | bytes 2970536 | tf_op jit(solution)/shard_map/mul | solution.py:177
  25.7 2.3 %fusion.36 = f32[72,36,128]{2,1,0:T(8,128)S(1)} fusion(f32[72,36,128]{2,1,0:T(8,128)S(1)} %fusion.77, f32[36,128]{1,0:T(8,128)S(1)} %get-tuple-element.51, f32[72]{0:T(128)S(1)} %get-tuple-element.30, f32[72]{0:T(128)S(1)} %get-tuple-element.29, f32[72]{0:T(128)S(1)} %get-tuple-element.28, pred[72]{0:T(512)(128)(4,1)S(1)} %get-tuple-element.26), kind=kLoop, calls=%fused_computation.70 | loop fusion | flops 9953280 | bytes 2673576 | tf_op jit(solution)/shard_map/mul | solution.py:177
  30.1 2.3 %fusion.50 = f32[72,40,128]{2,1,0:T(8,128)S(1)} fusion(f32[72,40,128]{2,1,0:T(8,128)S(1)} %fusion.76, f32[40,128]{1,0:T(8,128)S(1)} %get-tuple-element.52, f32[72]{0:T(128)S(1)} %get-tuple-element.32, f32[72]{0:T(128)S(1)} %get-tuple-element.31, f32[72]{0:T(128)S(1)} %get-tuple-element.33, pred[72]{0:T(512)(128)(4,1)S(1)} %get-tuple-element.27), kind=kLoop, calls=%fused_computation.84 | loop fusion | flops 11059200 | bytes 2970536 | tf_op jit(solution)/shard_map/mul | solution.py:177
  34.2 2.3 %fusion.64 = f32[72,36,128]{2,1,0:T(8,128)S(1)} fusion(f32[72,36,128]{2,1,0:T(8,128)S(1)} %fusion.70, f32[36,128]{1,0:T(8,128)S(1)} %get-tuple-element.50, f32[72]{0:T(128)S(1)} %get-tuple-element.32, f32[72]{0:T(128)S(1)} %get-tuple-element.31, f32[72]{0:T(128)S(1)} %get-tuple-element.33, pred[72]{0:T(512)(128)(4,1)S(1)} %get-tuple-element.27), kind=kLoop, calls=%fused_computation.98 | loop fusion | flops 9953280 | bytes 2673576 | tf_op jit(solution)/shard_map/mul | solution.py:177
  36.7 2.0 %fusion.90 = f32[72,32,128]{2,1,0:T(8,128)S(1)} fusion(f32[72,32,128]{2,1,0:T(8,128)S(1)} %slice.316, f32[72,36,128]{2,1,0:T(8,128)S(1)} %fusion.36, f32[32,128]{1,0:T(8,128)S(1)} %copy-done.3, f32[72]{0:T(128)S(1)} %get-tuple-element.24, f32[72]{0:T(128)S(1)} %get-tuple-element.22), kind=kLoop, calls=%fused_computation.135 | loop fusion | flops 5898240 | bytes 7094848 | tf_op jit(solution)/shard_map/mul | solution.py:211
  38.7 2.0 fusion.100
  40.9 3.3 %copy.28 = f32[144,32,128]{0,2,1:T(8,128)} copy(f32[144,32,128]{2,1,0:T(8,128)S(1)} %pad_maximum_fusion.2) | data formatting | bytes 4718592 | tf_op jit(solution)/shard_map/concatenate | solution.py:219
  44.1 12.0 %gather_fusion = f32[3072,144]{1,0:T(8,128)S(1)} fusion(f32[144,4096]{0,1:T(8,128)} %bitcast.31, s32[3072]{0:T(1024)S(1)} %copy-done.6), kind=kCustom, calls=%fused_computation | custom fusion | bytes 3551232 | tf_op jit(solution)/shard_map/gather | solution.py:222
  56.2 2.0 %copy.29 = f32[144,8,384]{2,0,1:T(8,128)} copy(f32[144,8,384]{0,2,1:T(8,128)S(1)} %bitcast.35) | data formatting | bytes 3538944 | tf_op jit(solution)/shard_map/all_to_all | solution.py:223
  58.2 5.3 %all-to-all-start = ((f32[144,8,384]{2,0,1:T(8,128)}), f32[144,8,384]{2,0,1:T(8,128)S(1)}, u32[]{:S(2)}, u32[]{:S(2)}) async-start(f32[144,8,384]{2,0,1:T(8,128)} %copy.29), calls=%async_computation | async-start | bytes 3538944 | tf_op jit(solution)/shard_map/all_to_all | solution.py:223
  66.2 39.3 %all-to-all-done = f32[144,8,384]{2,0,1:T(8,128)S(1)} async-done(((f32[144,8,384]{2,0,1:T(8,128)}), f32[144,8,384]{2,0,1:T(8,128)S(1)}, u32[]{:S(2)}, u32[]{:S(2)}) %all-to-all-start) | async-done | bytes 1769504 | tf_op jit(solution)/shard_map/all_to_all | solution.py:223
  106.7 1.5 reshape.135
  108.2 1.5 copy.39
  109.7 7.3 %shard_map.86 = f32[36,32,384]{2,1,0:T(8,128)} custom-call(s32[4]{0:T(128)} %off_ref.1, f32[32,1]{1,0:T(8,128)} %copy.31.w_ref, f32[36,32,384]{2,1,0:T(8,128)} %bitcast.38), custom_call_target="tpu_custom_call" | custom-call | tf_op jit(solution)/shard_map/pallas_call | solution.py:154
  117.0 2.5 %copy.32 = f32[32,36,384]{2,1,0:T(8,128)S(1)} copy(f32[32,36,384]{2,0,1:T(8,128)} %bitcast.34) | data formatting | bytes 3538944 | tf_op jit(solution)/shard_map/transpose | solution.py:165
  120.9 3.7 %all-to-all-start.1 = ((f32[8,144,384]{2,1,0:T(8,128)}), f32[8,144,384]{2,1,0:T(8,128)S(1)}, u32[]{:S(2)}, u32[]{:S(2)}) async-start(f32[8,144,384]{2,1,0:T(8,128)} %all_to_all.29), calls=%async_computation.1 | async-start | bytes 3538944 | tf_op jit(solution)/shard_map/all_to_all | solution.py:225
  126.1 40.4 %all-to-all-done.1 = f32[8,144,384]{2,1,0:T(8,128)S(1)} async-done(((f32[8,144,384]{2,1,0:T(8,128)}), f32[8,144,384]{2,1,0:T(8,128)S(1)}, u32[]{:S(2)}, u32[]{:S(2)}) %all-to-all-start.1) | async-done | bytes 1769504 | tf_op jit(solution)/shard_map/all_to_all | solution.py:225
  168.0 2.1 %copy.34 = f32[3072,144]{1,0:T(8,128)S(1)} copy(f32[3072,144]{0,1:T(8,128)} %bitcast.39) | data formatting | bytes 3538944 | tf_op jit(solution)/shard_map/all_to_all | solution.py:225
  170.1 21.1 %scatter_fusion = f32[144,4096]{0,1:T(8,128)} fusion(f32[144,4096]{0,1:T(8,128)} %bitcast.32, s32[3072]{0:T(1024)S(1)} %bitcast.43, f32[3072,144]{1,0:T(8,128)S(1)} %copy.34), kind=kCustom, calls=%fused_computation.1 | custom fusion | flops 442368 | bytes 5320704 | tf_op jit(solution)/shard_map/scatter-add | solution.py:226
  191.2 4.8 %copy.36 = f32[144,32,128]{2,1,0:T(8,128)} copy(f32[144,32,128]{0,2,1:T(8,128)} %bitcast.33) | data formatting | bytes 4718592
  (56 shorter events, 19.4 us)
Async XLA Ops:
  0.6 1.9 copy-start.2
  2.6 11.0 %collective-permute-start = (f32[73,6,128]{2,1,0:T(8,128)S(1)}, f32[73,6,128]{2,1,0:T(8,128)S(1)}, u32[]{:S(2)}, u32[]{:S(2)}) collective-permute-start(f32[73,6,128]{2,1,0:T(8,128)S(1)} %get-tuple-element.20), channel_id=1, source_target_pairs={{0,1},{1,0},{2,3},{3,2},{4,5},{5,4},{6,7},{7,6},{8,9},{9,8},{10,11... | collective-permute-start | bytes 672776 | tf_op jit(solution)/shard_map/ppermute | solution.py:28
  5.6 13.5 %collective-permute-start.1 = (f32[73,6,128]{2,1,0:T(8,128)S(1)}, f32[73,6,128]{2,1,0:T(8,128)S(1)}, u32[]{:S(2)}, u32[]{:S(2)}) collective-permute-start(f32[73,6,128]{2,1,0:T(8,128)S(1)} %get-tuple-element.21), channel_id=1, source_target_pairs={{0,1},{1,0},{2,3},{3,2},{4,5},{5,4},{6,7},{7,6},{8,9},{9,8},{10,11... | collective-permute-start | bytes 672776 | tf_op jit(solution)/shard_map/ppermute | solution.py:28
  5.7 13.5 %copy-start.3 = (f32[32,128]{1,0:T(8,128)S(1)}, f32[32,128]{1,0:T(8,128)}, u32[]{:S(2)}) copy-start(f32[32,128]{1,0:T(8,128)} %param.8) | copy-start | bytes 49156
  7.6 0.8 copy-start.4
  40.9 3.3 %copy-start.6 = (s32[3072]{0:T(1024)S(1)}, s32[3072]{0:T(1024)}, u32[]{:S(2)}) copy-start(s32[3072]{0:T(1024)} %broadcast_clamp_fusion) | copy-start | bytes 36868
  58.2 5.3 %copy-start.7 = (s32[4]{0:T(128)S(1)}, s32[4]{0:T(128)}, u32[]{:S(2)}) copy-start(s32[4]{0:T(128)} %off_ref.1) | copy-start | bytes 52
  58.2 5.9 %copy-start.8 = (f32[32]{0:T(128)S(1)}, f32[32]{0:T(128)}, u32[]{:S(2)}) copy-start(f32[32]{0:T(128)} %param.12) | copy-start | bytes 388
  58.2 47.3 %all-to-all-start = ((f32[144,8,384]{2,0,1:T(8,128)}), f32[144,8,384]{2,0,1:T(8,128)S(1)}, u32[]{:S(2)}, u32[]{:S(2)}) async-start(f32[144,8,384]{2,0,1:T(8,128)} %copy.29), calls=%async_computation | async-start | bytes 3538944 | tf_op jit(solution)/shard_map/all_to_all | solution.py:223
  105.5 1.2 copy-start.1
  120.9 3.7 %copy-start = (f32[36,32,384]{2,1,0:T(8,128)S(1)}, f32[36,32,384]{2,1,0:T(8,128)}, u32[]{:S(2)}) copy-start(f32[36,32,384]{2,1,0:T(8,128)} %shard_map.86) | copy-start | bytes 5308420
  120.9 45.7 %all-to-all-start.1 = ((f32[8,144,384]{2,1,0:T(8,128)}), f32[8,144,384]{2,1,0:T(8,128)S(1)}, u32[]{:S(2)}, u32[]{:S(2)}) async-start(f32[8,144,384]{2,1,0:T(8,128)} %all_to_all.29), calls=%async_computation.1 | async-start | bytes 3538944 | tf_op jit(solution)/shard_map/all_to_all | solution.py:225
  168.0 2.2 %copy-start.5 = (s32[3072,1]{0,1:T(1,128)S(1)}, s32[3072,1]{0,1:T(1,128)}, u32[]{:S(2)}) copy-start(s32[3072,1]{0,1:T(1,128)} %copy-done.4) | copy-start | bytes 36868

commit v11 on v10

--- a/solution.py
+++ b/solution.py
@@ -18,23 +18,17 @@
 gain_cross = 0.9375 ** (-4)
 
 
-def extended_2(block, sides, width):
-    for axis, dim in sides:
-        count = lax.axis_size(axis)
-        bottom = lax.slice_in_dim(block, block.shape[dim] - width, None, axis=dim)
-        top = lax.slice_in_dim(block, 0, width, axis=dim)
-        if count == 2:
-            first = lax.axis_index(axis) == 0
-            swapped = lax.ppermute(jnp.where(first, bottom, top), axis, [(0, 1), (1, 0)])
-            low = jnp.where(first, 0.0, swapped)
-            high = jnp.where(first, swapped, 0.0)
-        else:
-            forward = [(i, i + 1) for i in range(count - 1)]
-            backward = [(target, source) for source, target in forward]
-            low = lax.ppermute(bottom, axis, forward)
-            high = lax.ppermute(top, axis, backward)
-        block = jnp.concatenate([low, block, high], axis=dim)
-    return block
+def border_rows(block, axis, dim, width):
+    count = lax.axis_size(axis)
+    bottom = lax.slice_in_dim(block, block.shape[dim] - width, None, axis=dim)
+    top = lax.slice_in_dim(block, 0, width, axis=dim)
+    if count == 2:
+        first = lax.axis_index(axis) == 0
+        swapped = lax.ppermute(jnp.where(first, bottom, top), axis, [(0, 1), (1, 0)])
+        return jnp.where(first, 0.0, swapped), jnp.where(first, swapped, 0.0)
+    forward = [(i, i + 1) for i in range(count - 1)]
+    backward = [(target, source) for source, target in forward]
+    return lax.ppermute(bottom, axis, forward), lax.ppermute(top, axis, backward)
 
 
 def cut_slab(values, offset, length, along):
@@ -200,10 +194,13 @@
         jnp.concatenate([transparency[None], spectrum[start : start + split]], axis=0)
         for start in range(0, local_comps, split)
     ]
-    extended = [extended_2(part, (("lat", 1),), width) for part in parts]
+    borders = [border_rows(part, "lat", 1, width) for part in parts]
     pieces = []
     start = 0
-    for part in extended:
+    for part, (low, high) in zip(parts, borders):
+        if pieces:
+            pieces[-1], low, high = lax.optimization_barrier((pieces[-1], low, high))
+        part = jnp.concatenate([low, part, high], axis=1)
         stop = start + part.shape[0] - 1
         with_rim = propagate(part[1:], part[0], courant_y[start:stop], courant_x[start:stop])
         centre = cut_slab(with_rim, 2, band_rows, 1)

time: 197 us -> 198 us (level)
  waiting for transfers between devices: 90.5 us -> 92.7 us
    ppermute x2, waiting for transfers between devices: 10.7 us -> 12.9 us  [border_rows(): lax.ppermute(jnp.where(first, bottom, top), axis, [(0, 1), (1, 0)])]
    unnamed x19 -> x15, local copies, waits for them, and re-layouts: 6.07 us -> 6.06 us
  transfers between devices with their start and end apart: 4 -> 4, of which waited for: 4 -> 3; matrix products, arithmetic and copies ran while one was open for 3% -> 8% of each run, Pallas kernels for 0% -> 0%
where the time goes in v11:
time: 198 us; the launch traced here: 197 us
  waiting for transfers between devices  92.7 us (47%)
  other arithmetic  45.2 us (23%)
  local copies, waits for them, and re-layouts  38.9 us (20%)
  starting transfers between devices  12.1 us (6%)
  Pallas kernels  7.27 us (4%)
    all_to_all x1, waiting for transfers between devices, on_device(): lax.all_to_all(source_terms, 'spec', split_axis=0, concat_axis=1, tiled=T...  40.4 us
    all_to_all x1, waiting for transfers between devices, on_device(): lax.all_to_all(columns, 'spec', split_axis=1, concat_axis=0, tiled=True)  39.4 us
    scatter-add x1, other arithmetic, on_device(): flat_cells.at[:, sea_cells]  21.1 us
    ppermute x2, waiting for transfers between devices, border_rows(): lax.ppermute(jnp.where(first, bottom, top), axis, [(0, 1), (1, 0)])  12.9 us
    gather x1, local copies, waits for them, and re-layouts, on_device(): flat_cells.at[:, sea_cells]  12 us
    mul x4, other arithmetic, propagate(): energy = quickest_x(energy, courant_x) * ext_mask  9.31 us
    pallas_call x1, Pallas kernels, interact_pallas(): pl.pallas_call(interact_kernel, out_shape=jax.ShapeDtypeStruct((NDIR, NFR...  7.27 us
    unnamed x15, local copies, waits for them, and re-layouts  6.06 us
  transfers between devices with their start and end apart: 4, of which 3 were waited for; matrix products, arithmetic and copies ran while one was open for 8% of the time, Pallas kernels for 0%

profile of v11, /device:TPU:0, one launch (start us, length us, event | category | flops | bytes accessed | tf_op | source)
XLA Modules:
  0.0 197.1 jit_solution(8178387434254949204)
XLA Ops:
  0.6 1.8 fusion.134
  2.6 3.0 %collective-permute-start.1 = (f32[73,6,128]{2,1,0:T(8,128)S(1)}, f32[73,6,128]{2,1,0:T(8,128)S(1)}, u32[]{:S(2)}, u32[]{:S(2)}) collective-permute-start(f32[73,6,128]{2,1,0:T(8,128)S(1)} %get-tuple-element.24), channel_id=1, source_target_pairs={{0,1},{1,0},{2,3},{3,2},{4,5},{5,4},{6,7},{7,6},{8,9},{9,8},{10,11... | collective-permute-start | bytes 672776 | tf_op jit(solution)/shard_map/ppermute | solution.py:27
  6.4 12.9 %collective-permute-done = f32[73,6,128]{2,1,0:T(8,128)} collective-permute-done((f32[73,6,128]{2,1,0:T(8,128)S(1)}, f32[73,6,128]{2,1,0:T(8,128)}, u32[]{:S(2)}, u32[]{:S(2)}) %collective-permute-start) | collective-permute-done | bytes 224288 | tf_op jit(solution)/shard_map/ppermute | solution.py:27
  22.5 2.3 %fusion.22 = f32[72,40,128]{2,1,0:T(8,128)S(1)} fusion(f32[72,40,128]{2,1,0:T(8,128)S(1)} %fusion.83, f32[40,128]{1,0:T(8,128)S(1)} %slice_bitcast_fusion.3, f32[72]{0:T(128)S(1)} %get-tuple-element.34, f32[72]{0:T(128)S(1)} %get-tuple-element.33, f32[72]{0:T(128)S(1)} %get-tuple-element.37, pred[72]{0:T(512)(128)(4,1)S(1)} %get-tuple-element.31), kind=kLoop, calls=%fused_computation.56 | loop fusion | flops 11059200 | bytes 2970536 | tf_op jit(solution)/shard_map/mul | solution.py:171
  26.5 2.3 %fusion.36 = f32[72,36,128]{2,1,0:T(8,128)S(1)} fusion(f32[72,36,128]{2,1,0:T(8,128)S(1)} %fusion.77, f32[36,128]{1,0:T(8,128)S(1)} %slice_bitcast_fusion.2, f32[72]{0:T(128)S(1)} %get-tuple-element.34, f32[72]{0:T(128)S(1)} %get-tuple-element.33, f32[72]{0:T(128)S(1)} %get-tuple-element.37, pred[72]{0:T(512)(128)(4,1)S(1)} %get-tuple-element.31), kind=kLoop, calls=%fused_computation.70 | loop fusion | flops 9953280 | bytes 2673576 | tf_op jit(solution)/shard_map/mul | solution.py:171
  29.0 2.0 fusion.90
  31.3 1.4 fusion.8
  33.3 2.3 %fusion.50 = f32[72,40,128]{2,1,0:T(8,128)S(1)} fusion(f32[72,40,128]{2,1,0:T(8,128)S(1)} %fusion.76, f32[40,128]{1,0:T(8,128)S(1)} %slice_bitcast_fusion.1, f32[72]{0:T(128)S(1)} %get-tuple-element.36, f32[72]{0:T(128)S(1)} %get-tuple-element.35, f32[72]{0:T(128)S(1)} %get-tuple-element.32, pred[72]{0:T(512)(128)(4,1)S(1)} %get-tuple-element.30), kind=kLoop, calls=%fused_computation.84 | loop fusion | flops 11059200 | bytes 2970536 | tf_op jit(solution)/shard_map/mul | solution.py:171
  37.3 2.3 %fusion.64 = f32[72,36,128]{2,1,0:T(8,128)S(1)} fusion(f32[72,36,128]{2,1,0:T(8,128)S(1)} %fusion.70, f32[36,128]{1,0:T(8,128)S(1)} %slice_bitcast_fusion, f32[72]{0:T(128)S(1)} %get-tuple-element.36, f32[72]{0:T(128)S(1)} %get-tuple-element.35, f32[72]{0:T(128)S(1)} %get-tuple-element.32, pred[72]{0:T(512)(128)(4,1)S(1)} %get-tuple-element.30), kind=kLoop, calls=%fused_computation.98 | loop fusion | flops 9953280 | bytes 2673576 | tf_op jit(solution)/shard_map/mul | solution.py:171
  39.8 2.0 fusion.100
  41.9 3.3 %copy.28 = f32[144,32,128]{0,2,1:T(8,128)} copy(f32[144,32,128]{2,1,0:T(8,128)S(1)} %pad_maximum_fusion.2) | data formatting | bytes 4718592 | tf_op jit(solution)/shard_map/concatenate | solution.py:216
  45.2 12.0 %gather_fusion = f32[3072,144]{1,0:T(8,128)S(1)} fusion(f32[144,4096]{0,1:T(8,128)} %bitcast.31, s32[3072]{0:T(1024)S(1)} %broadcast_clamp_fusion), kind=kCustom, calls=%fused_computation | custom fusion | bytes 3551232 | tf_op jit(solution)/shard_map/gather | solution.py:219
  57.2 2.0 %copy.29 = f32[144,8,384]{2,0,1:T(8,128)} copy(f32[144,8,384]{0,2,1:T(8,128)S(1)} %bitcast.35) | data formatting | bytes 3538944 | tf_op jit(solution)/shard_map/all_to_all | solution.py:220
  59.2 5.3 %all-to-all-start = ((f32[144,8,384]{2,0,1:T(8,128)}), f32[144,8,384]{2,0,1:T(8,128)S(1)}, u32[]{:S(2)}, u32[]{:S(2)}) async-start(f32[144,8,384]{2,0,1:T(8,128)} %copy.29), calls=%async_computation | async-start | bytes 3538944 | tf_op jit(solution)/shard_map/all_to_all | solution.py:220
  67.1 39.4 %all-to-all-done = f32[144,8,384]{2,0,1:T(8,128)S(1)} async-done(((f32[144,8,384]{2,0,1:T(8,128)}), f32[144,8,384]{2,0,1:T(8,128)S(1)}, u32[]{:S(2)}, u32[]{:S(2)}) %all-to-all-start) | async-done | bytes 1769504 | tf_op jit(solution)/shard_map/all_to_all | solution.py:220
  107.7 1.5 reshape.135
  109.3 1.5 copy.39
  110.8 7.3 %shard_map.86 = f32[36,32,384]{2,1,0:T(8,128)} custom-call(s32[4]{0:T(128)} %off_ref.1, f32[32,1]{1,0:T(8,128)} %copy.31.w_ref, f32[36,32,384]{2,1,0:T(8,128)} %bitcast.38), custom_call_target="tpu_custom_call" | custom-call | tf_op jit(solution)/shard_map/pallas_call | solution.py:148
  118.1 2.5 %copy.32 = f32[32,36,384]{2,1,0:T(8,128)S(1)} copy(f32[32,36,384]{2,0,1:T(8,128)} %bitcast.34) | data formatting | bytes 3538944 | tf_op jit(solution)/shard_map/transpose | solution.py:159
  122.0 3.7 %all-to-all-start.1 = ((f32[8,144,384]{2,1,0:T(8,128)}), f32[8,144,384]{2,1,0:T(8,128)S(1)}, u32[]{:S(2)}, u32[]{:S(2)}) async-start(f32[8,144,384]{2,1,0:T(8,128)} %all_to_all.29), calls=%async_computation.1 | async-start | bytes 3538944 | tf_op jit(solution)/shard_map/all_to_all | solution.py:222
  127.2 40.4 %all-to-all-done.1 = f32[8,144,384]{2,1,0:T(8,128)S(1)} async-done(((f32[8,144,384]{2,1,0:T(8,128)}), f32[8,144,384]{2,1,0:T(8,128)S(1)}, u32[]{:S(2)}, u32[]{:S(2)}) %all-to-all-start.1) | async-done | bytes 1769504 | tf_op jit(solution)/shard_map/all_to_all | solution.py:222
  169.0 2.1 %copy.34 = f32[3072,144]{1,0:T(8,128)S(1)} copy(f32[3072,144]{0,1:T(8,128)} %bitcast.39) | data formatting | bytes 3538944 | tf_op jit(solution)/shard_map/all_to_all | solution.py:222
  171.2 21.1 %scatter_fusion = f32[144,4096]{0,1:T(8,128)} fusion(f32[144,4096]{0,1:T(8,128)} %bitcast.32, s32[3072]{0:T(1024)S(1)} %bitcast.44, f32[3072,144]{1,0:T(8,128)S(1)} %copy.34), kind=kCustom, calls=%fused_computation.1 | custom fusion | flops 442368 | bytes 5320704 | tf_op jit(solution)/shard_map/scatter-add | solution.py:223
  192.3 4.8 %copy.36 = f32[144,32,128]{2,1,0:T(8,128)} copy(f32[144,32,128]{0,2,1:T(8,128)} %bitcast.33) | data formatting | bytes 4718592
  (56 shorter events, 16.7 us)
Async XLA Ops:
  0.6 1.9 copy-start.2
  2.5 3.3 %copy-start.5 = (f32[32]{0:T(128)S(1)}, f32[32]{0:T(128)}, u32[]{:S(2)}) copy-start(f32[32]{0:T(128)} %param.11) | copy-start | bytes 388
  2.5 3.3 %copy-start.6 = (f32[32]{0:T(128)S(1)}, f32[32]{0:T(128)}, u32[]{:S(2)}) copy-start(f32[32]{0:T(128)} %param.10) | copy-start | bytes 388
  2.5 3.7 %slice-start = ((s32[32,128]{1,0:T(8,128)}), s32[24,128]{1,0:T(8,128)S(1)}, s32[]{:S(2)}) async-start(s32[32,128]{1,0:T(8,128)} %param.9), calls=%async_computation.2 | async-start | bytes 24576 | tf_op jit(solution)/shard_map/slice | solution.py:218
  2.6 28.3 %collective-permute-start.1 = (f32[73,6,128]{2,1,0:T(8,128)S(1)}, f32[73,6,128]{2,1,0:T(8,128)S(1)}, u32[]{:S(2)}, u32[]{:S(2)}) collective-permute-start(f32[73,6,128]{2,1,0:T(8,128)S(1)} %get-tuple-element.24), channel_id=1, source_target_pairs={{0,1},{1,0},{2,3},{3,2},{4,5},{5,4},{6,7},{7,6},{8,9},{9,8},{10,11... | collective-permute-start | bytes 672776 | tf_op jit(solution)/shard_map/ppermute | solution.py:27
  5.7 13.6 %collective-permute-start = (f32[73,6,128]{2,1,0:T(8,128)S(1)}, f32[73,6,128]{2,1,0:T(8,128)}, u32[]{:S(2)}, u32[]{:S(2)}) collective-permute-start(f32[73,6,128]{2,1,0:T(8,128)S(1)} %get-tuple-element.25), channel_id=1, source_target_pairs={{0,1},{1,0},{2,3},{3,2},{4,5},{5,4},{6,7},{7,6},{8,9},{9,8},{10,11... | collective-permute-start | bytes 672776 | tf_op jit(solution)/shard_map/ppermute | solution.py:27
  59.2 5.3 %copy-start.3 = (s32[4]{0:T(128)S(1)}, s32[4]{0:T(128)}, u32[]{:S(2)}) copy-start(s32[4]{0:T(128)} %off_ref.1) | copy-start | bytes 52
  59.2 5.9 %copy-start.4 = (f32[32]{0:T(128)S(1)}, f32[32]{0:T(128)}, u32[]{:S(2)}) copy-start(f32[32]{0:T(128)} %param.12) | copy-start | bytes 388
  59.2 47.3 %all-to-all-start = ((f32[144,8,384]{2,0,1:T(8,128)}), f32[144,8,384]{2,0,1:T(8,128)S(1)}, u32[]{:S(2)}, u32[]{:S(2)}) async-start(f32[144,8,384]{2,0,1:T(8,128)} %copy.29), calls=%async_computation | async-start | bytes 3538944 | tf_op jit(solution)/shard_map/all_to_all | solution.py:220
  106.5 1.2 copy-start.1
  122.0 3.7 %copy-start = (f32[36,32,384]{2,1,0:T(8,128)S(1)}, f32[36,32,384]{2,1,0:T(8,128)}, u32[]{:S(2)}) copy-start(f32[36,32,384]{2,1,0:T(8,128)} %shard_map.86) | copy-start | bytes 5308420
  122.0 45.7 %all-to-all-start.1 = ((f32[8,144,384]{2,1,0:T(8,128)}), f32[8,144,384]{2,1,0:T(8,128)S(1)}, u32[]{:S(2)}, u32[]{:S(2)}) async-start(f32[8,144,384]{2,1,0:T(8,128)} %all_to_all.29), calls=%async_computation.1 | async-start | bytes 3538944 | tf_op jit(solution)/shard_map/all_to_all | solution.py:222

commit v12 on v7

--- a/solution.py
+++ b/solution.py
@@ -35,10 +35,6 @@
     return lax.slice_in_dim(values, offset, offset + length, axis=along)
 
 
-def pad_along(values):
-    return jnp.pad(values, ((0, 0), (0, 0), (2, 2)))
-
-
 def quickest(padded, courant, along):
     length = padded.shape[along] - 4
     before_cell = cut_slab(padded, 0, length + 1, along)
@@ -59,6 +55,42 @@
     return cut_slab(padded, 2, length, along) - (
         cut_slab(face_flux, 1, length, along) - cut_slab(face_flux, 0, length, along)
     )
+
+
+def shifted(values, offset, along):
+    config = [(0, 0, 0)] * values.ndim
+    config[along] = (offset, -offset, 0)
+    return lax.pad(values, jnp.zeros((), values.dtype), config)
+
+
+def face_flux(before_cell, left_cell, right_cell, after_cell, courant):
+    curvature = jnp.where(
+        courant > 0,
+        right_cell - 2.0 * left_cell + before_cell,
+        after_cell - 2.0 * right_cell + left_cell,
+    )
+    face_value = (
+        0.5 * (left_cell + right_cell)
+        - 0.5 * courant * (right_cell - left_cell)
+        - (1.0 - courant * courant) / 6.0 * curvature
+    )
+    return courant * face_value
+
+
+def quickest_x(energy, courant):
+    back_two = shifted(energy, 2, 2)
+    back_one = shifted(energy, 1, 2)
+    ahead_one = shifted(energy, -1, 2)
+    ahead_two = shifted(energy, -2, 2)
+    right_face = face_flux(back_one, energy, ahead_one, ahead_two, courant)
+    left_face = face_flux(back_two, back_one, energy, ahead_one, courant)
+    return energy - (right_face - left_face)
+
+
+def laplace_x(centre):
+    near_sum = shifted(centre, 1, 2) + shifted(centre, -1, 2) - 2.0 * centre
+    far_sum = shifted(centre, 2, 2) + shifted(centre, -2, 2) - 2.0 * centre
+    return 4.0 / 3.0 * near_sum - 1.0 / 12.0 * far_sum
 
 
 def laplace(padded, along):
@@ -136,7 +168,7 @@
     for substep in range(SUBSTEPS):
         energy = quickest(energy, courant_y, 1)
         ext_mask = cut_slab(ext_mask, 2, ext_mask.shape[0] - 4, 0)
-        energy = quickest(pad_along(energy), courant_x, 2) * ext_mask
+        energy = quickest_x(energy, courant_x) * ext_mask
     return energy
 
 
@@ -164,7 +196,7 @@
         with_rim = propagate(window[1:], window[0], courant_y, courant_x)
         centre = cut_slab(with_rim, 2, rows, 1)
         return (
-            centre + spread_y * laplace(with_rim, 1) + spread_x * laplace(pad_along(centre), 2)
+            centre + spread_y * laplace(with_rim, 1) + spread_x * laplace_x(centre)
         ) * cut_slab(window[0], width, rows, 0)
 
     low, high = border_rows(stacked, "lat", 1, width)

time: 205 us -> 200 us (0.976)
  other arithmetic: 63.4 us -> 58.6 us
    mul x8 -> x4, other arithmetic: 25.6 us -> 8.79 us  [quickest(): face_flux = courant * face_value]
    mul x11 -> x10, other arithmetic: 7.16 us -> 19 us  [the longest x6 14.4 us: propagate(): energy = quickest_x(energy, courant_x) * ext_mask]
  transfers between devices with their start and end apart: 3 -> 3, of which waited for: 2 -> 2; matrix products, arithmetic and copies ran while one was open for 13% -> 12% of each run, Pallas kernels for 0% -> 0%
where the time goes in v12:
time: 200 us; the launch traced here: 199 us
  waiting for transfers between devices  79.7 us (40%)
  other arithmetic  58.6 us (29%)
  local copies, waits for them, and re-layouts  40.9 us (20%)
  starting transfers between devices  11.7 us (6%)
  Pallas kernels  7.25 us (4%)
    all_to_all x1, waiting for transfers between devices, on_device(): lax.all_to_all(source_terms, 'spec', split_axis=0, concat_axis=1, tiled=T...  40.4 us
    all_to_all x1, waiting for transfers between devices, on_device(): lax.all_to_all(columns, 'spec', split_axis=1, concat_axis=0, tiled=True)  39.3 us
    scatter-add x1, other arithmetic, on_device(): flat_cells.at[:, sea_cells]  21.1 us
    mul x6, other arithmetic, propagate(): energy = quickest_x(energy, courant_x) * ext_mask  14.4 us
    gather x1, local copies, waits for them, and re-layouts, on_device(): flat_cells.at[:, sea_cells]  12 us
    mul x4, other arithmetic, quickest(): face_flux = courant * face_value  8.79 us
    pallas_call x1, Pallas kernels, interact_pallas(): pl.pallas_call(interact_kernel, out_shape=jax.ShapeDtypeStruct((NDIR, NFR...  7.25 us
    unnamed x27, local copies, waits for them, and re-layouts  6.68 us
  transfers between devices with their start and end apart: 3, of which 2 were waited for; matrix products, arithmetic and copies ran while one was open for 12% of the time, Pallas kernels for 0%

profile of v12, /device:TPU:0, one launch (start us, length us, event | category | flops | bytes accessed | tf_op | source)
XLA Modules:
  0.0 199.1 jit_solution(7122725190604897329)
XLA Ops:
  3.0 3.0 %collective-permute-start = (f32[145,6,128]{2,0,1:T(8,128)}, f32[145,6,128]{2,0,1:T(8,128)}, u32[]{:S(2)}, u32[]{:S(2)}) collective-permute-start(f32[145,6,128]{2,0,1:T(8,128)} %copy.52), channel_id=1, source_target_pairs={{0,1},{1,0},{2,3},{3,2},{4,5},{5,4},{6,7},{7,6},{8,9},{9,8},{10,11... | collective-permute-start | bytes 1336328 | tf_op jit(solution)/shard_map/ppermute | solution.py:27
  10.9 2.2 %subtract_multiply_fusion = f32[144,29,128]{2,1,0:T(8,128)S(1)} fusion(f32[144,32,128]{2,1,0:T(8,128)S(1)} %copy-done, f32[144]{0:T(256)S(1)} %get-tuple-element.46, f32[144]{0:T(256)S(1)} %get-tuple-element.47, f32[144]{0:T(256)S(1)} %get-tuple-element.37, pred[144]{0:T(512)(128)(4,1)S(1)} %get-tuple-element.36), kind=kLoop, calls=%fused_computation.61 | loop fusion | flops 8017920 | bytes 10692432 | tf_op jit(solution)/shard_map/mul | solution.py:54
  13.9 3.8 %fusion.8 = f32[144,28,128]{2,1,0:T(8,128)S(1)} fusion(f32[144,28,128]{2,1,0:T(8,128)S(1)} %fusion.19, f32[28,128]{1,0:T(8,128)S(1)} %copy-done.7, f32[144]{0:T(256)S(1)} %get-tuple-element.35, f32[144]{0:T(256)S(1)} %get-tuple-element.34, f32[144]{0:T(256)S(1)} %get-tuple-element.17, pred[144]{0:T(512)(128)(4,1)S(1)} %get-tuple-element.16), kind=kLoop, calls=%fused_computation.37 | loop fusion | flops 15482880 | bytes 4144976 | tf_op jit(solution)/shard_map/mul | solution.py:171
  17.7 2.2 %fusion.18 = f32[144,25,128]{2,1,0:T(8,128)S(1)} fusion(f32[144,28,128]{2,1,0:T(8,128)S(1)} %fusion.8, f32[144]{0:T(256)S(1)} %get-tuple-element.46, f32[144]{0:T(256)S(1)} %get-tuple-element.47, f32[144]{0:T(256)S(1)} %get-tuple-element.37, pred[144]{0:T(512)(128)(4,1)S(1)} %get-tuple-element.36), kind=kLoop, calls=%fused_computation.48 | loop fusion | flops 6912000 | bytes 9217872 | tf_op jit(solution)/shard_map/mul | solution.py:54
  20.6 3.0 %fusion.29 = f32[144,24,128]{2,1,0:T(8,128)S(1)} fusion(f32[144,24,128]{2,1,0:T(8,128)S(1)} %fusion.51, f32[24,128]{1,0:T(8,128)S(1)} %copy-done.10, f32[144]{0:T(256)S(1)} %get-tuple-element.35, f32[144]{0:T(256)S(1)} %get-tuple-element.34, f32[144]{0:T(256)S(1)} %get-tuple-element.17, pred[144]{0:T(512)(128)(4,1)S(1)} %get-tuple-element.16), kind=kLoop, calls=%fused_computation.83 | loop fusion | flops 13271040 | bytes 3553104 | tf_op jit(solution)/shard_map/mul | solution.py:171
  24.3 2.6 %fusion.41 = f32[144,20,128]{2,1,0:T(8,128)S(1)} fusion(f32[144,20,128]{2,1,0:T(8,128)S(1)} %slice.414, f32[144,24,128]{2,1,0:T(8,128)S(1)} %fusion.29, f32[20,128]{1,0:T(8,128)S(1)} %copy-done.9, f32[144]{0:T(256)S(1)} %get-tuple-element.33, f32[144]{0:T(256)S(1)} %get-tuple-element.32), kind=kLoop, calls=%fused_computation.95 | loop fusion | flops 7372800 | bytes 8858752 | tf_op jit(solution)/shard_map/mul | solution.py:198
  28.4 2.3 %fusion.118 = (f32[144,15,128]{2,1,0:T(8,128)S(1)}, f32[144,15,128]{2,1,0:T(8,128)S(1)}) fusion(f32[145,12,128]{2,1,0:T(8,128)S(1)} %fusion.52, f32[145,6,128]{2,1,0:T(8,128)S(1)} %get-tuple-element.20, f32[144]{0:T(256)S(1)} %get-tuple-element.46, f32[144]{0:T(256)S(1)} %get-tuple-element.47, f32[144]{0:T(256)S(1)} %get-tuple-element.37, ...), kind=kLoop, calls=%fused_computation.177 | loop fusion | flops 9400320 | bytes 7973712 | tf_op jit(solution)/shard_map/mul | solution.py:54
  31.4 3.7 %fusion.61 = (f32[144,14,128]{2,1,0:T(8,128)S(1)}, f32[144,14,128]{2,1,0:T(8,128)S(1)}) fusion(f32[144,14,128]{2,1,0:T(8,128)S(1)} %fusion.110, f32[14,128]{1,0:T(8,128)S(1)} %get-tuple-element.45, f32[144]{0:T(256)S(1)} %get-tuple-element.35, f32[144]{0:T(256)S(1)} %get-tuple-element.34, f32[144]{0:T(256)S(1)} %get-tuple-element.17, ...), kind=kLoop, calls=%fused_computation.120 | loop fusion | flops 15482880 | bytes 4144976 | tf_op jit(solution)/shard_map/mul | solution.py:171
  35.1 2.1 %fusion.139 = (f32[144,11,128]{2,1,0:T(8,128)S(1)}, f32[144,11,128]{2,1,0:T(8,128)S(1)}) fusion(f32[144,14,128]{2,1,0:T(8,128)S(1)} %get-tuple-element.28, f32[144]{0:T(256)S(1)} %get-tuple-element.46, f32[144]{0:T(256)S(1)} %get-tuple-element.47, f32[144]{0:T(256)S(1)} %get-tuple-element.37, pred[144]{0:T(512)(128)(4,1)S(1)} %get-tuple-element.36, ...), kind=kLoop, calls=%fused_computation.206 | loop fusion | flops 6082560 | bytes 8111952 | tf_op jit(solution)/shard_map/mul | solution.py:54
  37.8 3.9 %fusion.75 = (f32[144,10,128]{2,1,0:T(8,128)S(1)}, f32[144,10,128]{2,1,0:T(8,128)S(1)}) fusion(f32[144,10,128]{2,1,0:T(8,128)S(1)} %fusion.134, f32[10,128]{1,0:T(8,128)S(1)} %get-tuple-element.43, f32[144]{0:T(256)S(1)} %get-tuple-element.35, f32[144]{0:T(256)S(1)} %get-tuple-element.34, f32[144]{0:T(256)S(1)} %get-tuple-element.17, ...), kind=kLoop, calls=%fused_computation.134 | loop fusion | flops 11059200 | bytes 2961232 | tf_op jit(solution)/shard_map/mul | solution.py:171
  44.2 3.3 %copy.55 = f32[144,32,128]{0,2,1:T(8,128)} copy(f32[144,32,128]{2,1,0:T(8,128)S(1)} %pad_maximum_fusion) | data formatting | bytes 4718592 | tf_op jit(solution)/shard_map/concatenate | solution.py:207
  47.4 12.0 %gather_fusion = f32[3072,144]{1,0:T(8,128)S(1)} fusion(f32[144,4096]{0,1:T(8,128)} %bitcast.35, s32[3072]{0:T(1024)S(1)} %copy-done.8), kind=kCustom, calls=%fused_computation | custom fusion | bytes 3551232 | tf_op jit(solution)/shard_map/gather | solution.py:212
  59.4 2.0 %copy.56 = f32[144,8,384]{2,0,1:T(8,128)} copy(f32[144,8,384]{0,2,1:T(8,128)S(1)} %bitcast.39) | data formatting | bytes 3538944 | tf_op jit(solution)/shard_map/all_to_all | solution.py:213
  61.5 5.0 %all-to-all-start = ((f32[144,8,384]{2,0,1:T(8,128)}), f32[144,8,384]{2,0,1:T(8,128)S(1)}, u32[]{:S(2)}, u32[]{:S(2)}) async-start(f32[144,8,384]{2,0,1:T(8,128)} %copy.56), calls=%async_computation | async-start | bytes 3538944 | tf_op jit(solution)/shard_map/all_to_all | solution.py:213
  69.2 39.3 %all-to-all-done = f32[144,8,384]{2,0,1:T(8,128)S(1)} async-done(((f32[144,8,384]{2,0,1:T(8,128)}), f32[144,8,384]{2,0,1:T(8,128)S(1)}, u32[]{:S(2)}, u32[]{:S(2)}) %all-to-all-start) | async-done | bytes 1769504 | tf_op jit(solution)/shard_map/all_to_all | solution.py:213
  109.7 1.5 reshape.178
  111.2 1.5 copy.68
  112.8 7.3 %shard_map.86 = f32[36,32,384]{2,1,0:T(8,128)} custom-call(s32[4]{0:T(128)} %off_ref.1, f32[32,1]{1,0:T(8,128)} %copy.58.w_ref, f32[36,32,384]{2,1,0:T(8,128)} %bitcast.42), custom_call_target="tpu_custom_call" | custom-call | tf_op jit(solution)/shard_map/pallas_call | solution.py:148
  120.0 2.5 %copy.59 = f32[32,36,384]{2,1,0:T(8,128)S(1)} copy(f32[32,36,384]{2,0,1:T(8,128)} %bitcast.38) | data formatting | bytes 3538944 | tf_op jit(solution)/shard_map/transpose | solution.py:159
  123.9 3.7 %all-to-all-start.1 = ((f32[8,144,384]{2,1,0:T(8,128)}), f32[8,144,384]{2,1,0:T(8,128)S(1)}, u32[]{:S(2)}, u32[]{:S(2)}) async-start(f32[8,144,384]{2,1,0:T(8,128)} %all_to_all.29), calls=%async_computation.1 | async-start | bytes 3538944 | tf_op jit(solution)/shard_map/all_to_all | solution.py:215
  129.2 40.4 %all-to-all-done.1 = f32[8,144,384]{2,1,0:T(8,128)S(1)} async-done(((f32[8,144,384]{2,1,0:T(8,128)}), f32[8,144,384]{2,1,0:T(8,128)S(1)}, u32[]{:S(2)}, u32[]{:S(2)}) %all-to-all-start.1) | async-done | bytes 1769504 | tf_op jit(solution)/shard_map/all_to_all | solution.py:215
  171.0 2.1 %copy.61 = f32[3072,144]{1,0:T(8,128)S(1)} copy(f32[3072,144]{0,1:T(8,128)} %bitcast.43) | data formatting | bytes 3538944 | tf_op jit(solution)/shard_map/all_to_all | solution.py:215
  173.1 21.1 %scatter_fusion = f32[144,4096]{0,1:T(8,128)} fusion(f32[144,4096]{0,1:T(8,128)} %bitcast.36, s32[3072]{0:T(1024)S(1)} %bitcast.51, f32[3072,144]{1,0:T(8,128)S(1)} %copy.61), kind=kCustom, calls=%fused_computation.1 | custom fusion | flops 442368 | bytes 5320704 | tf_op jit(solution)/shard_map/scatter-add | solution.py:216
  194.3 4.8 %copy.63 = f32[144,32,128]{2,1,0:T(8,128)} copy(f32[144,32,128]{0,2,1:T(8,128)} %bitcast.37) | data formatting | bytes 4718592
  (66 shorter events, 22.7 us)
Async XLA Ops:
  0.6 5.3 %copy-start.3 = (f32[32,128]{1,0:T(8,128)S(1)}, f32[32,128]{1,0:T(8,128)}, u32[]{:S(2)}) copy-start(f32[32,128]{1,0:T(8,128)} %param.8) | copy-start | bytes 49156
  0.6 7.1 %copy-start = (f32[144,32,128]{2,1,0:T(8,128)S(1)}, f32[144,32,128]{2,1,0:T(8,128)}, u32[]{:S(2)}) copy-start(f32[144,32,128]{2,1,0:T(8,128)} %param.7) | copy-start | bytes 7077892
  3.0 23.9 %collective-permute-start = (f32[145,6,128]{2,0,1:T(8,128)}, f32[145,6,128]{2,0,1:T(8,128)}, u32[]{:S(2)}, u32[]{:S(2)}) collective-permute-start(f32[145,6,128]{2,0,1:T(8,128)} %copy.52), channel_id=1, source_target_pairs={{0,1},{1,0},{2,3},{3,2},{4,5},{5,4},{6,7},{7,6},{8,9},{9,8},{10,11... | collective-permute-start | bytes 1336328 | tf_op jit(solution)/shard_map/ppermute | solution.py:27
  10.2 0.6 copy-start.5
  13.0 0.8 copy-start.7
  19.9 0.7 copy-start.10
  23.6 0.7 copy-start.9
  26.9 1.2 copy-start.4
  44.2 3.3 %copy-start.8 = (s32[3072]{0:T(1024)S(1)}, s32[3072]{0:T(1024)}, u32[]{:S(2)}) copy-start(s32[3072]{0:T(1024)} %broadcast_clamp_fusion) | copy-start | bytes 36868
  61.5 5.0 %copy-start.11 = (s32[4]{0:T(128)S(1)}, s32[4]{0:T(128)}, u32[]{:S(2)}) copy-start(s32[4]{0:T(128)} %off_ref.1) | copy-start | bytes 52
  61.5 5.7 %copy-start.12 = (f32[32]{0:T(128)S(1)}, f32[32]{0:T(128)}, u32[]{:S(2)}) copy-start(f32[32]{0:T(128)} %param.12) | copy-start | bytes 388
  61.5 47.0 %all-to-all-start = ((f32[144,8,384]{2,0,1:T(8,128)}), f32[144,8,384]{2,0,1:T(8,128)S(1)}, u32[]{:S(2)}, u32[]{:S(2)}) async-start(f32[144,8,384]{2,0,1:T(8,128)} %copy.56), calls=%async_computation | async-start | bytes 3538944 | tf_op jit(solution)/shard_map/all_to_all | solution.py:213
  108.5 1.2 copy-start.2
  123.9 3.7 %copy-start.1 = (f32[36,32,384]{2,1,0:T(8,128)S(1)}, f32[36,32,384]{2,1,0:T(8,128)}, u32[]{:S(2)}) copy-start(f32[36,32,384]{2,1,0:T(8,128)} %shard_map.86) | copy-start | bytes 5308420
  123.9 45.7 %all-to-all-start.1 = ((f32[8,144,384]{2,1,0:T(8,128)}), f32[8,144,384]{2,1,0:T(8,128)S(1)}, u32[]{:S(2)}, u32[]{:S(2)}) async-start(f32[8,144,384]{2,1,0:T(8,128)} %all_to_all.29), calls=%async_computation.1 | async-start | bytes 3538944 | tf_op jit(solution)/shard_map/all_to_all | solution.py:215
  171.0 2.2 %copy-start.6 = (s32[3072,1]{0,1:T(1,128)S(1)}, s32[3072,1]{0,1:T(1,128)}, u32[]{:S(2)}) copy-start(s32[3072,1]{0,1:T(1,128)} %copy-done.5) | copy-start | bytes 36868

commit v13 on v8

--- a/solution.py
+++ b/solution.py
@@ -208,10 +208,13 @@
     gathered = lax.all_to_all(columns, "spec", split_axis=1, concat_axis=0, tiled=True)
     source_terms = interact_pallas(gathered, coupling, quad_offsets)
     returned = lax.all_to_all(source_terms, "spec", split_axis=0, concat_axis=1, tiled=True)
-    new_cells = flat_cells.at[:, sea_cells].add(
-        returned, mode="promise_in_bounds", unique_indices=True
-    )
-    updated = new_cells.reshape(smoothed.shape)
+    order = sea_order.reshape(-1)
+    slot_of_cell = jnp.zeros_like(order).at[order].set(
+        lax.iota(jnp.int32, order.shape[0]), mode="promise_in_bounds", unique_indices=True
+    )
+    slot_terms = jnp.pad(returned, ((0, 0), (0, order.shape[0] - SEA_MAX)))
+    cell_terms = slot_terms.at[:, slot_of_cell].get(mode="promise_in_bounds", unique_indices=True)
+    updated = (flat_cells + cell_terms).reshape(smoothed.shape)
     return (updated, source_terms.astype(jnp.bfloat16)[None])
 
 

time: 196 us -> 207 us (1.056)
  local copies, waits for them, and re-layouts: 39.7 us -> 82.7 us
  waiting for transfers between devices: 89.9 us -> 73.1 us
  other arithmetic: 45.3 us -> 29.3 us
    gather x0 -> x2, local copies, waits for them, and re-layouts: none -> 23.2 us  [on_device(): slot_terms.at[:, slot_of_cell]]
    scatter-add x1 -> x0, other arithmetic: 21.1 us -> none  [on_device(): flat_cells.at[:, sea_cells]]
    all_to_all x1, waiting for transfers between devices: 40.2 us -> 23.3 us  [on_device(): lax.all_to_all(source_terms, 'spec', split_axis=0, concat_axis=1, tiled=T...]
    scatter x0 -> x1, local copies, waits for them, and re-layouts: none -> 15.7 us  [on_device(): jnp.zeros_like(order).at[order]]
    unnamed x17 -> x14, local copies, waits for them, and re-layouts: 6.06 us -> 0.03 us
    pad x0 -> x1, local copies, waits for them, and re-layouts: none -> 4.14 us  [on_device(): slot_terms = jnp.pad(returned, ((0, 0), (0, order.shape[0] - SEA_MAX)))]
    add x0 -> x1, other arithmetic: none -> 3.61 us  [on_device(): updated = (flat_cells + cell_terms).reshape(smoothed.shape)]
    reshape x2, local copies, waits for them, and re-layouts: 3.05 us -> 5.68 us  [interact_pallas(): spectra = columns.reshape(NFREQ, NDIR, points).transpose(1, 0, 2)]
  transfers between devices with their start and end apart: 3 -> 3, of which waited for: 3 -> 3; matrix products, arithmetic and copies ran while one was open for 2% -> 10% of each run, Pallas kernels for 0% -> 0%
where the time goes in v13:
time: 207 us; the launch traced here: 206 us
  local copies, waits for them, and re-layouts  82.7 us (40%)
  waiting for transfers between devices  73.1 us (35%)
  other arithmetic  29.3 us (14%)
  starting transfers between devices  12.6 us (6%)
  Pallas kernels  7.24 us (3%)
    all_to_all x1, waiting for transfers between devices, on_device(): lax.all_to_all(columns, 'spec', split_axis=1, concat_axis=0, tiled=True)  39.5 us
    all_to_all x1, waiting for transfers between devices, on_device(): lax.all_to_all(source_terms, 'spec', split_axis=0, concat_axis=1, tiled=T...  23.3 us
    gather x2, local copies, waits for them, and re-layouts, on_device(): slot_terms.at[:, slot_of_cell]  23.2 us
    scatter x1, local copies, waits for them, and re-layouts, on_device(): jnp.zeros_like(order).at[order]  15.7 us
    gather x1, local copies, waits for them, and re-layouts, on_device(): flat_cells.at[:, sea_cells]  14.6 us
    ppermute x1, waiting for transfers between devices, extended_2(): lax.ppermute(jnp.where(first, bottom, top), axis, [(0, 1), (1, 0)])  10.4 us
    mul x4, other arithmetic, propagate(): energy = quickest_x(energy, courant_x) * ext_mask  9.36 us
    pallas_call x1, Pallas kernels, interact_pallas(): pl.pallas_call(interact_kernel, out_shape=jax.ShapeDtypeStruct((NDIR, NFR...  7.24 us
  transfers between devices with their start and end apart: 3, of which 3 were waited for; matrix products, arithmetic and copies ran while one was open for 10% of the time, Pallas kernels for 0%

profile of v13, /device:TPU:0, one launch (start us, length us, event | category | flops | bytes accessed | tf_op | source)
XLA Modules:
  0.0 205.9 jit_solution(12622731387894040117)
XLA Ops:
  2.3 3.0 %collective-permute-start = (f32[145,6,128]{2,0,1:T(8,128)S(1)}, f32[145,6,128]{2,0,1:T(8,128)S(1)}, u32[]{:S(2)}, u32[]{:S(2)}) collective-permute-start(f32[145,6,128]{2,0,1:T(8,128)S(1)} %copy.41), channel_id=1, source_target_pairs={{0,1},{1,0},{2,3},{3,2},{4,5},{5,4},{6,7},{7,6},{8,9},{9,8},{10,11... | collective-permute-start | bytes 1336328 | tf_op jit(solution)/shard_map/ppermute | solution.py:28
  5.6 10.4 %collective-permute-done = f32[145,6,128]{2,0,1:T(8,128)S(1)} collective-permute-done((f32[145,6,128]{2,0,1:T(8,128)S(1)}, f32[145,6,128]{2,0,1:T(8,128)S(1)}, u32[]{:S(2)}, u32[]{:S(2)}) %collective-permute-start) | collective-permute-done | bytes 445472 | tf_op jit(solution)/shard_map/ppermute | solution.py:28
  16.7 2.8 %fusion.4 = f32[144,41,128]{2,1,0:T(8,128)S(1)} fusion(f32[145,44,128]{2,1,0:T(8,128)S(1)} %pad_maximum_fusion, f32[144]{0:T(256)S(1)} %get-tuple-element.22, f32[144]{0:T(256)S(1)} %get-tuple-element.23, f32[144]{0:T(256)S(1)} %get-tuple-element.17, pred[144]{0:T(512)(128)(4,1)S(1)} %get-tuple-element.16), kind=kLoop, calls=%fused_computation.21 | loop fusion | flops 11335680 | bytes 15116112 | tf_op jit(solution)/shard_map/mul | solution.py:60
  20.6 4.7 %fusion.13 = f32[144,40,128]{2,1,0:T(8,128)S(1)} fusion(f32[144,40,128]{2,1,0:T(8,128)S(1)} %fusion.39, f32[40,128]{1,0:T(8,128)S(1)} %maximum_bitcast_fusion.1, f32[144]{0:T(256)S(1)} %get-tuple-element.15, f32[144]{0:T(256)S(1)} %get-tuple-element.14, f32[144]{0:T(256)S(1)} %get-tuple-element.7, pred[144]{0:T(512)(128)(4,1)S(1)} %get-tuple-element.6), kind=kLoop, calls=%fused_computation.31 | loop fusion | flops 22118400 | bytes 5920592 | tf_op jit(solution)/shard_map/mul | solution.py:177
  25.3 2.6 %fusion.38 = f32[144,37,128]{2,1,0:T(8,128)S(1)} fusion(f32[144,40,128]{2,1,0:T(8,128)S(1)} %fusion.13, f32[144]{0:T(256)S(1)} %get-tuple-element.22, f32[144]{0:T(256)S(1)} %get-tuple-element.23, f32[144]{0:T(256)S(1)} %get-tuple-element.17, pred[144]{0:T(512)(128)(4,1)S(1)} %get-tuple-element.16), kind=kLoop, calls=%fused_computation.58 | loop fusion | flops 10229760 | bytes 13641552 | tf_op jit(solution)/shard_map/mul | solution.py:60
  28.5 4.7 %fusion.27 = f32[144,36,128]{2,1,0:T(8,128)S(1)} fusion(f32[144,36,128]{2,1,0:T(8,128)S(1)} %fusion.33, f32[36,128]{1,0:T(8,128)S(1)} %maximum_bitcast_fusion, f32[144]{0:T(256)S(1)} %get-tuple-element.15, f32[144]{0:T(256)S(1)} %get-tuple-element.14, f32[144]{0:T(256)S(1)} %get-tuple-element.7, pred[144]{0:T(512)(128)(4,1)S(1)} %get-tuple-element.6), kind=kLoop, calls=%fused_computation.45 | loop fusion | flops 19906560 | bytes 5328720 | tf_op jit(solution)/shard_map/mul | solution.py:177
  33.6 3.9 %fusion.46 = f32[144,32,128]{2,1,0:T(8,128)S(1)} fusion(f32[144,32,128]{2,1,0:T(8,128)S(1)} %slice.150, f32[144,36,128]{2,1,0:T(8,128)S(1)} %fusion.27, f32[32,128]{1,0:T(8,128)S(1)} %copy-done.1, f32[144]{0:T(256)S(1)} %get-tuple-element.13, f32[144]{0:T(256)S(1)} %get-tuple-element.12), kind=kLoop, calls=%fused_computation.68 | loop fusion | flops 11796480 | bytes 14173312 | tf_op jit(solution)/shard_map/mul | solution.py:202
  37.5 3.3 %copy.44 = f32[144,32,128]{0,2,1:T(8,128)} copy(f32[144,32,128]{2,1,0:T(8,128)S(1)} %fusion.46) | data formatting | bytes 4718592 | tf_op jit(solution)/shard_map/mul | solution.py:202
  40.8 14.6 %gather_fusion = f32[3072,144]{1,0:T(8,128)} fusion(f32[144,4096]{0,1:T(8,128)} %bitcast.29, s32[3072]{0:T(1024)S(1)} %broadcast_clamp_fusion), kind=kCustom, calls=%fused_computation | custom fusion | bytes 3551232 | tf_op jit(solution)/shard_map/gather | solution.py:207
  55.4 3.2 %copy.45 = f32[144,8,384]{2,0,1:T(8,128)} copy(f32[144,8,384]{0,2,1:T(8,128)} %bitcast.33) | data formatting | bytes 3538944 | tf_op jit(solution)/shard_map/all_to_all | solution.py:208
  58.6 5.3 %all-to-all-start = ((f32[144,8,384]{2,0,1:T(8,128)}), f32[144,8,384]{2,0,1:T(8,128)}, u32[]{:S(2)}, u32[]{:S(2)}) async-start(f32[144,8,384]{2,0,1:T(8,128)} %copy.45), calls=%async_computation | async-start | bytes 3538944 | tf_op jit(solution)/shard_map/all_to_all | solution.py:208
  66.5 39.5 %all-to-all-done = f32[144,8,384]{2,0,1:T(8,128)} async-done(((f32[144,8,384]{2,0,1:T(8,128)}), f32[144,8,384]{2,0,1:T(8,128)}, u32[]{:S(2)}, u32[]{:S(2)}) %all-to-all-start) | async-done | bytes 1769504 | tf_op jit(solution)/shard_map/all_to_all | solution.py:208
  108.6 3.1 %copy.55 = f32[32,36,384]{2,0,1:T(8,128)} copy(f32[32,36,384]{2,1,0:T(8,128)} %reshape.198) | data formatting | bytes 3538944 | tf_op jit(solution)/shard_map/reshape | solution.py:150
  111.7 7.2 %shard_map.86 = f32[36,32,384]{2,1,0:T(8,128)} custom-call(s32[4]{0:T(128)} %off_ref.1, f32[32,1]{1,0:T(8,128)} %copy.47.w_ref, f32[36,32,384]{2,1,0:T(8,128)} %bitcast.34), custom_call_target="tpu_custom_call" | custom-call | tf_op jit(solution)/shard_map/pallas_call | solution.py:154
  118.9 3.8 %copy.48 = f32[32,36,384]{2,1,0:T(8,128)} copy(f32[32,36,384]{2,0,1:T(8,128)} %bitcast.30) | data formatting | bytes 3538944 | tf_op jit(solution)/shard_map/transpose | solution.py:165
  122.7 2.6 %all_to_all.29 = f32[8,144,384]{2,1,0:T(8,128)} reshape(f32[32,36,384]{2,1,0:T(8,128)} %copy.48) | data formatting | bytes 3538944 | tf_op jit(solution)/shard_map/all_to_all | solution.py:210
  125.3 4.3 %all-to-all-start.1 = ((f32[8,144,384]{2,1,0:T(8,128)}), f32[8,144,384]{2,1,0:T(8,128)}, u32[]{:S(2)}, u32[]{:S(2)}) async-start(f32[8,144,384]{2,1,0:T(8,128)} %all_to_all.29), calls=%async_computation.1 | async-start | bytes 3538944 | tf_op jit(solution)/shard_map/all_to_all | solution.py:210
  129.7 15.7 %scatter_custom_fusion = s32[4096]{0:T(1024)S(1)} fusion(s32[4096]{0:T(1024)S(1)} %bitcast.42, s32[4096]{0:T(1024)S(1)} %iota.41, s32[]{:T(128)} %constant.20.clone.1), kind=kCustom, calls=%fused_computation.95 | custom fusion | bytes 16388 | tf_op jit(solution)/shard_map/scatter | solution.py:212
  148.4 23.3 %all-to-all-done.1 = f32[8,144,384]{2,1,0:T(8,128)} async-done(((f32[8,144,384]{2,1,0:T(8,128)}), f32[8,144,384]{2,1,0:T(8,128)}, u32[]{:S(2)}, u32[]{:S(2)}) %all-to-all-start.1) | async-done | bytes 1769504 | tf_op jit(solution)/shard_map/all_to_all | solution.py:210
  171.6 3.3 %copy.49 = f32[144,8,384]{0,2,1:T(8,128)} copy(f32[144,8,384]{2,0,1:T(8,128)} %bitcast.14) | data formatting | bytes 3538944 | tf_op jit(solution)/shard_map/all_to_all | solution.py:210
  175.0 4.1 %pad.84 = f32[144,4096]{0,1:T(8,128)} pad(f32[144,3072]{0,1:T(8,128)} %bitcast.31, f32[]{:T(128)} %constant.21.clone.1), padding=0_0x0_1024 | pad | bytes 4128772 | tf_op jit(solution)/shard_map/jit(_pad)/pad | solution.py:215
  179.1 18.3 %gather_fusion.1 = f32[4096,144]{1,0:T(8,128)} fusion(f32[144,4096]{0,1:T(8,128)} %pad.84, s32[4096]{0:T(1024)S(1)} %fusion.57), kind=kCustom, calls=%fused_computation.1 | custom fusion | bytes 4734976 | tf_op jit(solution)/shard_map/gather | solution.py:216
  197.4 4.8 %copy.50 = f32[144,32,128]{2,1,0:T(8,128)} copy(f32[144,32,128]{0,2,1:T(8,128)} %bitcast.32) | data formatting | bytes 4718592 | tf_op jit(solution)/shard_map/gather | solution.py:216
  202.3 3.6 %add.299 = f32[144,32,128]{2,1,0:T(8,128)} add(f32[144,32,128]{2,1,0:T(8,128)S(1)} %fusion.46, f32[144,32,128]{2,1,0:T(8,128)} %copy.50) | non-fusion elementwise | flops 589824 | bytes 7077888 | tf_op jit(solution)/shard_map/add | solution.py:217
  (42 shorter events, 12.8 us)
Async XLA Ops:
  0.6 15.5 %copy-start = (f32[144,32,128]{2,1,0:T(8,128)S(1)}, f32[144,32,128]{2,1,0:T(8,128)}, u32[]{:S(2)}) copy-start(f32[144,32,128]{2,1,0:T(8,128)} %param.7) | copy-start | bytes 7077892
  0.6 15.5 %copy-start.1 = (f32[32,128]{1,0:T(8,128)S(1)}, f32[32,128]{1,0:T(8,128)}, u32[]{:S(2)}) copy-start(f32[32,128]{1,0:T(8,128)} %param.8) | copy-start | bytes 49156
  0.7 4.7 %copy-start.5 = (f32[32]{0:T(128)S(1)}, f32[32]{0:T(128)}, u32[]{:S(2)}) copy-start(f32[32]{0:T(128)} %param.11) | copy-start | bytes 388
  0.7 4.7 %copy-start.6 = (f32[32]{0:T(128)S(1)}, f32[32]{0:T(128)}, u32[]{:S(2)}) copy-start(f32[32]{0:T(128)} %param.10) | copy-start | bytes 388
  0.7 4.8 %slice-start = ((s32[32,128]{1,0:T(8,128)}), s32[24,128]{1,0:T(8,128)S(1)}, s32[]{:S(2)}) async-start(s32[32,128]{1,0:T(8,128)} %param.9), calls=%async_computation.2 | async-start | bytes 24576 | tf_op jit(solution)/shard_map/slice | solution.py:206
  2.3 13.7 %collective-permute-start = (f32[145,6,128]{2,0,1:T(8,128)S(1)}, f32[145,6,128]{2,0,1:T(8,128)S(1)}, u32[]{:S(2)}, u32[]{:S(2)}) collective-permute-start(f32[145,6,128]{2,0,1:T(8,128)S(1)} %copy.41), channel_id=1, source_target_pairs={{0,1},{1,0},{2,3},{3,2},{4,5},{5,4},{6,7},{7,6},{8,9},{9,8},{10,11... | collective-permute-start | bytes 1336328 | tf_op jit(solution)/shard_map/ppermute | solution.py:28
  58.6 5.3 %copy-start.3 = (s32[4]{0:T(128)S(1)}, s32[4]{0:T(128)}, u32[]{:S(2)}) copy-start(s32[4]{0:T(128)} %off_ref.1) | copy-start | bytes 52
  58.6 5.9 %copy-start.4 = (f32[32]{0:T(128)S(1)}, f32[32]{0:T(128)}, u32[]{:S(2)}) copy-start(f32[32]{0:T(128)} %param.12) | copy-start | bytes 388
  58.6 47.4 %all-to-all-start = ((f32[144,8,384]{2,0,1:T(8,128)}), f32[144,8,384]{2,0,1:T(8,128)}, u32[]{:S(2)}, u32[]{:S(2)}) async-start(f32[144,8,384]{2,0,1:T(8,128)} %copy.45), calls=%async_computation | async-start | bytes 3538944 | tf_op jit(solution)/shard_map/all_to_all | solution.py:208
  122.7 6.9 %copy-start.2 = (s32[32,128]{1,0:T(8,128)S(1)}, s32[32,128]{1,0:T(8,128)}, u32[]{:S(2)}) copy-start(s32[32,128]{1,0:T(8,128)} %param.9) | copy-start | bytes 49156
  125.3 46.4 %all-to-all-start.1 = ((f32[8,144,384]{2,1,0:T(8,128)}), f32[8,144,384]{2,1,0:T(8,128)}, u32[]{:S(2)}, u32[]{:S(2)}) async-start(f32[8,144,384]{2,1,0:T(8,128)} %all_to_all.29), calls=%async_computation.1 | async-start | bytes 3538944 | tf_op jit(solution)/shard_map/all_to_all | solution.py:210

commit v14 on v8

--- a/solution.py
+++ b/solution.py
@@ -145,24 +145,21 @@
     lax.fori_loop(0, NDIR, sources, 0)
 
 
-def interact_pallas(columns, coupling, quad_offsets):
-    comps, points = columns.shape
-    spectra = columns.reshape(NFREQ, NDIR, points).transpose(1, 0, 2)
+def interact_pallas(spectra, coupling, quad_offsets):
     freq_index = lax.iota(jnp.int32, NFREQ)
     inside = ((freq_index + quad_offsets[0] < NFREQ) & (freq_index - quad_offsets[1] >= 0)).astype(jnp.float32)
     weight = (coupling * inside)[:, None]
-    out = pl.pallas_call(
+    return pl.pallas_call(
         interact_kernel,
-        out_shape=jax.ShapeDtypeStruct((NDIR, NFREQ, points), jnp.float32),
+        out_shape=jax.ShapeDtypeStruct(spectra.shape, jnp.float32),
         in_specs=[
             pl.BlockSpec(memory_space=pltpu.SMEM),
             pl.BlockSpec(memory_space=pltpu.VMEM),
             pl.BlockSpec(memory_space=pltpu.VMEM),
         ],
         out_specs=pl.BlockSpec(memory_space=pltpu.VMEM),
-        scratch_shapes=[pltpu.VMEM((2, NDIR, NFREQ, points), jnp.float32)],
+        scratch_shapes=[pltpu.VMEM((2,) + spectra.shape, jnp.float32)],
     )(quad_offsets, weight, spectra)
-    return out.transpose(1, 0, 2).reshape(comps, points)
 
 
 def per_component(lookup, freq_index):
@@ -202,16 +199,30 @@
     smoothed = (
         centre + spread_y * laplace(with_rim, 1) + spread_x * laplace_x(centre)
     ) * transparency
-    flat_cells = smoothed.reshape(local_comps, -1)
+    cells_first = smoothed.reshape(local_comps, -1).T
+    spec_size = lax.axis_size("spec")
+    local_freqs = local_comps // NDIR
     sea_cells = sea_order.reshape(-1)[:SEA_MAX]
-    columns = flat_cells.at[:, sea_cells].get(mode="promise_in_bounds", unique_indices=True)
-    gathered = lax.all_to_all(columns, "spec", split_axis=1, concat_axis=0, tiled=True)
-    source_terms = interact_pallas(gathered, coupling, quad_offsets)
-    returned = lax.all_to_all(source_terms, "spec", split_axis=0, concat_axis=1, tiled=True)
-    new_cells = flat_cells.at[:, sea_cells].add(
+    points = SEA_MAX // spec_size
+    rows = cells_first.at[sea_cells].get(mode="promise_in_bounds", unique_indices=True)
+    gathered = lax.all_to_all(rows, "spec", split_axis=0, concat_axis=0, tiled=True)
+    spectra = (
+        gathered.reshape(spec_size, points, local_freqs, NDIR)
+        .transpose(3, 0, 2, 1)
+        .reshape(NDIR, NFREQ, points)
+    )
+    by_dir = interact_pallas(spectra, coupling, quad_offsets)
+    source_terms = by_dir.transpose(1, 0, 2).reshape(NFREQ * NDIR, points)
+    outgoing = (
+        by_dir.reshape(NDIR, spec_size, local_freqs, points)
+        .transpose(1, 3, 2, 0)
+        .reshape(spec_size * points, local_comps)
+    )
+    returned = lax.all_to_all(outgoing, "spec", split_axis=0, concat_axis=0, tiled=True)
+    new_cells = cells_first.at[sea_cells].add(
         returned, mode="promise_in_bounds", unique_indices=True
     )
-    updated = new_cells.reshape(smoothed.shape)
+    updated = new_cells.T.reshape(smoothed.shape)
     return (updated, source_terms.astype(jnp.bfloat16)[None])
 
 

time: 196 us -> 191 us (0.974)
  local copies, waits for them, and re-layouts: 39.7 us -> 34.4 us
    transpose x1, local copies, waits for them, and re-layouts: 3.78 us -> 1.14 us  [on_device(): spectra = gathered.reshape(spec_size, points, local_freqs, NDIR).transpos...]
    all_to_all x4, local copies, waits for them, and re-layouts: 8.25 us -> 6.26 us  [the longest x2 3.66 us: on_device(): lax.all_to_all(outgoing, 'spec', split_axis=0, concat_axis=0, tiled=True)]
    unnamed x17 -> x15, local copies, waits for them, and re-layouts: 6.06 us -> 4.86 us
where the time goes in v14:
time: 191 us
  waiting for transfers between devices  90.4 us (47%)
  other arithmetic  45.2 us (24%)
  local copies, waits for them, and re-layouts  34.4 us (18%)
  starting transfers between devices  12.6 us (7%)
  Pallas kernels  7.24 us (4%)
    all_to_all x1, waiting for transfers between devices, on_device(): lax.all_to_all(outgoing, 'spec', split_axis=0, concat_axis=0, tiled=True)  40.5 us
    all_to_all x1, waiting for transfers between devices, on_device(): lax.all_to_all(rows, 'spec', split_axis=0, concat_axis=0, tiled=True)  39.5 us
    scatter-add x1, other arithmetic, on_device(): cells_first.at[sea_cells]  21.1 us
    gather x1, local copies, waits for them, and re-layouts, on_device(): cells_first.at[sea_cells].get(mode='promise_in_bounds', unique_indices=True)  12 us
    ppermute x1, waiting for transfers between devices, extended_2(): lax.ppermute(jnp.where(first, bottom, top), axis, [(0, 1), (1, 0)])  10.4 us
    mul x4, other arithmetic, propagate(): energy = quickest_x(energy, courant_x) * ext_mask  9.36 us
    pallas_call x1, Pallas kernels, interact_pallas(): pl.pallas_call(interact_kernel, out_shape=jax.ShapeDtypeStruct(spectra.sh...  7.24 us
    mul x2, other arithmetic, quickest(): face_flux = courant * face_value  5.47 us
  transfers between devices with their start and end apart: 3, of which 3 were waited for; matrix products, arithmetic and copies ran while one was open for 2% of the time, Pallas kernels for 0%

profile of v14, /device:TPU:0, one launch (start us, length us, event | category | flops | bytes accessed | tf_op | source)
XLA Modules:
  0.0 190.8 jit_solution(13903504885155208869)
XLA Ops:
  0.7 1.5 fusion.56
  2.3 3.0 %collective-permute-start = (f32[145,6,128]{2,0,1:T(8,128)S(1)}, f32[145,6,128]{2,0,1:T(8,128)S(1)}, u32[]{:S(2)}, u32[]{:S(2)}) collective-permute-start(f32[145,6,128]{2,0,1:T(8,128)S(1)} %copy.44), channel_id=1, source_target_pairs={{0,1},{1,0},{2,3},{3,2},{4,5},{5,4},{6,7},{7,6},{8,9},{9,8},{10,11... | collective-permute-start | bytes 1336328 | tf_op jit(solution)/shard_map/ppermute | solution.py:28
  5.6 10.4 %collective-permute-done = f32[145,6,128]{2,0,1:T(8,128)S(1)} collective-permute-done((f32[145,6,128]{2,0,1:T(8,128)S(1)}, f32[145,6,128]{2,0,1:T(8,128)S(1)}, u32[]{:S(2)}, u32[]{:S(2)}) %collective-permute-start) | collective-permute-done | bytes 445472 | tf_op jit(solution)/shard_map/ppermute | solution.py:28
  16.7 2.8 %fusion.4 = f32[144,41,128]{2,1,0:T(8,128)S(1)} fusion(f32[145,44,128]{2,1,0:T(8,128)S(1)} %pad_maximum_fusion, f32[144]{0:T(256)S(1)} %get-tuple-element.30, f32[144]{0:T(256)S(1)} %get-tuple-element.31, f32[144]{0:T(256)S(1)} %get-tuple-element.25, pred[144]{0:T(512)(128)(4,1)S(1)} %get-tuple-element.24), kind=kLoop, calls=%fused_computation.20 | loop fusion | flops 11335680 | bytes 15116112 | tf_op jit(solution)/shard_map/mul | solution.py:60
  20.6 4.7 %fusion.13 = f32[144,40,128]{2,1,0:T(8,128)S(1)} fusion(f32[144,40,128]{2,1,0:T(8,128)S(1)} %fusion.39, f32[40,128]{1,0:T(8,128)S(1)} %maximum_bitcast_fusion.1, f32[144]{0:T(256)S(1)} %get-tuple-element.23, f32[144]{0:T(256)S(1)} %get-tuple-element.22, f32[144]{0:T(256)S(1)} %get-tuple-element.15, pred[144]{0:T(512)(128)(4,1)S(1)} %get-tuple-element.14), kind=kLoop, calls=%fused_computation.30 | loop fusion | flops 22118400 | bytes 5920592 | tf_op jit(solution)/shard_map/mul | solution.py:174
  25.3 2.6 %fusion.38 = f32[144,37,128]{2,1,0:T(8,128)S(1)} fusion(f32[144,40,128]{2,1,0:T(8,128)S(1)} %fusion.13, f32[144]{0:T(256)S(1)} %get-tuple-element.30, f32[144]{0:T(256)S(1)} %get-tuple-element.31, f32[144]{0:T(256)S(1)} %get-tuple-element.25, pred[144]{0:T(512)(128)(4,1)S(1)} %get-tuple-element.24), kind=kLoop, calls=%fused_computation.57 | loop fusion | flops 10229760 | bytes 13641552 | tf_op jit(solution)/shard_map/mul | solution.py:60
  28.5 4.7 %fusion.27 = f32[144,36,128]{2,1,0:T(8,128)S(1)} fusion(f32[144,36,128]{2,1,0:T(8,128)S(1)} %fusion.33, f32[36,128]{1,0:T(8,128)S(1)} %maximum_bitcast_fusion, f32[144]{0:T(256)S(1)} %get-tuple-element.23, f32[144]{0:T(256)S(1)} %get-tuple-element.22, f32[144]{0:T(256)S(1)} %get-tuple-element.15, pred[144]{0:T(512)(128)(4,1)S(1)} %get-tuple-element.14), kind=kLoop, calls=%fused_computation.44 | loop fusion | flops 19906560 | bytes 5328720 | tf_op jit(solution)/shard_map/mul | solution.py:174
  33.6 3.9 %fusion.46 = f32[144,32,128]{2,1,0:T(8,128)S(1)} fusion(f32[144,32,128]{2,1,0:T(8,128)S(1)} %slice.148, f32[144,36,128]{2,1,0:T(8,128)S(1)} %fusion.27, f32[32,128]{1,0:T(8,128)S(1)} %copy-done.2, f32[144]{0:T(256)S(1)} %get-tuple-element.21, f32[144]{0:T(256)S(1)} %get-tuple-element.20), kind=kLoop, calls=%fused_computation.67 | loop fusion | flops 11796480 | bytes 14173312 | tf_op jit(solution)/shard_map/mul | solution.py:199
  37.5 3.3 %copy.47 = f32[144,32,128]{0,2,1:T(8,128)} copy(f32[144,32,128]{2,1,0:T(8,128)S(1)} %fusion.46) | data formatting | bytes 4718592 | tf_op jit(solution)/shard_map/mul | solution.py:199
  40.8 12.0 %gather_fusion = f32[3072,144]{1,0:T(8,128)S(1)} fusion(f32[4096,144]{1,0:T(8,128)} %bitcast.27, s32[3072]{0:T(1024)S(1)} %broadcast_clamp_fusion), kind=kCustom, calls=%fused_computation | custom fusion | bytes 3551232 | tf_op jit(solution)/shard_map/gather | solution.py:207
  52.8 2.0 %copy.48 = f32[8,384,144]{1,2,0:T(8,128)} copy(f32[8,384,144]{2,1,0:T(8,128)S(1)} %bitcast.31) | data formatting | bytes 3538944 | tf_op jit(solution)/shard_map/all_to_all | solution.py:208
  54.9 5.3 %all-to-all-start = ((f32[8,384,144]{1,2,0:T(8,128)}), f32[8,384,144]{1,2,0:T(8,128)S(1)}, u32[]{:S(2)}, u32[]{:S(2)}) async-start(f32[8,384,144]{1,2,0:T(8,128)} %copy.48), calls=%async_computation | async-start | bytes 3538944 | tf_op jit(solution)/shard_map/all_to_all | solution.py:208
  60.7 1.2 fusion.66
  62.6 39.5 %all-to-all-done = f32[8,384,144]{1,2,0:T(8,128)S(1)} async-done(((f32[8,384,144]{1,2,0:T(8,128)}), f32[8,384,144]{1,2,0:T(8,128)S(1)}, u32[]{:S(2)}, u32[]{:S(2)}) %all-to-all-start) | async-done | bytes 1769504 | tf_op jit(solution)/shard_map/all_to_all | solution.py:208
  102.7 1.1 copy.50
  103.8 1.8 reshape.174.e_ref
  105.7 7.2 %shard_map.86 = f32[36,32,384]{2,1,0:T(8,128)} custom-call(s32[4]{0:T(128)} %off_ref.1, f32[32,1]{1,0:T(8,128)} %copy.51.w_ref, f32[36,32,384]{2,1,0:T(8,128)} %reshape.174.e_ref), custom_call_target="tpu_custom_call" | custom-call | tf_op jit(solution)/shard_map/pallas_call | solution.py:152
  112.9 1.8 reshape.175
  114.9 1.5 copy.53
  116.4 4.3 %all-to-all-start.1 = ((f32[8,384,144]{1,2,0:T(8,128)}), f32[8,384,144]{1,2,0:T(8,128)}, u32[]{:S(2)}, u32[]{:S(2)}) async-start(f32[8,384,144]{1,2,0:T(8,128)} %copy.53), calls=%async_computation.1 | async-start | bytes 3538944 | tf_op jit(solution)/shard_map/all_to_all | solution.py:221
  122.2 40.5 %all-to-all-done.1 = f32[8,384,144]{1,2,0:T(8,128)} async-done(((f32[8,384,144]{1,2,0:T(8,128)}), f32[8,384,144]{1,2,0:T(8,128)}, u32[]{:S(2)}, u32[]{:S(2)}) %all-to-all-start.1) | async-done | bytes 1769504 | tf_op jit(solution)/shard_map/all_to_all | solution.py:221
  162.7 2.1 %copy.58 = f32[8,384,144]{2,1,0:T(8,128)S(1)} copy(f32[8,384,144]{1,2,0:T(8,128)} %all-to-all-done.1) | data formatting | bytes 3538944 | tf_op jit(solution)/shard_map/all_to_all | solution.py:221
  164.9 21.1 %scatter_fusion = f32[4096,144]{1,0:T(8,128)} fusion(f32[4096,144]{1,0:T(8,128)} %bitcast.28, s32[3072]{0:T(1024)S(1)} %bitcast.39, f32[3072,144]{1,0:T(8,128)S(1)} %bitcast.30), kind=kCustom, calls=%fused_computation.1 | custom fusion | flops 442368 | bytes 5320704 | tf_op jit(solution)/shard_map/scatter-add | solution.py:222
  186.0 4.8 %copy.57 = f32[144,32,128]{2,1,0:T(8,128)} copy(f32[144,32,128]{0,2,1:T(8,128)} %bitcast.29) | data formatting | bytes 4718592
  (38 shorter events, 6.6 us)
Async XLA Ops:
  0.6 15.5 %copy-start = (f32[144,32,128]{2,1,0:T(8,128)S(1)}, f32[144,32,128]{2,1,0:T(8,128)}, u32[]{:S(2)}) copy-start(f32[144,32,128]{2,1,0:T(8,128)} %param.7) | copy-start | bytes 7077892
  0.6 15.5 %copy-start.2 = (f32[32,128]{1,0:T(8,128)S(1)}, f32[32,128]{1,0:T(8,128)}, u32[]{:S(2)}) copy-start(f32[32,128]{1,0:T(8,128)} %param.8) | copy-start | bytes 49156
  0.7 4.7 %copy-start.5 = (f32[32]{0:T(128)S(1)}, f32[32]{0:T(128)}, u32[]{:S(2)}) copy-start(f32[32]{0:T(128)} %param.11) | copy-start | bytes 388
  0.7 4.7 %copy-start.6 = (f32[32]{0:T(128)S(1)}, f32[32]{0:T(128)}, u32[]{:S(2)}) copy-start(f32[32]{0:T(128)} %param.10) | copy-start | bytes 388
  0.7 4.8 %slice-start = ((s32[32,128]{1,0:T(8,128)}), s32[24,128]{1,0:T(8,128)S(1)}, s32[]{:S(2)}) async-start(s32[32,128]{1,0:T(8,128)} %param.9), calls=%async_computation.2 | async-start | bytes 24576 | tf_op jit(solution)/shard_map/slice | solution.py:205
  2.3 13.7 %collective-permute-start = (f32[145,6,128]{2,0,1:T(8,128)S(1)}, f32[145,6,128]{2,0,1:T(8,128)S(1)}, u32[]{:S(2)}, u32[]{:S(2)}) collective-permute-start(f32[145,6,128]{2,0,1:T(8,128)S(1)} %copy.44), channel_id=1, source_target_pairs={{0,1},{1,0},{2,3},{3,2},{4,5},{5,4},{6,7},{7,6},{8,9},{9,8},{10,11... | collective-permute-start | bytes 1336328 | tf_op jit(solution)/shard_map/ppermute | solution.py:28
  54.8 5.3 %copy-start.3 = (s32[4]{0:T(128)S(1)}, s32[4]{0:T(128)}, u32[]{:S(2)}) copy-start(s32[4]{0:T(128)} %off_ref.1) | copy-start | bytes 52
  54.9 5.9 %copy-start.4 = (f32[32]{0:T(128)S(1)}, f32[32]{0:T(128)}, u32[]{:S(2)}) copy-start(f32[32]{0:T(128)} %param.12) | copy-start | bytes 388
  54.9 47.3 %all-to-all-start = ((f32[8,384,144]{1,2,0:T(8,128)}), f32[8,384,144]{1,2,0:T(8,128)S(1)}, u32[]{:S(2)}, u32[]{:S(2)}) async-start(f32[8,384,144]{1,2,0:T(8,128)} %copy.48), calls=%async_computation | async-start | bytes 3538944 | tf_op jit(solution)/shard_map/all_to_all | solution.py:208
  114.8 5.9 %copy-start.1 = (f32[36,32,384]{2,1,0:T(8,128)S(1)}, f32[36,32,384]{2,1,0:T(8,128)}, u32[]{:S(2)}) copy-start(f32[36,32,384]{2,1,0:T(8,128)} %shard_map.86) | copy-start | bytes 5308420
  116.4 46.3 %all-to-all-start.1 = ((f32[8,384,144]{1,2,0:T(8,128)}), f32[8,384,144]{1,2,0:T(8,128)}, u32[]{:S(2)}, u32[]{:S(2)}) async-start(f32[8,384,144]{1,2,0:T(8,128)} %copy.53), calls=%async_computation.1 | async-start | bytes 3538944 | tf_op jit(solution)/shard_map/all_to_all | solution.py:221

commit v15 on v14

--- a/solution.py
+++ b/solution.py
@@ -219,10 +219,10 @@
         .reshape(spec_size * points, local_comps)
     )
     returned = lax.all_to_all(outgoing, "spec", split_axis=0, concat_axis=0, tiled=True)
-    new_cells = cells_first.at[sea_cells].add(
+    placed = jnp.zeros_like(cells_first).at[sea_cells].set(
         returned, mode="promise_in_bounds", unique_indices=True
     )
-    updated = new_cells.T.reshape(smoothed.shape)
+    updated = smoothed + placed.T.reshape(smoothed.shape)
     return (updated, source_terms.astype(jnp.bfloat16)[None])
 
 

time: 191 us -> 201 us (1.052)
  local copies, waits for them, and re-layouts: 34.4 us -> 61.3 us
  other arithmetic: 45.2 us -> 29.2 us
    scatter-add x1 -> x0, other arithmetic: 21.1 us -> none  [on_device(): cells_first.at[sea_cells]]
    scatter x0 -> x1, local copies, waits for them, and re-layouts: none -> 15.8 us  [on_device(): jnp.zeros_like(cells_first).at[sea_cells]]
    unnamed x15 -> x12, local copies, waits for them, and re-layouts: 4.86 us -> 0.02 us
    reshape x0 -> x1, local copies, waits for them, and re-layouts: none -> 4.83 us  [on_device(): updated = smoothed + placed.T.reshape(smoothed.shape)]
    add x0 -> x1, other arithmetic: none -> 3.61 us  [on_device(): updated = smoothed + placed.T.reshape(smoothed.shape)]
    all_to_all x2, local copies, waits for them, and re-layouts: 2.6 us -> 5.28 us  [on_device(): lax.all_to_all(rows, 'spec', split_axis=0, concat_axis=0, tiled=True)]
    gather x1, local copies, waits for them, and re-layouts: 12 us -> 14.5 us  [on_device(): cells_first.at[sea_cells].get(mode='promise_in_bounds', unique_indices=True)]
    reshape x2, local copies, waits for them, and re-layouts: 1.93 us -> 4.37 us  [on_device(): by_dir.reshape(NDIR, spec_size, local_freqs, points).transpose(1, 3, 2, 0)]
  transfers between devices with their start and end apart: 3 -> 3, of which waited for: 3 -> 3; matrix products, arithmetic and copies ran while one was open for 2% -> 3% of each run, Pallas kernels for 0% -> 0%
where the time goes in v15:
time: 201 us; the launch traced here: 200 us
  waiting for transfers between devices  88.9 us (44%)
  local copies, waits for them, and re-layouts  61.3 us (30%)
  other arithmetic  29.2 us (15%)
  starting transfers between devices  12.6 us (6%)
  Pallas kernels  7.24 us (4%)
    all_to_all x1, waiting for transfers between devices, on_device(): lax.all_to_all(rows, 'spec', split_axis=0, concat_axis=0, tiled=True)  39.5 us
    all_to_all x1, waiting for transfers between devices, on_device(): lax.all_to_all(outgoing, 'spec', split_axis=0, concat_axis=0, tiled=True)  39 us
    scatter x1, local copies, waits for them, and re-layouts, on_device(): jnp.zeros_like(cells_first).at[sea_cells]  15.8 us
    gather x1, local copies, waits for them, and re-layouts, on_device(): cells_first.at[sea_cells].get(mode='promise_in_bounds', unique_indices=True)  14.5 us
    ppermute x1, waiting for transfers between devices, extended_2(): lax.ppermute(jnp.where(first, bottom, top), axis, [(0, 1), (1, 0)])  10.4 us
    mul x4, other arithmetic, propagate(): energy = quickest_x(energy, courant_x) * ext_mask  9.35 us
    pallas_call x1, Pallas kernels, interact_pallas(): pl.pallas_call(interact_kernel, out_shape=jax.ShapeDtypeStruct(spectra.sh...  7.24 us
    mul x2, other arithmetic, quickest(): face_flux = courant * face_value  5.46 us
  transfers between devices with their start and end apart: 3, of which 3 were waited for; matrix products, arithmetic and copies ran while one was open for 3% of the time, Pallas kernels for 0%

profile of v15, /device:TPU:0, one launch (start us, length us, event | category | flops | bytes accessed | tf_op | source)
XLA Modules:
  0.0 200.2 jit_solution(14829528199645286374)
XLA Ops:
  2.3 3.0 %collective-permute-start = (f32[145,6,128]{2,0,1:T(8,128)S(1)}, f32[145,6,128]{2,0,1:T(8,128)S(1)}, u32[]{:S(2)}, u32[]{:S(2)}) collective-permute-start(f32[145,6,128]{2,0,1:T(8,128)S(1)} %copy.44), channel_id=1, source_target_pairs={{0,1},{1,0},{2,3},{3,2},{4,5},{5,4},{6,7},{7,6},{8,9},{9,8},{10,11... | collective-permute-start | bytes 1336328 | tf_op jit(solution)/shard_map/ppermute | solution.py:28
  5.6 10.4 %collective-permute-done = f32[145,6,128]{2,0,1:T(8,128)S(1)} collective-permute-done((f32[145,6,128]{2,0,1:T(8,128)S(1)}, f32[145,6,128]{2,0,1:T(8,128)S(1)}, u32[]{:S(2)}, u32[]{:S(2)}) %collective-permute-start) | collective-permute-done | bytes 445472 | tf_op jit(solution)/shard_map/ppermute | solution.py:28
  16.7 2.8 %fusion.4 = f32[144,41,128]{2,1,0:T(8,128)S(1)} fusion(f32[145,44,128]{2,1,0:T(8,128)S(1)} %pad_maximum_fusion, f32[144]{0:T(256)S(1)} %get-tuple-element.22, f32[144]{0:T(256)S(1)} %get-tuple-element.23, f32[144]{0:T(256)S(1)} %get-tuple-element.17, pred[144]{0:T(512)(128)(4,1)S(1)} %get-tuple-element.16), kind=kLoop, calls=%fused_computation.20 | loop fusion | flops 11335680 | bytes 15116112 | tf_op jit(solution)/shard_map/mul | solution.py:60
  20.6 4.7 %fusion.13 = f32[144,40,128]{2,1,0:T(8,128)S(1)} fusion(f32[144,40,128]{2,1,0:T(8,128)S(1)} %fusion.39, f32[40,128]{1,0:T(8,128)S(1)} %maximum_bitcast_fusion.1, f32[144]{0:T(256)S(1)} %get-tuple-element.15, f32[144]{0:T(256)S(1)} %get-tuple-element.14, f32[144]{0:T(256)S(1)} %get-tuple-element.7, pred[144]{0:T(512)(128)(4,1)S(1)} %get-tuple-element.6), kind=kLoop, calls=%fused_computation.30 | loop fusion | flops 22118400 | bytes 5920592 | tf_op jit(solution)/shard_map/mul | solution.py:174
  25.3 2.6 %fusion.38 = f32[144,37,128]{2,1,0:T(8,128)S(1)} fusion(f32[144,40,128]{2,1,0:T(8,128)S(1)} %fusion.13, f32[144]{0:T(256)S(1)} %get-tuple-element.22, f32[144]{0:T(256)S(1)} %get-tuple-element.23, f32[144]{0:T(256)S(1)} %get-tuple-element.17, pred[144]{0:T(512)(128)(4,1)S(1)} %get-tuple-element.16), kind=kLoop, calls=%fused_computation.57 | loop fusion | flops 10229760 | bytes 13641552 | tf_op jit(solution)/shard_map/mul | solution.py:60
  28.5 4.7 %fusion.27 = f32[144,36,128]{2,1,0:T(8,128)S(1)} fusion(f32[144,36,128]{2,1,0:T(8,128)S(1)} %fusion.33, f32[36,128]{1,0:T(8,128)S(1)} %maximum_bitcast_fusion, f32[144]{0:T(256)S(1)} %get-tuple-element.15, f32[144]{0:T(256)S(1)} %get-tuple-element.14, f32[144]{0:T(256)S(1)} %get-tuple-element.7, pred[144]{0:T(512)(128)(4,1)S(1)} %get-tuple-element.6), kind=kLoop, calls=%fused_computation.44 | loop fusion | flops 19906560 | bytes 5328720 | tf_op jit(solution)/shard_map/mul | solution.py:174
  33.6 3.9 %fusion.46 = f32[144,32,128]{2,1,0:T(8,128)S(1)} fusion(f32[144,32,128]{2,1,0:T(8,128)S(1)} %slice.148, f32[144,36,128]{2,1,0:T(8,128)S(1)} %fusion.27, f32[32,128]{1,0:T(8,128)S(1)} %copy-done.1, f32[144]{0:T(256)S(1)} %get-tuple-element.13, f32[144]{0:T(256)S(1)} %get-tuple-element.12), kind=kLoop, calls=%fused_computation.67 | loop fusion | flops 11796480 | bytes 14173312 | tf_op jit(solution)/shard_map/mul | solution.py:199
  37.5 3.3 %copy.47 = f32[144,32,128]{0,2,1:T(8,128)} copy(f32[144,32,128]{2,1,0:T(8,128)S(1)} %fusion.46) | data formatting | bytes 4718592 | tf_op jit(solution)/shard_map/mul | solution.py:199
  40.8 14.5 %gather_fusion = f32[3072,144]{1,0:T(8,128)} fusion(f32[4096,144]{1,0:T(8,128)} %bitcast.28, s32[3072]{0:T(1024)S(1)} %broadcast_clamp_fusion), kind=kCustom, calls=%fused_computation | custom fusion | bytes 3551232 | tf_op jit(solution)/shard_map/gather | solution.py:207
  55.3 3.2 %copy.48 = f32[8,384,144]{1,2,0:T(8,128)} copy(f32[8,384,144]{2,1,0:T(8,128)} %bitcast.30) | data formatting | bytes 3538944 | tf_op jit(solution)/shard_map/all_to_all | solution.py:208
  58.5 5.3 %all-to-all-start = ((f32[8,384,144]{1,2,0:T(8,128)}), f32[8,384,144]{1,2,0:T(8,128)}, u32[]{:S(2)}, u32[]{:S(2)}) async-start(f32[8,384,144]{1,2,0:T(8,128)} %copy.48), calls=%async_computation | async-start | bytes 3538944 | tf_op jit(solution)/shard_map/all_to_all | solution.py:208
  66.4 39.5 %all-to-all-done = f32[8,384,144]{1,2,0:T(8,128)} async-done(((f32[8,384,144]{1,2,0:T(8,128)}), f32[8,384,144]{1,2,0:T(8,128)}, u32[]{:S(2)}, u32[]{:S(2)}) %all-to-all-start) | async-done | bytes 1769504 | tf_op jit(solution)/shard_map/all_to_all | solution.py:208
  105.9 2.0 %copy.49 = f32[8,384,144]{1,0,2:T(8,128)S(1)} copy(f32[8,384,144]{1,2,0:T(8,128)} %all-to-all-done) | data formatting | bytes 3538944 | tf_op jit(solution)/shard_map/all_to_all | solution.py:208
  107.9 2.3 %copy.50 = f32[36,8,4,384]{3,2,1,0:T(4,128)} copy(f32[36,8,4,384]{3,1,0,2:T(8,128)S(1)} %bitcast.31) | data formatting | bytes 3538944 | tf_op jit(solution)/shard_map/transpose | solution.py:211
  110.3 2.8 %reshape.174.e_ref = f32[36,32,384]{2,1,0:T(8,128)} reshape(f32[36,8,4,384]{3,2,1,0:T(4,128)} %copy.50) | data formatting | bytes 3538944 | tf_op jit(solution)/shard_map/reshape | solution.py:212
  113.1 7.2 %shard_map.86 = f32[36,32,384]{2,1,0:T(8,128)} custom-call(s32[4]{0:T(128)} %off_ref.1, f32[32,1]{1,0:T(8,128)} %copy.51.w_ref, f32[36,32,384]{2,1,0:T(8,128)} %reshape.174.e_ref), custom_call_target="tpu_custom_call" | custom-call | tf_op jit(solution)/shard_map/pallas_call | solution.py:152
  120.4 2.8 %reshape.175 = f32[36,8,4,384]{3,2,1,0:T(4,128)} reshape(f32[36,32,384]{2,1,0:T(8,128)} %shard_map.86) | data formatting | bytes 3538944 | tf_op jit(solution)/shard_map/reshape | solution.py:217
  123.1 1.6 copy.52
  126.3 4.3 %all-to-all-start.1 = ((f32[8,384,144]{1,2,0:T(8,128)}), f32[8,384,144]{1,2,0:T(8,128)}, u32[]{:S(2)}, u32[]{:S(2)}) async-start(f32[8,384,144]{1,2,0:T(8,128)} %copy.53), calls=%async_computation.1 | async-start | bytes 3538944 | tf_op jit(solution)/shard_map/all_to_all | solution.py:221
  133.6 39.0 %all-to-all-done.1 = f32[8,384,144]{1,2,0:T(8,128)} async-done(((f32[8,384,144]{1,2,0:T(8,128)}), f32[8,384,144]{1,2,0:T(8,128)}, u32[]{:S(2)}, u32[]{:S(2)}) %all-to-all-start.1) | async-done | bytes 1769504 | tf_op jit(solution)/shard_map/all_to_all | solution.py:221
  172.6 3.3 %copy.58 = f32[8,384,144]{2,1,0:T(8,128)} copy(f32[8,384,144]{1,2,0:T(8,128)} %all-to-all-done.1) | data formatting | bytes 3538944 | tf_op jit(solution)/shard_map/all_to_all | solution.py:221
  175.9 15.8 %scatter_custom_fusion = f32[4096,144]{1,0:T(8,128)} fusion(s32[3072]{0:T(1024)S(1)} %bitcast.39, f32[3072,144]{1,0:T(8,128)} %bitcast.33, f32[]{:T(128)} %constant.20.clone.1), kind=kCustom, calls=%fused_computation.80 | custom fusion | bytes 2359808 | tf_op jit(solution)/shard_map/scatter | solution.py:222
  191.7 4.8 %copy.56 = f32[144,32,128]{2,1,0:T(8,128)} copy(f32[144,32,128]{0,2,1:T(8,128)} %bitcast.29) | data formatting | bytes 4718592 | tf_op jit(solution)/shard_map/reshape | solution.py:225
  196.5 3.6 %add.278 = f32[144,32,128]{2,1,0:T(8,128)} add(f32[144,32,128]{2,1,0:T(8,128)S(1)} %fusion.46, f32[144,32,128]{2,1,0:T(8,128)} %copy.56) | non-fusion elementwise | flops 589824 | bytes 7077888 | tf_op jit(solution)/shard_map/add | solution.py:225
  (37 shorter events, 11.7 us)
Async XLA Ops:
  0.6 15.5 %copy-start = (f32[144,32,128]{2,1,0:T(8,128)S(1)}, f32[144,32,128]{2,1,0:T(8,128)}, u32[]{:S(2)}) copy-start(f32[144,32,128]{2,1,0:T(8,128)} %param.7) | copy-start | bytes 7077892
  0.6 15.5 %copy-start.1 = (f32[32,128]{1,0:T(8,128)S(1)}, f32[32,128]{1,0:T(8,128)}, u32[]{:S(2)}) copy-start(f32[32,128]{1,0:T(8,128)} %param.8) | copy-start | bytes 49156
  0.7 4.7 %copy-start.4 = (f32[32]{0:T(128)S(1)}, f32[32]{0:T(128)}, u32[]{:S(2)}) copy-start(f32[32]{0:T(128)} %param.11) | copy-start | bytes 388
  0.7 4.7 %copy-start.5 = (f32[32]{0:T(128)S(1)}, f32[32]{0:T(128)}, u32[]{:S(2)}) copy-start(f32[32]{0:T(128)} %param.10) | copy-start | bytes 388
  0.7 4.8 %slice-start = ((s32[32,128]{1,0:T(8,128)}), s32[24,128]{1,0:T(8,128)S(1)}, s32[]{:S(2)}) async-start(s32[32,128]{1,0:T(8,128)} %param.9), calls=%async_computation.2 | async-start | bytes 24576 | tf_op jit(solution)/shard_map/slice | solution.py:205
  2.3 13.7 %collective-permute-start = (f32[145,6,128]{2,0,1:T(8,128)S(1)}, f32[145,6,128]{2,0,1:T(8,128)S(1)}, u32[]{:S(2)}, u32[]{:S(2)}) collective-permute-start(f32[145,6,128]{2,0,1:T(8,128)S(1)} %copy.44), channel_id=1, source_target_pairs={{0,1},{1,0},{2,3},{3,2},{4,5},{5,4},{6,7},{7,6},{8,9},{9,8},{10,11... | collective-permute-start | bytes 1336328 | tf_op jit(solution)/shard_map/ppermute | solution.py:28
  58.5 5.3 %copy-start.2 = (s32[4]{0:T(128)S(1)}, s32[4]{0:T(128)}, u32[]{:S(2)}) copy-start(s32[4]{0:T(128)} %off_ref.1) | copy-start | bytes 52
  58.5 5.9 %copy-start.3 = (f32[32]{0:T(128)S(1)}, f32[32]{0:T(128)}, u32[]{:S(2)}) copy-start(f32[32]{0:T(128)} %param.12) | copy-start | bytes 388
  58.5 47.4 %all-to-all-start = ((f32[8,384,144]{1,2,0:T(8,128)}), f32[8,384,144]{1,2,0:T(8,128)}, u32[]{:S(2)}, u32[]{:S(2)}) async-start(f32[8,384,144]{1,2,0:T(8,128)} %copy.48), calls=%async_computation | async-start | bytes 3538944 | tf_op jit(solution)/shard_map/all_to_all | solution.py:208
  126.3 46.3 %all-to-all-start.1 = ((f32[8,384,144]{1,2,0:T(8,128)}), f32[8,384,144]{1,2,0:T(8,128)}, u32[]{:S(2)}, u32[]{:S(2)}) async-start(f32[8,384,144]{1,2,0:T(8,128)} %copy.53), calls=%async_computation.1 | async-start | bytes 3538944 | tf_op jit(solution)/shard_map/all_to_all | solution.py:221

commit v16 on v14

--- a/solution.py
+++ b/solution.py
@@ -149,16 +149,20 @@
     freq_index = lax.iota(jnp.int32, NFREQ)
     inside = ((freq_index + quad_offsets[0] < NFREQ) & (freq_index - quad_offsets[1] >= 0)).astype(jnp.float32)
     weight = (coupling * inside)[:, None]
+    points = spectra.shape[2]
+    block = 128 if points % 128 == 0 else points
+    window = (NDIR, NFREQ, block)
     return pl.pallas_call(
         interact_kernel,
         out_shape=jax.ShapeDtypeStruct(spectra.shape, jnp.float32),
+        grid=(points // block,),
         in_specs=[
             pl.BlockSpec(memory_space=pltpu.SMEM),
-            pl.BlockSpec(memory_space=pltpu.VMEM),
-            pl.BlockSpec(memory_space=pltpu.VMEM),
+            pl.BlockSpec((NFREQ, 1), lambda i: (0, 0)),
+            pl.BlockSpec(window, lambda i: (0, 0, i)),
         ],
-        out_specs=pl.BlockSpec(memory_space=pltpu.VMEM),
-        scratch_shapes=[pltpu.VMEM((2,) + spectra.shape, jnp.float32)],
+        out_specs=pl.BlockSpec(window, lambda i: (0, 0, i)),
+        scratch_shapes=[pltpu.VMEM((2,) + window, jnp.float32)],
     )(quad_offsets, weight, spectra)
 
 

time: 191 us -> 197 us (1.031)
  Pallas kernels: 7.24 us -> 13.3 us
    pallas_call x1, Pallas kernels: 7.24 us -> 13.3 us  [interact_pallas(): pl.pallas_call(interact_kernel, out_shape=jax.ShapeDtypeStruct(spectra.sh...]
where the time goes in v16:
time: 197 us
  waiting for transfers between devices  90.4 us (46%)
  other arithmetic  45.2 us (23%)
  local copies, waits for them, and re-layouts  34.4 us (17%)
  Pallas kernels  13.3 us (7%)
  starting transfers between devices  12.6 us (6%)
    all_to_all x1, waiting for transfers between devices, on_device(): lax.all_to_all(outgoing, 'spec', split_axis=0, concat_axis=0, tiled=True)  40.5 us
    all_to_all x1, waiting for transfers between devices, on_device(): lax.all_to_all(rows, 'spec', split_axis=0, concat_axis=0, tiled=True)  39.5 us
    scatter-add x1, other arithmetic, on_device(): cells_first.at[sea_cells]  21.1 us
    pallas_call x1, Pallas kernels, interact_pallas(): pl.pallas_call(interact_kernel, out_shape=jax.ShapeDtypeStruct(spectra.sh...  13.3 us
    gather x1, local copies, waits for them, and re-layouts, on_device(): cells_first.at[sea_cells].get(mode='promise_in_bounds', unique_indices=True)  12 us
    ppermute x1, waiting for transfers between devices, extended_2(): lax.ppermute(jnp.where(first, bottom, top), axis, [(0, 1), (1, 0)])  10.4 us
    mul x4, other arithmetic, propagate(): energy = quickest_x(energy, courant_x) * ext_mask  9.36 us
    mul x2, other arithmetic, quickest(): face_flux = courant * face_value  5.47 us
  transfers between devices with their start and end apart: 3, of which 3 were waited for; matrix products, arithmetic and copies ran while one was open for 2% of the time, Pallas kernels for 0%

profile of v16, /device:TPU:0, one launch (start us, length us, event | category | flops | bytes accessed | tf_op | source)
XLA Modules:
  0.0 196.9 jit_solution(1764185219983780677)
XLA Ops:
  0.7 1.5 fusion.56
  2.3 3.0 %collective-permute-start = (f32[145,6,128]{2,0,1:T(8,128)S(1)}, f32[145,6,128]{2,0,1:T(8,128)S(1)}, u32[]{:S(2)}, u32[]{:S(2)}) collective-permute-start(f32[145,6,128]{2,0,1:T(8,128)S(1)} %copy.44), channel_id=1, source_target_pairs={{0,1},{1,0},{2,3},{3,2},{4,5},{5,4},{6,7},{7,6},{8,9},{9,8},{10,11... | collective-permute-start | bytes 1336328 | tf_op jit(solution)/shard_map/ppermute | solution.py:28
  5.6 10.4 %collective-permute-done = f32[145,6,128]{2,0,1:T(8,128)S(1)} collective-permute-done((f32[145,6,128]{2,0,1:T(8,128)S(1)}, f32[145,6,128]{2,0,1:T(8,128)S(1)}, u32[]{:S(2)}, u32[]{:S(2)}) %collective-permute-start) | collective-permute-done | bytes 445472 | tf_op jit(solution)/shard_map/ppermute | solution.py:28
  16.7 2.8 %fusion.4 = f32[144,41,128]{2,1,0:T(8,128)S(1)} fusion(f32[145,44,128]{2,1,0:T(8,128)S(1)} %pad_maximum_fusion, f32[144]{0:T(256)S(1)} %get-tuple-element.30, f32[144]{0:T(256)S(1)} %get-tuple-element.31, f32[144]{0:T(256)S(1)} %get-tuple-element.25, pred[144]{0:T(512)(128)(4,1)S(1)} %get-tuple-element.24), kind=kLoop, calls=%fused_computation.20 | loop fusion | flops 11335680 | bytes 15116112 | tf_op jit(solution)/shard_map/mul | solution.py:60
  20.6 4.7 %fusion.13 = f32[144,40,128]{2,1,0:T(8,128)S(1)} fusion(f32[144,40,128]{2,1,0:T(8,128)S(1)} %fusion.39, f32[40,128]{1,0:T(8,128)S(1)} %maximum_bitcast_fusion.1, f32[144]{0:T(256)S(1)} %get-tuple-element.23, f32[144]{0:T(256)S(1)} %get-tuple-element.22, f32[144]{0:T(256)S(1)} %get-tuple-element.15, pred[144]{0:T(512)(128)(4,1)S(1)} %get-tuple-element.14), kind=kLoop, calls=%fused_computation.30 | loop fusion | flops 22118400 | bytes 5920592 | tf_op jit(solution)/shard_map/mul | solution.py:178
  25.3 2.6 %fusion.38 = f32[144,37,128]{2,1,0:T(8,128)S(1)} fusion(f32[144,40,128]{2,1,0:T(8,128)S(1)} %fusion.13, f32[144]{0:T(256)S(1)} %get-tuple-element.30, f32[144]{0:T(256)S(1)} %get-tuple-element.31, f32[144]{0:T(256)S(1)} %get-tuple-element.25, pred[144]{0:T(512)(128)(4,1)S(1)} %get-tuple-element.24), kind=kLoop, calls=%fused_computation.57 | loop fusion | flops 10229760 | bytes 13641552 | tf_op jit(solution)/shard_map/mul | solution.py:60
  28.5 4.7 %fusion.27 = f32[144,36,128]{2,1,0:T(8,128)S(1)} fusion(f32[144,36,128]{2,1,0:T(8,128)S(1)} %fusion.33, f32[36,128]{1,0:T(8,128)S(1)} %maximum_bitcast_fusion, f32[144]{0:T(256)S(1)} %get-tuple-element.23, f32[144]{0:T(256)S(1)} %get-tuple-element.22, f32[144]{0:T(256)S(1)} %get-tuple-element.15, pred[144]{0:T(512)(128)(4,1)S(1)} %get-tuple-element.14), kind=kLoop, calls=%fused_computation.44 | loop fusion | flops 19906560 | bytes 5328720 | tf_op jit(solution)/shard_map/mul | solution.py:178
  33.6 3.9 %fusion.46 = f32[144,32,128]{2,1,0:T(8,128)S(1)} fusion(f32[144,32,128]{2,1,0:T(8,128)S(1)} %slice.148, f32[144,36,128]{2,1,0:T(8,128)S(1)} %fusion.27, f32[32,128]{1,0:T(8,128)S(1)} %copy-done.2, f32[144]{0:T(256)S(1)} %get-tuple-element.21, f32[144]{0:T(256)S(1)} %get-tuple-element.20), kind=kLoop, calls=%fused_computation.67 | loop fusion | flops 11796480 | bytes 14173312 | tf_op jit(solution)/shard_map/mul | solution.py:203
  37.5 3.3 %copy.47 = f32[144,32,128]{0,2,1:T(8,128)} copy(f32[144,32,128]{2,1,0:T(8,128)S(1)} %fusion.46) | data formatting | bytes 4718592 | tf_op jit(solution)/shard_map/mul | solution.py:203
  40.8 12.0 %gather_fusion = f32[3072,144]{1,0:T(8,128)S(1)} fusion(f32[4096,144]{1,0:T(8,128)} %bitcast.27, s32[3072]{0:T(1024)S(1)} %broadcast_clamp_fusion), kind=kCustom, calls=%fused_computation | custom fusion | bytes 3551232 | tf_op jit(solution)/shard_map/gather | solution.py:211
  52.8 2.0 %copy.48 = f32[8,384,144]{1,2,0:T(8,128)} copy(f32[8,384,144]{2,1,0:T(8,128)S(1)} %bitcast.31) | data formatting | bytes 3538944 | tf_op jit(solution)/shard_map/all_to_all | solution.py:212
  54.9 5.3 %all-to-all-start = ((f32[8,384,144]{1,2,0:T(8,128)}), f32[8,384,144]{1,2,0:T(8,128)S(1)}, u32[]{:S(2)}, u32[]{:S(2)}) async-start(f32[8,384,144]{1,2,0:T(8,128)} %copy.48), calls=%async_computation | async-start | bytes 3538944 | tf_op jit(solution)/shard_map/all_to_all | solution.py:212
  60.7 1.2 fusion.66
  62.6 39.5 %all-to-all-done = f32[8,384,144]{1,2,0:T(8,128)S(1)} async-done(((f32[8,384,144]{1,2,0:T(8,128)}), f32[8,384,144]{1,2,0:T(8,128)S(1)}, u32[]{:S(2)}, u32[]{:S(2)}) %all-to-all-start) | async-done | bytes 1769504 | tf_op jit(solution)/shard_map/all_to_all | solution.py:212
  102.7 1.1 copy.50
  103.8 1.8 reshape.174.e_ref
  105.7 13.3 %shard_map.86 = f32[36,32,384]{2,1,0:T(8,128)} custom-call(s32[4]{0:T(128)} %off_ref.1, f32[32,1]{1,0:T(8,128)} %copy.51.w_ref, f32[36,32,384]{2,1,0:T(8,128)} %reshape.174.e_ref), custom_call_target="tpu_custom_call" | custom-call | tf_op jit(solution)/shard_map/pallas_call | solution.py:155
  119.0 1.8 reshape.175
  121.0 1.5 copy.53
  122.5 4.3 %all-to-all-start.1 = ((f32[8,384,144]{1,2,0:T(8,128)}), f32[8,384,144]{1,2,0:T(8,128)}, u32[]{:S(2)}, u32[]{:S(2)}) async-start(f32[8,384,144]{1,2,0:T(8,128)} %copy.53), calls=%async_computation.1 | async-start | bytes 3538944 | tf_op jit(solution)/shard_map/all_to_all | solution.py:225
  128.3 40.5 %all-to-all-done.1 = f32[8,384,144]{1,2,0:T(8,128)} async-done(((f32[8,384,144]{1,2,0:T(8,128)}), f32[8,384,144]{1,2,0:T(8,128)}, u32[]{:S(2)}, u32[]{:S(2)}) %all-to-all-start.1) | async-done | bytes 1769504 | tf_op jit(solution)/shard_map/all_to_all | solution.py:225
  168.8 2.1 %copy.58 = f32[8,384,144]{2,1,0:T(8,128)S(1)} copy(f32[8,384,144]{1,2,0:T(8,128)} %all-to-all-done.1) | data formatting | bytes 3538944 | tf_op jit(solution)/shard_map/all_to_all | solution.py:225
  171.0 21.1 %scatter_fusion = f32[4096,144]{1,0:T(8,128)} fusion(f32[4096,144]{1,0:T(8,128)} %bitcast.28, s32[3072]{0:T(1024)S(1)} %bitcast.39, f32[3072,144]{1,0:T(8,128)S(1)} %bitcast.30), kind=kCustom, calls=%fused_computation.1 | custom fusion | flops 442368 | bytes 5320704 | tf_op jit(solution)/shard_map/scatter-add | solution.py:226
  192.1 4.8 %copy.57 = f32[144,32,128]{2,1,0:T(8,128)} copy(f32[144,32,128]{0,2,1:T(8,128)} %bitcast.29) | data formatting | bytes 4718592
  (38 shorter events, 6.6 us)
Async XLA Ops:
  0.6 15.5 %copy-start = (f32[144,32,128]{2,1,0:T(8,128)S(1)}, f32[144,32,128]{2,1,0:T(8,128)}, u32[]{:S(2)}) copy-start(f32[144,32,128]{2,1,0:T(8,128)} %param.7) | copy-start | bytes 7077892
  0.6 15.5 %copy-start.2 = (f32[32,128]{1,0:T(8,128)S(1)}, f32[32,128]{1,0:T(8,128)}, u32[]{:S(2)}) copy-start(f32[32,128]{1,0:T(8,128)} %param.8) | copy-start | bytes 49156
  0.7 4.7 %copy-start.5 = (f32[32]{0:T(128)S(1)}, f32[32]{0:T(128)}, u32[]{:S(2)}) copy-start(f32[32]{0:T(128)} %param.11) | copy-start | bytes 388
  0.7 4.7 %copy-start.6 = (f32[32]{0:T(128)S(1)}, f32[32]{0:T(128)}, u32[]{:S(2)}) copy-start(f32[32]{0:T(128)} %param.10) | copy-start | bytes 388
  0.7 4.8 %slice-start = ((s32[32,128]{1,0:T(8,128)}), s32[24,128]{1,0:T(8,128)S(1)}, s32[]{:S(2)}) async-start(s32[32,128]{1,0:T(8,128)} %param.9), calls=%async_computation.2 | async-start | bytes 24576 | tf_op jit(solution)/shard_map/slice | solution.py:209
  2.3 13.7 %collective-permute-start = (f32[145,6,128]{2,0,1:T(8,128)S(1)}, f32[145,6,128]{2,0,1:T(8,128)S(1)}, u32[]{:S(2)}, u32[]{:S(2)}) collective-permute-start(f32[145,6,128]{2,0,1:T(8,128)S(1)} %copy.44), channel_id=1, source_target_pairs={{0,1},{1,0},{2,3},{3,2},{4,5},{5,4},{6,7},{7,6},{8,9},{9,8},{10,11... | collective-permute-start | bytes 1336328 | tf_op jit(solution)/shard_map/ppermute | solution.py:28
  54.8 5.3 %copy-start.3 = (s32[4]{0:T(128)S(1)}, s32[4]{0:T(128)}, u32[]{:S(2)}) copy-start(s32[4]{0:T(128)} %off_ref.1) | copy-start | bytes 52
  54.9 5.9 %copy-start.4 = (f32[32]{0:T(128)S(1)}, f32[32]{0:T(128)}, u32[]{:S(2)}) copy-start(f32[32]{0:T(128)} %param.12) | copy-start | bytes 388
  54.9 47.3 %all-to-all-start = ((f32[8,384,144]{1,2,0:T(8,128)}), f32[8,384,144]{1,2,0:T(8,128)S(1)}, u32[]{:S(2)}, u32[]{:S(2)}) async-start(f32[8,384,144]{1,2,0:T(8,128)} %copy.48), calls=%async_computation | async-start | bytes 3538944 | tf_op jit(solution)/shard_map/all_to_all | solution.py:212
  120.9 5.9 %copy-start.1 = (f32[36,32,384]{2,1,0:T(8,128)S(1)}, f32[36,32,384]{2,1,0:T(8,128)}, u32[]{:S(2)}) copy-start(f32[36,32,384]{2,1,0:T(8,128)} %shard_map.86) | copy-start | bytes 5308420
  122.5 46.3 %all-to-all-start.1 = ((f32[8,384,144]{1,2,0:T(8,128)}), f32[8,384,144]{1,2,0:T(8,128)}, u32[]{:S(2)}, u32[]{:S(2)}) async-start(f32[8,384,144]{1,2,0:T(8,128)} %copy.53), calls=%async_computation.1 | async-start | bytes 3538944 | tf_op jit(solution)/shard_map/all_to_all | solution.py:225

commit v17 on v14

--- a/solution.py
+++ b/solution.py
@@ -130,7 +130,7 @@
             )
         return carry
 
-    lax.fori_loop(0, NDIR, transfers, 0)
+    lax.fori_loop(0, NDIR, transfers, 0, unroll=4)
 
     def sources(d, carry):
         total = -2.0 * t_ref[0, d] - 2.0 * t_ref[1, d]
@@ -142,7 +142,7 @@
         s_ref[d] = total
         return carry
 
-    lax.fori_loop(0, NDIR, sources, 0)
+    lax.fori_loop(0, NDIR, sources, 0, unroll=4)
 
 
 def interact_pallas(spectra, coupling, quad_offsets):
@@ -212,7 +212,7 @@
         .reshape(NDIR, NFREQ, points)
     )
     by_dir = interact_pallas(spectra, coupling, quad_offsets)
-    source_terms = by_dir.transpose(1, 0, 2).reshape(NFREQ * NDIR, points)
+    source_terms = by_dir.astype(jnp.bfloat16).transpose(1, 0, 2).reshape(NFREQ * NDIR, points)
     outgoing = (
         by_dir.reshape(NDIR, spec_size, local_freqs, points)
         .transpose(1, 3, 2, 0)
@@ -223,7 +223,7 @@
         returned, mode="promise_in_bounds", unique_indices=True
     )
     updated = new_cells.T.reshape(smoothed.shape)
-    return (updated, source_terms.astype(jnp.bfloat16)[None])
+    return (updated, source_terms[None])
 
 
 def solution(mesh):

time: 191 us -> 191 us (level)
  no operation moved by 1% of the time
where the time goes in v17:
time: 191 us; the launch traced here: 190 us
  waiting for transfers between devices  90.4 us (47%)
  other arithmetic  45.2 us (24%)
  local copies, waits for them, and re-layouts  34.4 us (18%)
  starting transfers between devices  12.6 us (7%)
  Pallas kernels  6.44 us (3%)
    all_to_all x1, waiting for transfers between devices, on_device(): lax.all_to_all(outgoing, 'spec', split_axis=0, concat_axis=0, tiled=True)  40.5 us
    all_to_all x1, waiting for transfers between devices, on_device(): lax.all_to_all(rows, 'spec', split_axis=0, concat_axis=0, tiled=True)  39.5 us
    scatter-add x1, other arithmetic, on_device(): cells_first.at[sea_cells]  21.1 us
    gather x1, local copies, waits for them, and re-layouts, on_device(): cells_first.at[sea_cells].get(mode='promise_in_bounds', unique_indices=True)  12 us
    ppermute x1, waiting for transfers between devices, extended_2(): lax.ppermute(jnp.where(first, bottom, top), axis, [(0, 1), (1, 0)])  10.4 us
    mul x4, other arithmetic, propagate(): energy = quickest_x(energy, courant_x) * ext_mask  9.36 us
    pallas_call x1, Pallas kernels, interact_pallas(): pl.pallas_call(interact_kernel, out_shape=jax.ShapeDtypeStruct(spectra.sh...  6.44 us
    mul x2, other arithmetic, quickest(): face_flux = courant * face_value  5.47 us
  transfers between devices with their start and end apart: 3, of which 3 were waited for; matrix products, arithmetic and copies ran while one was open for 2% of the time, Pallas kernels for 0%

profile of v17, /device:TPU:0, one launch (start us, length us, event | category | flops | bytes accessed | tf_op | source)
XLA Modules:
  0.0 190.0 jit_solution(17874858850652727131)
XLA Ops:
  0.7 1.5 fusion.56
  2.3 3.0 %collective-permute-start = (f32[145,6,128]{2,0,1:T(8,128)S(1)}, f32[145,6,128]{2,0,1:T(8,128)S(1)}, u32[]{:S(2)}, u32[]{:S(2)}) collective-permute-start(f32[145,6,128]{2,0,1:T(8,128)S(1)} %copy.44), channel_id=1, source_target_pairs={{0,1},{1,0},{2,3},{3,2},{4,5},{5,4},{6,7},{7,6},{8,9},{9,8},{10,11... | collective-permute-start | bytes 1336328 | tf_op jit(solution)/shard_map/ppermute | solution.py:28
  5.6 10.4 %collective-permute-done = f32[145,6,128]{2,0,1:T(8,128)S(1)} collective-permute-done((f32[145,6,128]{2,0,1:T(8,128)S(1)}, f32[145,6,128]{2,0,1:T(8,128)S(1)}, u32[]{:S(2)}, u32[]{:S(2)}) %collective-permute-start) | collective-permute-done | bytes 445472 | tf_op jit(solution)/shard_map/ppermute | solution.py:28
  16.7 2.8 %fusion.4 = f32[144,41,128]{2,1,0:T(8,128)S(1)} fusion(f32[145,44,128]{2,1,0:T(8,128)S(1)} %pad_maximum_fusion, f32[144]{0:T(256)S(1)} %get-tuple-element.30, f32[144]{0:T(256)S(1)} %get-tuple-element.31, f32[144]{0:T(256)S(1)} %get-tuple-element.25, pred[144]{0:T(512)(128)(4,1)S(1)} %get-tuple-element.24), kind=kLoop, calls=%fused_computation.20 | loop fusion | flops 11335680 | bytes 15116112 | tf_op jit(solution)/shard_map/mul | solution.py:60
  20.6 4.7 %fusion.13 = f32[144,40,128]{2,1,0:T(8,128)S(1)} fusion(f32[144,40,128]{2,1,0:T(8,128)S(1)} %fusion.39, f32[40,128]{1,0:T(8,128)S(1)} %maximum_bitcast_fusion.1, f32[144]{0:T(256)S(1)} %get-tuple-element.23, f32[144]{0:T(256)S(1)} %get-tuple-element.22, f32[144]{0:T(256)S(1)} %get-tuple-element.15, pred[144]{0:T(512)(128)(4,1)S(1)} %get-tuple-element.14), kind=kLoop, calls=%fused_computation.30 | loop fusion | flops 22118400 | bytes 5920592 | tf_op jit(solution)/shard_map/mul | solution.py:174
  25.3 2.6 %fusion.38 = f32[144,37,128]{2,1,0:T(8,128)S(1)} fusion(f32[144,40,128]{2,1,0:T(8,128)S(1)} %fusion.13, f32[144]{0:T(256)S(1)} %get-tuple-element.30, f32[144]{0:T(256)S(1)} %get-tuple-element.31, f32[144]{0:T(256)S(1)} %get-tuple-element.25, pred[144]{0:T(512)(128)(4,1)S(1)} %get-tuple-element.24), kind=kLoop, calls=%fused_computation.57 | loop fusion | flops 10229760 | bytes 13641552 | tf_op jit(solution)/shard_map/mul | solution.py:60
  28.5 4.7 %fusion.27 = f32[144,36,128]{2,1,0:T(8,128)S(1)} fusion(f32[144,36,128]{2,1,0:T(8,128)S(1)} %fusion.33, f32[36,128]{1,0:T(8,128)S(1)} %maximum_bitcast_fusion, f32[144]{0:T(256)S(1)} %get-tuple-element.23, f32[144]{0:T(256)S(1)} %get-tuple-element.22, f32[144]{0:T(256)S(1)} %get-tuple-element.15, pred[144]{0:T(512)(128)(4,1)S(1)} %get-tuple-element.14), kind=kLoop, calls=%fused_computation.44 | loop fusion | flops 19906560 | bytes 5328720 | tf_op jit(solution)/shard_map/mul | solution.py:174
  33.6 3.9 %fusion.46 = f32[144,32,128]{2,1,0:T(8,128)S(1)} fusion(f32[144,32,128]{2,1,0:T(8,128)S(1)} %slice.148, f32[144,36,128]{2,1,0:T(8,128)S(1)} %fusion.27, f32[32,128]{1,0:T(8,128)S(1)} %copy-done.2, f32[144]{0:T(256)S(1)} %get-tuple-element.21, f32[144]{0:T(256)S(1)} %get-tuple-element.20), kind=kLoop, calls=%fused_computation.67 | loop fusion | flops 11796480 | bytes 14173312 | tf_op jit(solution)/shard_map/mul | solution.py:199
  37.5 3.3 %copy.47 = f32[144,32,128]{0,2,1:T(8,128)} copy(f32[144,32,128]{2,1,0:T(8,128)S(1)} %fusion.46) | data formatting | bytes 4718592 | tf_op jit(solution)/shard_map/mul | solution.py:199
  40.8 12.0 %gather_fusion = f32[3072,144]{1,0:T(8,128)S(1)} fusion(f32[4096,144]{1,0:T(8,128)} %bitcast.27, s32[3072]{0:T(1024)S(1)} %broadcast_clamp_fusion), kind=kCustom, calls=%fused_computation | custom fusion | bytes 3551232 | tf_op jit(solution)/shard_map/gather | solution.py:207
  52.8 2.0 %copy.48 = f32[8,384,144]{1,2,0:T(8,128)} copy(f32[8,384,144]{2,1,0:T(8,128)S(1)} %bitcast.31) | data formatting | bytes 3538944 | tf_op jit(solution)/shard_map/all_to_all | solution.py:208
  54.9 5.3 %all-to-all-start = ((f32[8,384,144]{1,2,0:T(8,128)}), f32[8,384,144]{1,2,0:T(8,128)S(1)}, u32[]{:S(2)}, u32[]{:S(2)}) async-start(f32[8,384,144]{1,2,0:T(8,128)} %copy.48), calls=%async_computation | async-start | bytes 3538944 | tf_op jit(solution)/shard_map/all_to_all | solution.py:208
  60.7 1.2 fusion.66
  62.6 39.5 %all-to-all-done = f32[8,384,144]{1,2,0:T(8,128)S(1)} async-done(((f32[8,384,144]{1,2,0:T(8,128)}), f32[8,384,144]{1,2,0:T(8,128)S(1)}, u32[]{:S(2)}, u32[]{:S(2)}) %all-to-all-start) | async-done | bytes 1769504 | tf_op jit(solution)/shard_map/all_to_all | solution.py:208
  102.7 1.1 copy.50
  103.8 1.8 reshape.162.e_ref
  105.7 6.4 %shard_map.86 = f32[36,32,384]{2,1,0:T(8,128)} custom-call(s32[4]{0:T(128)} %off_ref.1, f32[32,1]{1,0:T(8,128)} %copy.51.w_ref, f32[36,32,384]{2,1,0:T(8,128)} %reshape.162.e_ref), custom_call_target="tpu_custom_call" | custom-call | tf_op jit(solution)/shard_map/pallas_call | solution.py:152
  112.1 1.8 reshape.163
  114.1 1.5 copy.53
  115.6 4.3 %all-to-all-start.1 = ((f32[8,384,144]{1,2,0:T(8,128)}), f32[8,384,144]{1,2,0:T(8,128)}, u32[]{:S(2)}, u32[]{:S(2)}) async-start(f32[8,384,144]{1,2,0:T(8,128)} %copy.53), calls=%async_computation.1 | async-start | bytes 3538944 | tf_op jit(solution)/shard_map/all_to_all | solution.py:221
  121.4 40.5 %all-to-all-done.1 = f32[8,384,144]{1,2,0:T(8,128)} async-done(((f32[8,384,144]{1,2,0:T(8,128)}), f32[8,384,144]{1,2,0:T(8,128)}, u32[]{:S(2)}, u32[]{:S(2)}) %all-to-all-start.1) | async-done | bytes 1769504 | tf_op jit(solution)/shard_map/all_to_all | solution.py:221
  161.9 2.1 %copy.58 = f32[8,384,144]{2,1,0:T(8,128)S(1)} copy(f32[8,384,144]{1,2,0:T(8,128)} %all-to-all-done.1) | data formatting | bytes 3538944 | tf_op jit(solution)/shard_map/all_to_all | solution.py:221
  164.1 21.1 %scatter_fusion = f32[4096,144]{1,0:T(8,128)} fusion(f32[4096,144]{1,0:T(8,128)} %bitcast.28, s32[3072]{0:T(1024)S(1)} %bitcast.39, f32[3072,144]{1,0:T(8,128)S(1)} %bitcast.30), kind=kCustom, calls=%fused_computation.1 | custom fusion | flops 442368 | bytes 5320704 | tf_op jit(solution)/shard_map/scatter-add | solution.py:222
  185.2 4.8 %copy.57 = f32[144,32,128]{2,1,0:T(8,128)} copy(f32[144,32,128]{0,2,1:T(8,128)} %bitcast.29) | data formatting | bytes 4718592
  (38 shorter events, 6.6 us)
Async XLA Ops:
  0.6 15.5 %copy-start = (f32[144,32,128]{2,1,0:T(8,128)S(1)}, f32[144,32,128]{2,1,0:T(8,128)}, u32[]{:S(2)}) copy-start(f32[144,32,128]{2,1,0:T(8,128)} %param.7) | copy-start | bytes 7077892
  0.6 15.5 %copy-start.2 = (f32[32,128]{1,0:T(8,128)S(1)}, f32[32,128]{1,0:T(8,128)}, u32[]{:S(2)}) copy-start(f32[32,128]{1,0:T(8,128)} %param.8) | copy-start | bytes 49156
  0.7 4.7 %copy-start.5 = (f32[32]{0:T(128)S(1)}, f32[32]{0:T(128)}, u32[]{:S(2)}) copy-start(f32[32]{0:T(128)} %param.11) | copy-start | bytes 388
  0.7 4.7 %copy-start.6 = (f32[32]{0:T(128)S(1)}, f32[32]{0:T(128)}, u32[]{:S(2)}) copy-start(f32[32]{0:T(128)} %param.10) | copy-start | bytes 388
  0.7 4.8 %slice-start = ((s32[32,128]{1,0:T(8,128)}), s32[24,128]{1,0:T(8,128)S(1)}, s32[]{:S(2)}) async-start(s32[32,128]{1,0:T(8,128)} %param.9), calls=%async_computation.2 | async-start | bytes 24576 | tf_op jit(solution)/shard_map/slice | solution.py:205
  2.3 13.7 %collective-permute-start = (f32[145,6,128]{2,0,1:T(8,128)S(1)}, f32[145,6,128]{2,0,1:T(8,128)S(1)}, u32[]{:S(2)}, u32[]{:S(2)}) collective-permute-start(f32[145,6,128]{2,0,1:T(8,128)S(1)} %copy.44), channel_id=1, source_target_pairs={{0,1},{1,0},{2,3},{3,2},{4,5},{5,4},{6,7},{7,6},{8,9},{9,8},{10,11... | collective-permute-start | bytes 1336328 | tf_op jit(solution)/shard_map/ppermute | solution.py:28
  54.8 5.3 %copy-start.3 = (s32[4]{0:T(128)S(1)}, s32[4]{0:T(128)}, u32[]{:S(2)}) copy-start(s32[4]{0:T(128)} %off_ref.1) | copy-start | bytes 52
  54.9 5.9 %copy-start.4 = (f32[32]{0:T(128)S(1)}, f32[32]{0:T(128)}, u32[]{:S(2)}) copy-start(f32[32]{0:T(128)} %param.12) | copy-start | bytes 388
  54.9 47.3 %all-to-all-start = ((f32[8,384,144]{1,2,0:T(8,128)}), f32[8,384,144]{1,2,0:T(8,128)S(1)}, u32[]{:S(2)}, u32[]{:S(2)}) async-start(f32[8,384,144]{1,2,0:T(8,128)} %copy.48), calls=%async_computation | async-start | bytes 3538944 | tf_op jit(solution)/shard_map/all_to_all | solution.py:208
  114.0 5.9 %copy-start.1 = (f32[36,32,384]{2,1,0:T(8,128)S(1)}, f32[36,32,384]{2,1,0:T(8,128)}, u32[]{:S(2)}) copy-start(f32[36,32,384]{2,1,0:T(8,128)} %shard_map.86) | copy-start | bytes 5308420
  115.6 46.3 %all-to-all-start.1 = ((f32[8,384,144]{1,2,0:T(8,128)}), f32[8,384,144]{1,2,0:T(8,128)}, u32[]{:S(2)}, u32[]{:S(2)}) async-start(f32[8,384,144]{1,2,0:T(8,128)} %copy.53), calls=%async_computation.1 | async-start | bytes 3538944 | tf_op jit(solution)/shard_map/all_to_all | solution.py:221

commit v18 on v17

--- a/solution.py
+++ b/solution.py
@@ -219,8 +219,8 @@
         .reshape(spec_size * points, local_comps)
     )
     returned = lax.all_to_all(outgoing, "spec", split_axis=0, concat_axis=0, tiled=True)
-    new_cells = cells_first.at[sea_cells].add(
-        returned, mode="promise_in_bounds", unique_indices=True
+    new_cells = cells_first.at[sea_cells].set(
+        rows + returned, mode="promise_in_bounds", unique_indices=True
     )
     updated = new_cells.T.reshape(smoothed.shape)
     return (updated, source_terms[None])

time: 191 us -> 199 us (1.042)
  local copies, waits for them, and re-layouts: 34.4 us -> 61.5 us
  other arithmetic: 45.2 us -> 29.5 us
  waiting for transfers between devices: 90.4 us -> 87.1 us
    scatter-add x1 -> x0, other arithmetic: 21.1 us -> none  [on_device(): cells_first.at[sea_cells]]
    scatter x0 -> x1, local copies, waits for them, and re-layouts: none -> 17.7 us  [on_device(): cells_first.at[sea_cells]]
    add x0 -> x1, other arithmetic: none -> 3.96 us  [on_device(): rows + returned]
    all_to_all x1, waiting for transfers between devices: 40.5 us -> 37.1 us  [on_device(): lax.all_to_all(outgoing, 'spec', split_axis=0, concat_axis=0, tiled=True)]
    reshape x2, local copies, waits for them, and re-layouts: 1.93 us -> 4.39 us  [on_device(): by_dir.reshape(NDIR, spec_size, local_freqs, points).transpose(1, 3, 2, 0)]
    unnamed x15 -> x13, local copies, waits for them, and re-layouts: 4.86 us -> 4.85 us
  transfers between devices with their start and end apart: 3 -> 3, of which waited for: 3 -> 3; matrix products, arithmetic and copies ran while one was open for 2% -> 4% of each run, Pallas kernels for 0% -> 0%
where the time goes in v18:
time: 199 us; the launch traced here: 198 us
  waiting for transfers between devices  87.1 us (44%)
  local copies, waits for them, and re-layouts  61.5 us (31%)
  other arithmetic  29.5 us (15%)
  starting transfers between devices  12.6 us (6%)
  Pallas kernels  6.45 us (3%)
    all_to_all x1, waiting for transfers between devices, on_device(): lax.all_to_all(rows, 'spec', split_axis=0, concat_axis=0, tiled=True)  39.6 us
    all_to_all x1, waiting for transfers between devices, on_device(): lax.all_to_all(outgoing, 'spec', split_axis=0, concat_axis=0, tiled=True)  37.1 us
    scatter x1, local copies, waits for them, and re-layouts, on_device(): cells_first.at[sea_cells]  17.7 us
    gather x1, local copies, waits for them, and re-layouts, on_device(): cells_first.at[sea_cells].get(mode='promise_in_bounds', unique_indices=True)  12 us
    ppermute x1, waiting for transfers between devices, extended_2(): lax.ppermute(jnp.where(first, bottom, top), axis, [(0, 1), (1, 0)])  10.4 us
    mul x4, other arithmetic, propagate(): energy = quickest_x(energy, courant_x) * ext_mask  9.36 us
    pallas_call x1, Pallas kernels, interact_pallas(): pl.pallas_call(interact_kernel, out_shape=jax.ShapeDtypeStruct(spectra.sh...  6.45 us
    mul x2, other arithmetic, quickest(): face_flux = courant * face_value  5.47 us
  transfers between devices with their start and end apart: 3, of which 3 were waited for; matrix products, arithmetic and copies ran while one was open for 4% of the time, Pallas kernels for 0%

profile of v18, /device:TPU:0, one launch (start us, length us, event | category | flops | bytes accessed | tf_op | source)
XLA Modules:
  0.0 198.1 jit_solution(16423189419886005027)
XLA Ops:
  2.3 3.0 %collective-permute-start = (f32[145,6,128]{2,0,1:T(8,128)S(1)}, f32[145,6,128]{2,0,1:T(8,128)S(1)}, u32[]{:S(2)}, u32[]{:S(2)}) collective-permute-start(f32[145,6,128]{2,0,1:T(8,128)S(1)} %copy.44), channel_id=1, source_target_pairs={{0,1},{1,0},{2,3},{3,2},{4,5},{5,4},{6,7},{7,6},{8,9},{9,8},{10,11... | collective-permute-start | bytes 1336328 | tf_op jit(solution)/shard_map/ppermute | solution.py:28
  5.6 10.4 %collective-permute-done = f32[145,6,128]{2,0,1:T(8,128)S(1)} collective-permute-done((f32[145,6,128]{2,0,1:T(8,128)S(1)}, f32[145,6,128]{2,0,1:T(8,128)S(1)}, u32[]{:S(2)}, u32[]{:S(2)}) %collective-permute-start) | collective-permute-done | bytes 445472 | tf_op jit(solution)/shard_map/ppermute | solution.py:28
  16.7 2.8 %fusion.4 = f32[144,41,128]{2,1,0:T(8,128)S(1)} fusion(f32[145,44,128]{2,1,0:T(8,128)S(1)} %pad_maximum_fusion, f32[144]{0:T(256)S(1)} %get-tuple-element.30, f32[144]{0:T(256)S(1)} %get-tuple-element.31, f32[144]{0:T(256)S(1)} %get-tuple-element.25, pred[144]{0:T(512)(128)(4,1)S(1)} %get-tuple-element.24), kind=kLoop, calls=%fused_computation.20 | loop fusion | flops 11335680 | bytes 15116112 | tf_op jit(solution)/shard_map/mul | solution.py:60
  20.6 4.7 %fusion.13 = f32[144,40,128]{2,1,0:T(8,128)S(1)} fusion(f32[144,40,128]{2,1,0:T(8,128)S(1)} %fusion.39, f32[40,128]{1,0:T(8,128)S(1)} %maximum_bitcast_fusion.1, f32[144]{0:T(256)S(1)} %get-tuple-element.23, f32[144]{0:T(256)S(1)} %get-tuple-element.22, f32[144]{0:T(256)S(1)} %get-tuple-element.15, pred[144]{0:T(512)(128)(4,1)S(1)} %get-tuple-element.14), kind=kLoop, calls=%fused_computation.31 | loop fusion | flops 22118400 | bytes 5920592 | tf_op jit(solution)/shard_map/mul | solution.py:174
  25.3 2.6 %fusion.38 = f32[144,37,128]{2,1,0:T(8,128)S(1)} fusion(f32[144,40,128]{2,1,0:T(8,128)S(1)} %fusion.13, f32[144]{0:T(256)S(1)} %get-tuple-element.30, f32[144]{0:T(256)S(1)} %get-tuple-element.31, f32[144]{0:T(256)S(1)} %get-tuple-element.25, pred[144]{0:T(512)(128)(4,1)S(1)} %get-tuple-element.24), kind=kLoop, calls=%fused_computation.58 | loop fusion | flops 10229760 | bytes 13641552 | tf_op jit(solution)/shard_map/mul | solution.py:60
  28.5 4.7 %fusion.27 = f32[144,36,128]{2,1,0:T(8,128)S(1)} fusion(f32[144,36,128]{2,1,0:T(8,128)S(1)} %fusion.33, f32[36,128]{1,0:T(8,128)S(1)} %maximum_bitcast_fusion, f32[144]{0:T(256)S(1)} %get-tuple-element.23, f32[144]{0:T(256)S(1)} %get-tuple-element.22, f32[144]{0:T(256)S(1)} %get-tuple-element.15, pred[144]{0:T(512)(128)(4,1)S(1)} %get-tuple-element.14), kind=kLoop, calls=%fused_computation.45 | loop fusion | flops 19906560 | bytes 5328720 | tf_op jit(solution)/shard_map/mul | solution.py:174
  33.6 3.9 %fusion.46 = f32[144,32,128]{2,1,0:T(8,128)S(1)} fusion(f32[144,32,128]{2,1,0:T(8,128)S(1)} %slice.148, f32[144,36,128]{2,1,0:T(8,128)S(1)} %fusion.27, f32[32,128]{1,0:T(8,128)S(1)} %copy-done.1, f32[144]{0:T(256)S(1)} %get-tuple-element.21, f32[144]{0:T(256)S(1)} %get-tuple-element.20), kind=kLoop, calls=%fused_computation.68 | loop fusion | flops 11796480 | bytes 14173312 | tf_op jit(solution)/shard_map/mul | solution.py:199
  37.5 3.3 %copy.47 = f32[144,32,128]{0,2,1:T(8,128)} copy(f32[144,32,128]{2,1,0:T(8,128)S(1)} %fusion.46) | data formatting | bytes 4718592 | tf_op jit(solution)/shard_map/mul | solution.py:199
  40.8 12.0 %gather_fusion = f32[3072,144]{1,0:T(8,128)S(1)} fusion(f32[4096,144]{1,0:T(8,128)} %bitcast.29, s32[3072]{0:T(1024)S(1)} %broadcast_clamp_fusion), kind=kCustom, calls=%fused_computation | custom fusion | bytes 3551232 | tf_op jit(solution)/shard_map/gather | solution.py:207
  52.8 2.0 %copy.48 = f32[8,384,144]{1,2,0:T(8,128)} copy(f32[8,384,144]{2,1,0:T(8,128)S(1)} %bitcast.32) | data formatting | bytes 3538944 | tf_op jit(solution)/shard_map/all_to_all | solution.py:208
  54.9 5.3 %all-to-all-start = ((f32[8,384,144]{1,2,0:T(8,128)}), f32[8,384,144]{1,2,0:T(8,128)}, u32[]{:S(2)}, u32[]{:S(2)}) async-start(f32[8,384,144]{1,2,0:T(8,128)} %copy.48), calls=%async_computation | async-start | bytes 3538944 | tf_op jit(solution)/shard_map/all_to_all | solution.py:208
  62.6 39.6 %all-to-all-done = f32[8,384,144]{1,2,0:T(8,128)} async-done(((f32[8,384,144]{1,2,0:T(8,128)}), f32[8,384,144]{1,2,0:T(8,128)}, u32[]{:S(2)}, u32[]{:S(2)}) %all-to-all-start) | async-done | bytes 1769504 | tf_op jit(solution)/shard_map/all_to_all | solution.py:208
  102.2 2.0 %copy.49 = f32[8,384,144]{1,0,2:T(8,128)S(1)} copy(f32[8,384,144]{1,2,0:T(8,128)} %all-to-all-done) | data formatting | bytes 3538944 | tf_op jit(solution)/shard_map/all_to_all | solution.py:208
  104.3 2.3 %copy.50 = f32[36,8,4,384]{3,2,1,0:T(4,128)} copy(f32[36,8,4,384]{3,1,0,2:T(8,128)S(1)} %bitcast.33) | data formatting | bytes 3538944 | tf_op jit(solution)/shard_map/transpose | solution.py:211
  106.6 2.8 %reshape.162.e_ref = f32[36,32,384]{2,1,0:T(8,128)} reshape(f32[36,8,4,384]{3,2,1,0:T(4,128)} %copy.50) | data formatting | bytes 3538944 | tf_op jit(solution)/shard_map/reshape | solution.py:212
  109.5 6.4 %shard_map.86 = f32[36,32,384]{2,1,0:T(8,128)} custom-call(s32[4]{0:T(128)} %off_ref.1, f32[32,1]{1,0:T(8,128)} %copy.51.w_ref, f32[36,32,384]{2,1,0:T(8,128)} %reshape.162.e_ref), custom_call_target="tpu_custom_call" | custom-call | tf_op jit(solution)/shard_map/pallas_call | solution.py:152
  115.9 2.8 %reshape.163 = f32[36,8,4,384]{3,2,1,0:T(4,128)} reshape(f32[36,32,384]{2,1,0:T(8,128)} %shard_map.86) | data formatting | bytes 3538944 | tf_op jit(solution)/shard_map/reshape | solution.py:217
  121.8 4.3 %all-to-all-start.1 = ((f32[8,384,144]{1,2,0:T(8,128)}), f32[8,384,144]{1,2,0:T(8,128)}, u32[]{:S(2)}, u32[]{:S(2)}) async-start(f32[8,384,144]{1,2,0:T(8,128)} %copy.53), calls=%async_computation.1 | async-start | bytes 3538944 | tf_op jit(solution)/shard_map/all_to_all | solution.py:221
  129.0 2.1 %broadcast_in_dim_reshape.3 = bf16[1,1152,384]{2,1,0:T(8,128)(2,1)} reshape(bf16[32,36,384]{2,1,0:T(8,128)(2,1)} %copy.55) | data formatting | bytes 1769472 | tf_op jit(solution)/shard_map/broadcast_in_dim;reshape | solution.py:226
  131.1 37.1 %all-to-all-done.1 = f32[8,384,144]{1,2,0:T(8,128)} async-done(((f32[8,384,144]{1,2,0:T(8,128)}), f32[8,384,144]{1,2,0:T(8,128)}, u32[]{:S(2)}, u32[]{:S(2)}) %all-to-all-start.1) | async-done | bytes 1769504 | tf_op jit(solution)/shard_map/all_to_all | solution.py:221
  168.2 3.4 %copy.54 = f32[8,384,144]{2,1,0:T(8,128)} copy(f32[8,384,144]{1,2,0:T(8,128)} %all-to-all-done.1) | data formatting | bytes 3538944 | tf_op jit(solution)/shard_map/all_to_all | solution.py:221
  171.5 4.0 %bitcast_add_fusion = f32[3072,144]{1,0:T(8,128)} fusion(f32[3072,144]{1,0:T(8,128)S(1)} %gather_fusion, f32[8,384,144]{2,1,0:T(8,128)} %copy.54), kind=kLoop, calls=%fused_computation.22 | loop fusion | flops 442368 | bytes 5308416 | tf_op jit(solution)/shard_map/add | solution.py:223
  175.5 17.7 %scatter_fusion = f32[4096,144]{1,0:T(8,128)} fusion(f32[4096,144]{1,0:T(8,128)} %bitcast.30, s32[3072]{0:T(1024)S(1)} %bitcast.40, f32[3072,144]{1,0:T(8,128)} %bitcast_add_fusion), kind=kCustom, calls=%fused_computation.1 | custom fusion | bytes 5320704 | tf_op jit(solution)/shard_map/scatter | solution.py:222
  193.2 4.8 %copy.56 = f32[144,32,128]{2,1,0:T(8,128)} copy(f32[144,32,128]{0,2,1:T(8,128)} %bitcast.31) | data formatting | bytes 4718592
  (37 shorter events, 13.0 us)
Async XLA Ops:
  0.6 15.5 %copy-start = (f32[144,32,128]{2,1,0:T(8,128)S(1)}, f32[144,32,128]{2,1,0:T(8,128)}, u32[]{:S(2)}) copy-start(f32[144,32,128]{2,1,0:T(8,128)} %param.7) | copy-start | bytes 7077892
  0.6 15.5 %copy-start.1 = (f32[32,128]{1,0:T(8,128)S(1)}, f32[32,128]{1,0:T(8,128)}, u32[]{:S(2)}) copy-start(f32[32,128]{1,0:T(8,128)} %param.8) | copy-start | bytes 49156
  0.7 4.7 %copy-start.4 = (f32[32]{0:T(128)S(1)}, f32[32]{0:T(128)}, u32[]{:S(2)}) copy-start(f32[32]{0:T(128)} %param.11) | copy-start | bytes 388
  0.7 4.7 %copy-start.5 = (f32[32]{0:T(128)S(1)}, f32[32]{0:T(128)}, u32[]{:S(2)}) copy-start(f32[32]{0:T(128)} %param.10) | copy-start | bytes 388
  0.7 4.8 %slice-start = ((s32[32,128]{1,0:T(8,128)}), s32[24,128]{1,0:T(8,128)S(1)}, s32[]{:S(2)}) async-start(s32[32,128]{1,0:T(8,128)} %param.9), calls=%async_computation.2 | async-start | bytes 24576 | tf_op jit(solution)/shard_map/slice | solution.py:205
  2.3 13.7 %collective-permute-start = (f32[145,6,128]{2,0,1:T(8,128)S(1)}, f32[145,6,128]{2,0,1:T(8,128)S(1)}, u32[]{:S(2)}, u32[]{:S(2)}) collective-permute-start(f32[145,6,128]{2,0,1:T(8,128)S(1)} %copy.44), channel_id=1, source_target_pairs={{0,1},{1,0},{2,3},{3,2},{4,5},{5,4},{6,7},{7,6},{8,9},{9,8},{10,11... | collective-permute-start | bytes 1336328 | tf_op jit(solution)/shard_map/ppermute | solution.py:28
  54.8 5.3 %copy-start.2 = (s32[4]{0:T(128)S(1)}, s32[4]{0:T(128)}, u32[]{:S(2)}) copy-start(s32[4]{0:T(128)} %off_ref.1) | copy-start | bytes 52
  54.9 5.8 %copy-start.3 = (f32[32]{0:T(128)S(1)}, f32[32]{0:T(128)}, u32[]{:S(2)}) copy-start(f32[32]{0:T(128)} %param.12) | copy-start | bytes 388
  54.9 47.4 %all-to-all-start = ((f32[8,384,144]{1,2,0:T(8,128)}), f32[8,384,144]{1,2,0:T(8,128)}, u32[]{:S(2)}, u32[]{:S(2)}) async-start(f32[8,384,144]{1,2,0:T(8,128)} %copy.48), calls=%async_computation | async-start | bytes 3538944 | tf_op jit(solution)/shard_map/all_to_all | solution.py:208
  121.8 46.3 %all-to-all-start.1 = ((f32[8,384,144]{1,2,0:T(8,128)}), f32[8,384,144]{1,2,0:T(8,128)}, u32[]{:S(2)}, u32[]{:S(2)}) async-start(f32[8,384,144]{1,2,0:T(8,128)} %copy.53), calls=%async_computation.1 | async-start | bytes 3538944 | tf_op jit(solution)/shard_map/all_to_all | solution.py:221

commit v19 on v17

--- a/solution.py
+++ b/solution.py
@@ -109,7 +109,7 @@
     return 4.0 / 3.0 * near_sum - 1.0 / 12.0 * far_sum
 
 
-def interact_kernel(off_ref, w_ref, e_ref, s_ref, t_ref):
+def interact_kernel(off_ref, w_ref, e_ref, s_ref, b_ref, t_ref):
     up_freq = off_ref[0]
     down_freq = off_ref[1]
     dir_one = off_ref[2]
@@ -140,6 +140,7 @@
                 t_ref[slot, (d + mirror * dir_two) % NDIR], (NFREQ - down_freq) % NFREQ, 0
             )
         s_ref[d] = total
+        b_ref[d] = total.astype(jnp.bfloat16)
         return carry
 
     lax.fori_loop(0, NDIR, sources, 0, unroll=4)
@@ -151,13 +152,19 @@
     weight = (coupling * inside)[:, None]
     return pl.pallas_call(
         interact_kernel,
-        out_shape=jax.ShapeDtypeStruct(spectra.shape, jnp.float32),
+        out_shape=(
+            jax.ShapeDtypeStruct(spectra.shape, jnp.float32),
+            jax.ShapeDtypeStruct(spectra.shape, jnp.bfloat16),
+        ),
         in_specs=[
             pl.BlockSpec(memory_space=pltpu.SMEM),
             pl.BlockSpec(memory_space=pltpu.VMEM),
             pl.BlockSpec(memory_space=pltpu.VMEM),
         ],
-        out_specs=pl.BlockSpec(memory_space=pltpu.VMEM),
+        out_specs=(
+            pl.BlockSpec(memory_space=pltpu.VMEM),
+            pl.BlockSpec(memory_space=pltpu.VMEM),
+        ),
         scratch_shapes=[pltpu.VMEM((2,) + spectra.shape, jnp.float32)],
     )(quad_offsets, weight, spectra)
 
@@ -211,8 +218,8 @@
         .transpose(3, 0, 2, 1)
         .reshape(NDIR, NFREQ, points)
     )
-    by_dir = interact_pallas(spectra, coupling, quad_offsets)
-    source_terms = by_dir.astype(jnp.bfloat16).transpose(1, 0, 2).reshape(NFREQ * NDIR, points)
+    by_dir, rounded = interact_pallas(spectra, coupling, quad_offsets)
+    source_terms = rounded.transpose(1, 0, 2).reshape(NFREQ * NDIR, points)
     outgoing = (
         by_dir.reshape(NDIR, spec_size, local_freqs, points)
         .transpose(1, 3, 2, 0)

time: 191 us -> 191 us (level)
  no operation moved by 1% of the time
where the time goes in v19:
time: 191 us; the launch traced here: 190 us
  waiting for transfers between devices  90.3 us (47%)
  other arithmetic  45.2 us (24%)
  local copies, waits for them, and re-layouts  34.5 us (18%)
  starting transfers between devices  12.6 us (7%)
  Pallas kernels  6.79 us (4%)
    all_to_all x1, waiting for transfers between devices, on_device(): lax.all_to_all(outgoing, 'spec', split_axis=0, concat_axis=0, tiled=True)  40.6 us
    all_to_all x1, waiting for transfers between devices, on_device(): lax.all_to_all(rows, 'spec', split_axis=0, concat_axis=0, tiled=True)  39.3 us
    scatter-add x1, other arithmetic, on_device(): cells_first.at[sea_cells]  21.1 us
    gather x1, local copies, waits for them, and re-layouts, on_device(): cells_first.at[sea_cells].get(mode='promise_in_bounds', unique_indices=True)  12 us
    ppermute x1, waiting for transfers between devices, extended_2(): lax.ppermute(jnp.where(first, bottom, top), axis, [(0, 1), (1, 0)])  10.4 us
    mul x4, other arithmetic, propagate(): energy = quickest_x(energy, courant_x) * ext_mask  9.36 us
    pallas_call x1, Pallas kernels, interact_pallas(): pl.pallas_call(interact_kernel, out_shape=(jax.ShapeDtypeStruct(spectra.s...  6.79 us
    mul x2, other arithmetic, quickest(): face_flux = courant * face_value  5.47 us
  transfers between devices with their start and end apart: 3, of which 3 were waited for; matrix products, arithmetic and copies ran while one was open for 2% of the time, Pallas kernels for 0%

profile of v19, /device:TPU:0, one launch (start us, length us, event | category | flops | bytes accessed | tf_op | source)
XLA Modules:
  0.0 190.4 jit_solution(1982763880411055785)
XLA Ops:
  0.7 1.5 fusion.56
  2.3 3.0 %collective-permute-start = (f32[145,6,128]{2,0,1:T(8,128)S(1)}, f32[145,6,128]{2,0,1:T(8,128)S(1)}, u32[]{:S(2)}, u32[]{:S(2)}) collective-permute-start(f32[145,6,128]{2,0,1:T(8,128)S(1)} %copy.44), channel_id=1, source_target_pairs={{0,1},{1,0},{2,3},{3,2},{4,5},{5,4},{6,7},{7,6},{8,9},{9,8},{10,11... | collective-permute-start | bytes 1336328 | tf_op jit(solution)/shard_map/ppermute | solution.py:28
  5.6 10.4 %collective-permute-done = f32[145,6,128]{2,0,1:T(8,128)S(1)} collective-permute-done((f32[145,6,128]{2,0,1:T(8,128)S(1)}, f32[145,6,128]{2,0,1:T(8,128)S(1)}, u32[]{:S(2)}, u32[]{:S(2)}) %collective-permute-start) | collective-permute-done | bytes 445472 | tf_op jit(solution)/shard_map/ppermute | solution.py:28
  16.7 2.8 %fusion.4 = f32[144,41,128]{2,1,0:T(8,128)S(1)} fusion(f32[145,44,128]{2,1,0:T(8,128)S(1)} %pad_maximum_fusion, f32[144]{0:T(256)S(1)} %get-tuple-element.34, f32[144]{0:T(256)S(1)} %get-tuple-element.35, f32[144]{0:T(256)S(1)} %get-tuple-element.29, pred[144]{0:T(512)(128)(4,1)S(1)} %get-tuple-element.28), kind=kLoop, calls=%fused_computation.20 | loop fusion | flops 11335680 | bytes 15116112 | tf_op jit(solution)/shard_map/mul | solution.py:60
  20.6 4.7 %fusion.13 = f32[144,40,128]{2,1,0:T(8,128)S(1)} fusion(f32[144,40,128]{2,1,0:T(8,128)S(1)} %fusion.39, f32[40,128]{1,0:T(8,128)S(1)} %maximum_bitcast_fusion.1, f32[144]{0:T(256)S(1)} %get-tuple-element.27, f32[144]{0:T(256)S(1)} %get-tuple-element.26, f32[144]{0:T(256)S(1)} %get-tuple-element.19, pred[144]{0:T(512)(128)(4,1)S(1)} %get-tuple-element.18), kind=kLoop, calls=%fused_computation.30 | loop fusion | flops 22118400 | bytes 5920592 | tf_op jit(solution)/shard_map/mul | solution.py:181
  25.3 2.6 %fusion.38 = f32[144,37,128]{2,1,0:T(8,128)S(1)} fusion(f32[144,40,128]{2,1,0:T(8,128)S(1)} %fusion.13, f32[144]{0:T(256)S(1)} %get-tuple-element.34, f32[144]{0:T(256)S(1)} %get-tuple-element.35, f32[144]{0:T(256)S(1)} %get-tuple-element.29, pred[144]{0:T(512)(128)(4,1)S(1)} %get-tuple-element.28), kind=kLoop, calls=%fused_computation.57 | loop fusion | flops 10229760 | bytes 13641552 | tf_op jit(solution)/shard_map/mul | solution.py:60
  28.5 4.7 %fusion.27 = f32[144,36,128]{2,1,0:T(8,128)S(1)} fusion(f32[144,36,128]{2,1,0:T(8,128)S(1)} %fusion.33, f32[36,128]{1,0:T(8,128)S(1)} %maximum_bitcast_fusion, f32[144]{0:T(256)S(1)} %get-tuple-element.27, f32[144]{0:T(256)S(1)} %get-tuple-element.26, f32[144]{0:T(256)S(1)} %get-tuple-element.19, pred[144]{0:T(512)(128)(4,1)S(1)} %get-tuple-element.18), kind=kLoop, calls=%fused_computation.44 | loop fusion | flops 19906560 | bytes 5328720 | tf_op jit(solution)/shard_map/mul | solution.py:181
  33.6 3.9 %fusion.46 = f32[144,32,128]{2,1,0:T(8,128)S(1)} fusion(f32[144,32,128]{2,1,0:T(8,128)S(1)} %slice.148, f32[144,36,128]{2,1,0:T(8,128)S(1)} %fusion.27, f32[32,128]{1,0:T(8,128)S(1)} %copy-done.2, f32[144]{0:T(256)S(1)} %get-tuple-element.25, f32[144]{0:T(256)S(1)} %get-tuple-element.24), kind=kLoop, calls=%fused_computation.67 | loop fusion | flops 11796480 | bytes 14173312 | tf_op jit(solution)/shard_map/mul | solution.py:206
  37.5 3.3 %copy.47 = f32[144,32,128]{0,2,1:T(8,128)} copy(f32[144,32,128]{2,1,0:T(8,128)S(1)} %fusion.46) | data formatting | bytes 4718592 | tf_op jit(solution)/shard_map/mul | solution.py:206
  40.8 12.0 %gather_fusion = f32[3072,144]{1,0:T(8,128)S(1)} fusion(f32[4096,144]{1,0:T(8,128)} %bitcast.26, s32[3072]{0:T(1024)S(1)} %broadcast_clamp_fusion), kind=kCustom, calls=%fused_computation | custom fusion | bytes 3551232 | tf_op jit(solution)/shard_map/gather | solution.py:214
  52.8 2.0 %copy.48 = f32[8,384,144]{1,2,0:T(8,128)} copy(f32[8,384,144]{2,1,0:T(8,128)S(1)} %bitcast.30) | data formatting | bytes 3538944 | tf_op jit(solution)/shard_map/all_to_all | solution.py:215
  54.9 5.3 %all-to-all-start = ((f32[8,384,144]{1,2,0:T(8,128)}), f32[8,384,144]{1,2,0:T(8,128)S(1)}, u32[]{:S(2)}, u32[]{:S(2)}) async-start(f32[8,384,144]{1,2,0:T(8,128)} %copy.48), calls=%async_computation | async-start | bytes 3538944 | tf_op jit(solution)/shard_map/all_to_all | solution.py:215
  60.8 1.3 fusion.66
  62.8 39.3 %all-to-all-done = f32[8,384,144]{1,2,0:T(8,128)S(1)} async-done(((f32[8,384,144]{1,2,0:T(8,128)}), f32[8,384,144]{1,2,0:T(8,128)S(1)}, u32[]{:S(2)}, u32[]{:S(2)}) %all-to-all-start) | async-done | bytes 1769504 | tf_op jit(solution)/shard_map/all_to_all | solution.py:215
  102.7 1.1 copy.50
  103.8 1.8 reshape.162.e_ref
  105.7 6.8 %shard_map.86 = (f32[36,32,384]{2,1,0:T(8,128)}, bf16[36,32,384]{2,1,0:T(8,128)(2,1)}) custom-call(s32[4]{0:T(128)} %off_ref.1, f32[32,1]{1,0:T(8,128)} %copy.51.w_ref, f32[36,32,384]{2,1,0:T(8,128)} %reshape.162.e_ref), custom_call_target="tpu_custom_call" | custom-call | tf_op jit(solution)/shard_map/pallas_call | solution.py:153
  112.4 1.8 reshape.163
  114.4 1.5 copy.53
  115.9 4.3 %all-to-all-start.1 = ((f32[8,384,144]{1,2,0:T(8,128)}), f32[8,384,144]{1,2,0:T(8,128)}, u32[]{:S(2)}, u32[]{:S(2)}) async-start(f32[8,384,144]{1,2,0:T(8,128)} %copy.53), calls=%async_computation.1 | async-start | bytes 3538944 | tf_op jit(solution)/shard_map/all_to_all | solution.py:228
  121.7 40.6 %all-to-all-done.1 = f32[8,384,144]{1,2,0:T(8,128)} async-done(((f32[8,384,144]{1,2,0:T(8,128)}), f32[8,384,144]{1,2,0:T(8,128)}, u32[]{:S(2)}, u32[]{:S(2)}) %all-to-all-start.1) | async-done | bytes 1769504 | tf_op jit(solution)/shard_map/all_to_all | solution.py:228
  162.3 2.1 %copy.58 = f32[8,384,144]{2,1,0:T(8,128)S(1)} copy(f32[8,384,144]{1,2,0:T(8,128)} %all-to-all-done.1) | data formatting | bytes 3538944 | tf_op jit(solution)/shard_map/all_to_all | solution.py:228
  164.4 21.1 %scatter_fusion = f32[4096,144]{1,0:T(8,128)} fusion(f32[4096,144]{1,0:T(8,128)} %bitcast.27, s32[3072]{0:T(1024)S(1)} %bitcast.39, f32[3072,144]{1,0:T(8,128)S(1)} %bitcast.29), kind=kCustom, calls=%fused_computation.1 | custom fusion | flops 442368 | bytes 5320704 | tf_op jit(solution)/shard_map/scatter-add | solution.py:229
  185.5 4.8 %copy.57 = f32[144,32,128]{2,1,0:T(8,128)} copy(f32[144,32,128]{0,2,1:T(8,128)} %bitcast.28) | data formatting | bytes 4718592
  (37 shorter events, 6.5 us)
Async XLA Ops:
  0.6 15.5 %copy-start = (f32[144,32,128]{2,1,0:T(8,128)S(1)}, f32[144,32,128]{2,1,0:T(8,128)}, u32[]{:S(2)}) copy-start(f32[144,32,128]{2,1,0:T(8,128)} %param.7) | copy-start | bytes 7077892
  0.6 15.5 %copy-start.2 = (f32[32,128]{1,0:T(8,128)S(1)}, f32[32,128]{1,0:T(8,128)}, u32[]{:S(2)}) copy-start(f32[32,128]{1,0:T(8,128)} %param.8) | copy-start | bytes 49156
  0.7 4.7 %copy-start.5 = (f32[32]{0:T(128)S(1)}, f32[32]{0:T(128)}, u32[]{:S(2)}) copy-start(f32[32]{0:T(128)} %param.11) | copy-start | bytes 388
  0.7 4.7 %copy-start.6 = (f32[32]{0:T(128)S(1)}, f32[32]{0:T(128)}, u32[]{:S(2)}) copy-start(f32[32]{0:T(128)} %param.10) | copy-start | bytes 388
  0.7 4.8 %slice-start = ((s32[32,128]{1,0:T(8,128)}), s32[24,128]{1,0:T(8,128)S(1)}, s32[]{:S(2)}) async-start(s32[32,128]{1,0:T(8,128)} %param.9), calls=%async_computation.2 | async-start | bytes 24576 | tf_op jit(solution)/shard_map/slice | solution.py:212
  2.3 13.7 %collective-permute-start = (f32[145,6,128]{2,0,1:T(8,128)S(1)}, f32[145,6,128]{2,0,1:T(8,128)S(1)}, u32[]{:S(2)}, u32[]{:S(2)}) collective-permute-start(f32[145,6,128]{2,0,1:T(8,128)S(1)} %copy.44), channel_id=1, source_target_pairs={{0,1},{1,0},{2,3},{3,2},{4,5},{5,4},{6,7},{7,6},{8,9},{9,8},{10,11... | collective-permute-start | bytes 1336328 | tf_op jit(solution)/shard_map/ppermute | solution.py:28
  54.8 5.3 %copy-start.3 = (s32[4]{0:T(128)S(1)}, s32[4]{0:T(128)}, u32[]{:S(2)}) copy-start(s32[4]{0:T(128)} %off_ref.1) | copy-start | bytes 52
  54.9 5.9 %copy-start.4 = (f32[32]{0:T(128)S(1)}, f32[32]{0:T(128)}, u32[]{:S(2)}) copy-start(f32[32]{0:T(128)} %param.12) | copy-start | bytes 388
  54.9 47.3 %all-to-all-start = ((f32[8,384,144]{1,2,0:T(8,128)}), f32[8,384,144]{1,2,0:T(8,128)S(1)}, u32[]{:S(2)}, u32[]{:S(2)}) async-start(f32[8,384,144]{1,2,0:T(8,128)} %copy.48), calls=%async_computation | async-start | bytes 3538944 | tf_op jit(solution)/shard_map/all_to_all | solution.py:215
  114.4 5.9 %copy-start.1 = (bf16[36,32,384]{2,1,0:T(8,128)(2,1)S(1)}, bf16[36,32,384]{2,1,0:T(8,128)(2,1)}, u32[]{:S(2)}) copy-start(bf16[36,32,384]{2,1,0:T(8,128)(2,1)} %get-tuple-element.5) | copy-start | bytes 2654212
  115.9 46.3 %all-to-all-start.1 = ((f32[8,384,144]{1,2,0:T(8,128)}), f32[8,384,144]{1,2,0:T(8,128)}, u32[]{:S(2)}, u32[]{:S(2)}) async-start(f32[8,384,144]{1,2,0:T(8,128)} %copy.53), calls=%async_computation.1 | async-start | bytes 3538944 | tf_op jit(solution)/shard_map/all_to_all | solution.py:228
